TPU v7x, 32 devices: a whole 2x2x4 slice. The times are simulated.
32 devices in a mesh: tensor: 4 (over x, core), replica: 4 (over z), fsdp: 2 (over y).
Axes of the slice: x: 2, y: 2, z: 4, core: 2. Of those that a mesh axis runs over, the one named last changes fastest.
Arguments:
- gradients: bfloat16 [4, 128, 28672], P('replica', 'fsdp', 'tensor'), may hold values from -6 to 6
- seeds: int32 [2], replicated, may hold values from 0 to 1073741823
- adam_step: int32 [1], replicated, may hold values from 1 to 8
- first_moment: float32 [128, 28672], P(('fsdp', 'replica'), 'tensor'), may hold values from -0.6 to 0.6
- second_moment: float32 [128, 28672], P(('fsdp', 'replica'), 'tensor'), may hold values from 0.001 to 0.1
Outputs:
- new_first: float32 [128, 28672], P(('fsdp', 'replica'), 'tensor')
- new_second: float32 [128, 28672], P(('fsdp', 'replica'), 'tensor')
- step_update: float32 [128, 28672], P(('fsdp', 'replica'), 'tensor')
All inputs are finite; a program needn't handle non-finite values.
Results may differ from a plain program's by a relative error of at most 0.012.
The roundings to bfloat16 on the way count: a program that leaves them out, or rounds other values in their place, can miss the bound.
Values may be sent and summed in bfloat16 or wider, within the bound.
No kernel may reach another device: no remote copies, remote signals or barrier semaphores. Data moves between devices by JAX's collectives and lax.ppermute only.
A program may use at most 64 MiB of HBM per device.

v0:
```python
import math

import jax
import jax.numpy as jnp
from jax import lax
from jax.sharding import PartitionSpec as P

RANK = 512


def scramble(value):
    value = value ^ lax.shift_right_logical(value, jnp.full_like(value, 16))
    value = value * jnp.int32(-2048144789)
    value = value ^ lax.shift_right_logical(value, jnp.full_like(value, 13))
    value = value * jnp.int32(-1028477387)
    value = value ^ lax.shift_right_logical(value, jnp.full_like(value, 16))
    return value


def projection_block(first_column, columns, rank, seeds):
    seed_key = seeds[0] ^ seeds[1] * jnp.int32(668265263)
    column = lax.broadcasted_iota(jnp.int32, (columns, rank), 0) + first_column
    entry = lax.broadcasted_iota(jnp.int32, (columns, rank), 1)
    counter = (column * jnp.int32(rank) + entry) * jnp.int32(2)
    hash_a = scramble(counter * jnp.int32(-1640531535) ^ seed_key)
    hash_b = scramble((counter + jnp.int32(1)) * jnp.int32(-1640531535) ^ seed_key)
    inverse = 1.0 / 16777216.0
    uniform_a = (
        lax.shift_right_logical(hash_a, jnp.full_like(hash_a, 8)).astype(jnp.float32) + 0.5
    ) * inverse
    uniform_b = (
        lax.shift_right_logical(hash_b, jnp.full_like(hash_b, 8)).astype(jnp.float32) + 0.5
    ) * inverse
    gauss = jnp.sqrt(-2.0 * jnp.log(uniform_a)) * jnp.cos(6.283185307179586 * uniform_b)
    return (gauss * rank ** (-0.5)).astype(jnp.bfloat16)


def per_device(gradients, seeds, adam_step, first_moment, second_moment):
    gradient = gradients[0]
    columns = gradient.shape[1]
    replicas = lax.axis_size("replica")
    column_start = lax.axis_index("tensor") * jnp.int32(columns)
    piece_cols = math.gcd(columns, 512)
    blocks = columns // piece_cols
    starts = column_start + lax.iota(jnp.int32, blocks) * jnp.int32(piece_cols)
    tiles = lax.map(lambda first: projection_block(first, piece_cols, RANK, seeds), starts)
    projection = tiles.reshape(columns, RANK)
    partial_value = jnp.dot(gradient, projection, preferred_element_type=jnp.float32) * (
        1.0 / replicas
    )
    share = lax.psum_scatter(partial_value, "replica", scatter_dimension=0, tiled=True)
    sketch = lax.psum(share, "tensor")
    sketch_rounded = sketch.astype(jnp.bfloat16)
    estimate = lax.dot_general(
        sketch_rounded, projection, (((1,), (1,)), ((), ())), preferred_element_type=jnp.float32
    )
    new_first = 0.9 * first_moment + 0.1 * estimate
    new_second = 0.95 * second_moment + 0.05 * estimate * estimate
    step_float = adam_step[0].astype(jnp.float32)
    fix_first = 1.0 - jnp.power(jnp.float32(0.9), step_float)
    fix_second = 1.0 - jnp.power(jnp.float32(0.95), step_float)
    step_update = new_first / fix_first / (jnp.sqrt(new_second / fix_second) + 1e-08)
    return (new_first, new_second, step_update)


def solution(mesh):
    placed = (
        P("replica", "fsdp", "tensor"),
        P(),
        P(),
        P(("fsdp", "replica"), "tensor"),
        P(("fsdp", "replica"), "tensor"),
    )
    return jax.shard_map(
        per_device,
        mesh=mesh,
        in_specs=placed,
        out_specs=(
            P(("fsdp", "replica"), "tensor"),
            P(("fsdp", "replica"), "tensor"),
            P(("fsdp", "replica"), "tensor"),
        ),
        check_vma=False,
    )
```

profile of v0, /device:TPU:0, one launch (start us, length us, event | category | flops | bytes accessed | tf_op | source)
XLA Modules:
  0.0 164.6 jit_solution(9987295474891056560)
XLA Ops:
  7.2 1.3 fusion.26
  9.9 99.4 %while.12 = (s32[]{:T(128)}, bf16[14,512,512]{2,1,0:T(8,128)(2,1)}, s32[14]{0:T(128)S(1)}, s32[]{:T(128)}, s32[]{:T(128)}) while((s32[]{:T(128)}, bf16[14,512,512]{2,1,0:T(8,128)(2,1)}, s32[14]{0:T(128)S(1)}, s32[]{:T(128)}, s32[]{:T(128)}) %tuple.33), condition=%wide.region_1.2_spmd, body=%wide.region_0.1_spmd.sunk | while | flops 9176066 | bytes 529485 | solution.py:46
  10.5 0.6 add_multiply_fusion.2
  11.1 5.9 %fusion.31 = bf16[14,512,512]{2,1,0:T(8,128)(2,1)} fusion(bf16[14,512,512]{2,1,0:T(8,128)(2,1)} %get-tuple-element.105, s32[]{:T(128)} %get-tuple-element.104, s32[]{:T(128)} %get-tuple-element.112, s32[512]{0:T(512)S(1)} %add_multiply_fusion.2), kind=kLoop, calls=%fused_computation.25.clone.1 | loop fusion | flops 9175040 | bytes 527360 | tf_op jit(solution)/shard_map/while/body/jit(dynamic_update_index_in_dim)/dynamic_update_slice | solution.py:46
  17.6 0.6 add_multiply_fusion.2
  18.2 5.9 %fusion.31 = bf16[14,512,512]{2,1,0:T(8,128)(2,1)} fusion(bf16[14,512,512]{2,1,0:T(8,128)(2,1)} %get-tuple-element.105, s32[]{:T(128)} %get-tuple-element.104, s32[]{:T(128)} %get-tuple-element.112, s32[512]{0:T(512)S(1)} %add_multiply_fusion.2), kind=kLoop, calls=%fused_computation.25.clone.1 | loop fusion | flops 9175040 | bytes 527360 | tf_op jit(solution)/shard_map/while/body/jit(dynamic_update_index_in_dim)/dynamic_update_slice | solution.py:46
  24.7 0.6 add_multiply_fusion.2
  25.3 5.9 %fusion.31 = bf16[14,512,512]{2,1,0:T(8,128)(2,1)} fusion(bf16[14,512,512]{2,1,0:T(8,128)(2,1)} %get-tuple-element.105, s32[]{:T(128)} %get-tuple-element.104, s32[]{:T(128)} %get-tuple-element.112, s32[512]{0:T(512)S(1)} %add_multiply_fusion.2), kind=kLoop, calls=%fused_computation.25.clone.1 | loop fusion | flops 9175040 | bytes 527360 | tf_op jit(solution)/shard_map/while/body/jit(dynamic_update_index_in_dim)/dynamic_update_slice | solution.py:46
  31.8 0.6 add_multiply_fusion.2
  32.4 5.9 %fusion.31 = bf16[14,512,512]{2,1,0:T(8,128)(2,1)} fusion(bf16[14,512,512]{2,1,0:T(8,128)(2,1)} %get-tuple-element.105, s32[]{:T(128)} %get-tuple-element.104, s32[]{:T(128)} %get-tuple-element.112, s32[512]{0:T(512)S(1)} %add_multiply_fusion.2), kind=kLoop, calls=%fused_computation.25.clone.1 | loop fusion | flops 9175040 | bytes 527360 | tf_op jit(solution)/shard_map/while/body/jit(dynamic_update_index_in_dim)/dynamic_update_slice | solution.py:46
  38.9 0.6 add_multiply_fusion.2
  39.5 5.8 %fusion.31 = bf16[14,512,512]{2,1,0:T(8,128)(2,1)} fusion(bf16[14,512,512]{2,1,0:T(8,128)(2,1)} %get-tuple-element.105, s32[]{:T(128)} %get-tuple-element.104, s32[]{:T(128)} %get-tuple-element.112, s32[512]{0:T(512)S(1)} %add_multiply_fusion.2), kind=kLoop, calls=%fused_computation.25.clone.1 | loop fusion | flops 9175040 | bytes 527360 | tf_op jit(solution)/shard_map/while/body/jit(dynamic_update_index_in_dim)/dynamic_update_slice | solution.py:46
  46.0 0.6 add_multiply_fusion.2
  46.6 5.9 %fusion.31 = bf16[14,512,512]{2,1,0:T(8,128)(2,1)} fusion(bf16[14,512,512]{2,1,0:T(8,128)(2,1)} %get-tuple-element.105, s32[]{:T(128)} %get-tuple-element.104, s32[]{:T(128)} %get-tuple-element.112, s32[512]{0:T(512)S(1)} %add_multiply_fusion.2), kind=kLoop, calls=%fused_computation.25.clone.1 | loop fusion | flops 9175040 | bytes 527360 | tf_op jit(solution)/shard_map/while/body/jit(dynamic_update_index_in_dim)/dynamic_update_slice | solution.py:46
  53.0 0.6 add_multiply_fusion.2
  53.7 5.9 %fusion.31 = bf16[14,512,512]{2,1,0:T(8,128)(2,1)} fusion(bf16[14,512,512]{2,1,0:T(8,128)(2,1)} %get-tuple-element.105, s32[]{:T(128)} %get-tuple-element.104, s32[]{:T(128)} %get-tuple-element.112, s32[512]{0:T(512)S(1)} %add_multiply_fusion.2), kind=kLoop, calls=%fused_computation.25.clone.1 | loop fusion | flops 9175040 | bytes 527360 | tf_op jit(solution)/shard_map/while/body/jit(dynamic_update_index_in_dim)/dynamic_update_slice | solution.py:46
  60.8 5.9 %fusion.31 = bf16[14,512,512]{2,1,0:T(8,128)(2,1)} fusion(bf16[14,512,512]{2,1,0:T(8,128)(2,1)} %get-tuple-element.105, s32[]{:T(128)} %get-tuple-element.104, s32[]{:T(128)} %get-tuple-element.112, s32[512]{0:T(512)S(1)} %add_multiply_fusion.2), kind=kLoop, calls=%fused_computation.25.clone.1 | loop fusion | flops 9175040 | bytes 527360 | tf_op jit(solution)/shard_map/while/body/jit(dynamic_update_index_in_dim)/dynamic_update_slice | solution.py:46
  67.9 5.9 %fusion.31 = bf16[14,512,512]{2,1,0:T(8,128)(2,1)} fusion(bf16[14,512,512]{2,1,0:T(8,128)(2,1)} %get-tuple-element.105, s32[]{:T(128)} %get-tuple-element.104, s32[]{:T(128)} %get-tuple-element.112, s32[512]{0:T(512)S(1)} %add_multiply_fusion.2), kind=kLoop, calls=%fused_computation.25.clone.1 | loop fusion | flops 9175040 | bytes 527360 | tf_op jit(solution)/shard_map/while/body/jit(dynamic_update_index_in_dim)/dynamic_update_slice | solution.py:46
  74.3 0.6 add_multiply_fusion.2
  75.0 5.9 %fusion.31 = bf16[14,512,512]{2,1,0:T(8,128)(2,1)} fusion(bf16[14,512,512]{2,1,0:T(8,128)(2,1)} %get-tuple-element.105, s32[]{:T(128)} %get-tuple-element.104, s32[]{:T(128)} %get-tuple-element.112, s32[512]{0:T(512)S(1)} %add_multiply_fusion.2), kind=kLoop, calls=%fused_computation.25.clone.1 | loop fusion | flops 9175040 | bytes 527360 | tf_op jit(solution)/shard_map/while/body/jit(dynamic_update_index_in_dim)/dynamic_update_slice | solution.py:46
  82.1 5.9 %fusion.31 = bf16[14,512,512]{2,1,0:T(8,128)(2,1)} fusion(bf16[14,512,512]{2,1,0:T(8,128)(2,1)} %get-tuple-element.105, s32[]{:T(128)} %get-tuple-element.104, s32[]{:T(128)} %get-tuple-element.112, s32[512]{0:T(512)S(1)} %add_multiply_fusion.2), kind=kLoop, calls=%fused_computation.25.clone.1 | loop fusion | flops 9175040 | bytes 527360 | tf_op jit(solution)/shard_map/while/body/jit(dynamic_update_index_in_dim)/dynamic_update_slice | solution.py:46
  88.5 0.6 add_multiply_fusion.2
  89.2 5.9 %fusion.31 = bf16[14,512,512]{2,1,0:T(8,128)(2,1)} fusion(bf16[14,512,512]{2,1,0:T(8,128)(2,1)} %get-tuple-element.105, s32[]{:T(128)} %get-tuple-element.104, s32[]{:T(128)} %get-tuple-element.112, s32[512]{0:T(512)S(1)} %add_multiply_fusion.2), kind=kLoop, calls=%fused_computation.25.clone.1 | loop fusion | flops 9175040 | bytes 527360 | tf_op jit(solution)/shard_map/while/body/jit(dynamic_update_index_in_dim)/dynamic_update_slice | solution.py:46
  95.6 0.6 add_multiply_fusion.2
  96.3 5.9 %fusion.31 = bf16[14,512,512]{2,1,0:T(8,128)(2,1)} fusion(bf16[14,512,512]{2,1,0:T(8,128)(2,1)} %get-tuple-element.105, s32[]{:T(128)} %get-tuple-element.104, s32[]{:T(128)} %get-tuple-element.112, s32[512]{0:T(512)S(1)} %add_multiply_fusion.2), kind=kLoop, calls=%fused_computation.25.clone.1 | loop fusion | flops 9175040 | bytes 527360 | tf_op jit(solution)/shard_map/while/body/jit(dynamic_update_index_in_dim)/dynamic_update_slice | solution.py:46
  103.4 5.9 %fusion.31 = bf16[14,512,512]{2,1,0:T(8,128)(2,1)} fusion(bf16[14,512,512]{2,1,0:T(8,128)(2,1)} %get-tuple-element.105, s32[]{:T(128)} %get-tuple-element.104, s32[]{:T(128)} %get-tuple-element.112, s32[512]{0:T(512)S(1)} %add_multiply_fusion.2), kind=kLoop, calls=%fused_computation.25.clone.1 | loop fusion | flops 9175040 | bytes 527360 | tf_op jit(solution)/shard_map/while/body/jit(dynamic_update_index_in_dim)/dynamic_update_slice | solution.py:46
  109.2 5.2 %fusion.20 = f32[64,512]{0,1:T(8,128)S(1)} fusion(bf16[7168,512]{1,0:T(8,128)(2,1)} %bitcast.16, bf16[1,64,7168]{2,1,0:T(8,128)(2,1)S(1)} %copy-done), kind=kOutput, calls=%fused_computation.28 | convolution fusion | flops 469794816 | bytes 8388608 | tf_op jit(solution)/shard_map/dot_general | solution.py:48
  114.4 0.8 copy.8
  116.0 21.6 %reduce-scatter.4.cloned.1.call-done = f32[16,512]{1,0:T(8,128)} async-done(((f32[64,512]{1,0:T(8,128)}), f32[16,512]{1,0:T(8,128)}) %reduce-scatter.4.cloned.1.call-update) | async-done | bytes 32784
  137.5 0.9 copy.9
  138.4 13.1 %psum.7 = bf16[16,512]{0,1:T(8,128)(2,1)S(1)} all-reduce(f32[16,512]{0,1:T(8,128)S(1)} %copy.9), channel_id=1, replica_groups=mesh['tensor'=4,'replica'=4,'fsdp'=2] {'tensor'}, use_global_device_ids=true, to_apply=%region_3.4 | all-reduce | flops 8192 | bytes 49152 | tf_op jit(solution)/shard_map/psum | solution.py:52
  151.5 6.2 %multiply_divide_fusion = (f32[16,7168]{1,0:T(8,128)}, f32[16,7168]{1,0:T(8,128)}, f32[16,7168]{1,0:T(8,128)}) fusion(f32[]{:T(128)} %bitcast.6, f32[]{:T(128)} %bitcast.5, f32[16,7168]{1,0:T(8,128)S(1)} %copy-done.1, f32[16,7168]{1,0:T(8,128)S(1)} %copy-done.2, bf16[16,512]{0,1:T(8,128)(2,1)S(1)} %psum.7, bf16[7168,512]{1,0:T(8,128)(2,1)} %bitcast.17), kind=kOutput, calls=%fused_computation.32 | convolution fusion | flops 118702080 | bytes 9650184 | tf_op jit(solution)/shard_map/dot_general | solution.py:54
  (28 shorter events, 10.8 us)
Async XLA Ops:
  7.2 102.1 %copy-start = (bf16[1,64,7168]{2,1,0:T(8,128)(2,1)S(1)}, bf16[1,64,7168]{2,1,0:T(8,128)(2,1)}, u32[]{:S(2)}) copy-start(bf16[1,64,7168]{2,1,0:T(8,128)(2,1)} %param.7) | copy-start | bytes 2752516
  7.2 130.4 %reduce-scatter.4.cloned.1.call-start = ((), (), s32[]{:S(2)}) async-start(), calls=%async_computation.1 | async-start | bytes 163840
  9.9 141.6 %copy-start.1 = (f32[16,7168]{1,0:T(8,128)S(1)}, f32[16,7168]{1,0:T(8,128)}, u32[]{:S(2)}) copy-start(f32[16,7168]{1,0:T(8,128)} %param.11) | copy-start | bytes 1376260
  9.9 141.6 %copy-start.2 = (f32[16,7168]{1,0:T(8,128)S(1)}, f32[16,7168]{1,0:T(8,128)}, u32[]{:S(2)}) copy-start(f32[16,7168]{1,0:T(8,128)} %param.10) | copy-start | bytes 1376260
Sparse Core Ops, SparseCore 0:
  115.3 22.1 reduce-scatter.3
where the time goes:
time: 165 us
  other arithmetic  91.1 us (55%)
  waiting for transfers between devices  21.6 us (13%)
  between operations  16.1 us (10%)
  blocking collectives  13.1 us (8%)
  matrix products  11.4 us (7%)
  local copies, waits for them, and re-layouts  11.2 us (7%)
    dynamic_update_slice x14, other arithmetic, per_device(): lax.map(lambda first: projection_block(first, piece_cols, RANK, seeds), s...  82 us
    unnamed x2, waiting for transfers between devices  21.6 us
    psum x1, blocking collectives, per_device(): sketch = lax.psum(share, 'tensor')  13.1 us
    mul x14, other arithmetic, projection_block(): counter = (column * jnp.int32(rank) + entry) * jnp.int32(2)  9.07 us
    dynamic_slice x14, local copies, waits for them, and re-layouts, per_device(): lax.map(lambda first: projection_block(first, piece_cols, RANK, seeds), s...  8.15 us
    dot_general x1, matrix products, per_device(): lax.dot_general(sketch_rounded, projection, (((1,), (1,)), ((), ())), pre...  6.19 us
    dot_general x1, matrix products, per_device(): jnp.dot(gradient, projection, preferred_element_type=jnp.float32)  5.17 us
  transfers between devices with their start and end apart: 1, of which 1 were waited for; matrix products, arithmetic and copies ran while one was open for 0% of the time, Pallas kernels for 0%

commit v1 on v0

--- a/solution.py
+++ b/solution.py
@@ -6,6 +6,7 @@
 from jax.sharding import PartitionSpec as P
 
 RANK = 512
+GROUP = ("fsdp", "replica")
 
 
 def scramble(value):
@@ -35,7 +36,17 @@
     return (gauss * rank ** (-0.5)).astype(jnp.bfloat16)
 
 
-def per_device(gradients, seeds, adam_step, first_moment, second_moment):
+def adam(first_moment, second_moment, estimate, adam_step):
+    new_first = 0.9 * first_moment + 0.1 * estimate
+    new_second = 0.95 * second_moment + 0.05 * estimate * estimate
+    step_float = adam_step[0].astype(jnp.float32)
+    fix_first = 1.0 - jnp.power(jnp.float32(0.9), step_float)
+    fix_second = 1.0 - jnp.power(jnp.float32(0.95), step_float)
+    step_update = new_first / fix_first / (jnp.sqrt(new_second / fix_second) + 1e-08)
+    return (new_first, new_second, step_update)
+
+
+def per_device_whole(gradients, seeds, adam_step, first_moment, second_moment):
     gradient = gradients[0]
     columns = gradient.shape[1]
     replicas = lax.axis_size("replica")
@@ -54,13 +65,46 @@
     estimate = lax.dot_general(
         sketch_rounded, projection, (((1,), (1,)), ((), ())), preferred_element_type=jnp.float32
     )
-    new_first = 0.9 * first_moment + 0.1 * estimate
-    new_second = 0.95 * second_moment + 0.05 * estimate * estimate
-    step_float = adam_step[0].astype(jnp.float32)
-    fix_first = 1.0 - jnp.power(jnp.float32(0.9), step_float)
-    fix_second = 1.0 - jnp.power(jnp.float32(0.95), step_float)
-    step_update = new_first / fix_first / (jnp.sqrt(new_second / fix_second) + 1e-08)
-    return (new_first, new_second, step_update)
+    return adam(first_moment, second_moment, estimate, adam_step)
+
+
+def per_device(gradients, seeds, adam_step, first_moment, second_moment):
+    gradient = gradients[0]
+    rows, columns = gradient.shape
+    n_fsdp = lax.axis_size("fsdp")
+    n_rep = lax.axis_size("replica")
+    n_group = n_fsdp * n_rep
+    width = columns // n_group
+    if columns % (n_group * 128) != 0:
+        return per_device_whole(gradients, seeds, adam_step, first_moment, second_moment)
+    member = lax.axis_index(GROUP)
+    first = lax.axis_index("tensor") * jnp.int32(columns) + member * jnp.int32(width)
+
+    projection = lax.optimization_barrier(projection_block(first, width, RANK, seeds))
+
+    pieces = gradient.reshape(rows, n_group, width).transpose(1, 0, 2)
+    held = lax.all_to_all(pieces, GROUP, 0, 0, tiled=True)
+    held = held.reshape(n_fsdp, n_rep, rows, width)
+
+    partial_value = None
+    for r in range(n_rep):
+        term = lax.dot_general(
+            held[:, r], projection, (((2,), (0,)), ((), ())),
+            preferred_element_type=jnp.float32,
+        )
+        partial_value = term if partial_value is None else partial_value + term
+    partial_value = partial_value.reshape(n_fsdp * rows, RANK) * (1.0 / n_rep)
+    sketch = lax.psum(partial_value, ("tensor",) + GROUP)
+    sketch_rounded = sketch.astype(jnp.bfloat16)
+
+    estimate = lax.dot_general(
+        sketch_rounded, projection, (((1,), (1,)), ((), ())), preferred_element_type=jnp.float32
+    )
+    out_rows = first_moment.shape[0]
+    estimate = estimate.reshape(n_group, out_rows, width)
+    estimate = lax.all_to_all(estimate, GROUP, 0, 0, tiled=True)
+    estimate = estimate.transpose(1, 0, 2).reshape(out_rows, columns)
+    return adam(first_moment, second_moment, estimate, adam_step)
 
 
 def solution(mesh):

time: 165 us -> 96.5 us (0.58)
  other arithmetic: 91.1 us -> 10.4 us
  blocking collectives: 13.1 us -> 40.4 us
  between operations: 16.1 us -> 2.75 us
  starting transfers between devices: 0.04 us -> 11.8 us
  matrix products: 11.4 us -> 2.47 us
  local copies, waits for them, and re-layouts: 11.2 us -> 3.04 us
  waiting for transfers between devices: 21.6 us -> 25.1 us
    dynamic_update_slice x14 -> x0, other arithmetic: 82 us -> none  [per_device(): lax.map(lambda first: projection_block(first, piece_cols, RANK, seeds), s...]
    psum x1, blocking collectives: 13.1 us -> 40.4 us  [per_device(): sketch = lax.psum(partial_value, ('tensor',) + GROUP)]
    all_to_all x0 -> x2, waiting for transfers between devices: none -> 25.1 us  [the longest x1 12.7 us: per_device(): held = lax.all_to_all(pieces, GROUP, 0, 0, tiled=True)]
    unnamed x2 -> x0, waiting for transfers between devices: 21.6 us -> none
    all_to_all x0 -> x2, starting transfers between devices: none -> 11.8 us  [the longest x1 7.44 us: per_device(): held = lax.all_to_all(pieces, GROUP, 0, 0, tiled=True)]
    convert_element_type x0 -> x1, other arithmetic: none -> 9.2 us  [projection_block(): return (gauss * rank ** (-0.5)).astype(jnp.bfloat16)]
    mul x14 -> x1, other arithmetic: 9.07 us -> 0.01 us  [projection_block(): counter = (column * jnp.int32(rank) + entry) * jnp.int32(2)]
    dynamic_slice x14 -> x0, local copies, waits for them, and re-layouts: 8.15 us -> none  [per_device(): lax.map(lambda first: projection_block(first, piece_cols, RANK, seeds), s...]
  transfers between devices with their start and end apart: 1 -> 2, of which waited for: 1 -> 2; matrix products, arithmetic and copies ran while one was open for 0% -> 10% of each run, Pallas kernels for 0% -> 0%
where the time goes in v1:
time: 96.5 us; the launch traced here: 96.1 us
  blocking collectives  40.4 us (42%)
  waiting for transfers between devices  25.1 us (26%)
  starting transfers between devices  11.8 us (12%)
  other arithmetic  10.4 us (11%)
  local copies, waits for them, and re-layouts  3.04 us (3%)
  between operations  2.75 us (3%)
  matrix products  2.47 us (3%)
    psum x1, blocking collectives, per_device(): sketch = lax.psum(partial_value, ('tensor',) + GROUP)  40.4 us
    all_to_all x1, waiting for transfers between devices, per_device(): held = lax.all_to_all(pieces, GROUP, 0, 0, tiled=True)  12.7 us
    all_to_all x1, waiting for transfers between devices, per_device(): estimate = lax.all_to_all(estimate, GROUP, 0, 0, tiled=True)  12.4 us
    convert_element_type x1, other arithmetic, projection_block(): return (gauss * rank ** (-0.5)).astype(jnp.bfloat16)  9.2 us
    all_to_all x1, starting transfers between devices, per_device(): held = lax.all_to_all(pieces, GROUP, 0, 0, tiled=True)  7.44 us
    all_to_all x1, starting transfers between devices, per_device(): estimate = lax.all_to_all(estimate, GROUP, 0, 0, tiled=True)  4.35 us
  transfers between devices with their start and end apart: 2, of which 2 were waited for; matrix products, arithmetic and copies ran while one was open for 10% of the time, Pallas kernels for 0%

profile of v1, /device:TPU:0, one launch (start us, length us, event | category | flops | bytes accessed | tf_op | source)
XLA Modules:
  0.0 96.1 jit_solution(1003083572574440337)
XLA Ops:
  0.6 1.3 %copy.31 = bf16[8,8,8,896]{3,2,1,0:T(8,128)(2,1)S(1)} copy(bf16[8,8,8,896]{3,1,2,0:T(8,128)(2,1)} %bitcast.55) | data formatting | bytes 1835008
  2.0 1.1 %copy.20 = bf16[8,64,896]{2,1,0:T(8,128)(2,1)} copy(bf16[8,64,896]{2,0,1:T(8,128)(2,1)S(1)} %bitcast.51) | data formatting | bytes 1835008 | tf_op jit(solution)/shard_map/transpose | solution.py:85
  3.1 0.0 copy-start.2
  3.1 7.4 %all-to-all-start = ((bf16[8,64,896]{2,1,0:T(8,128)(2,1)}), bf16[8,64,896]{2,1,0:T(8,128)(2,1)S(1)}, u32[]{:S(2)}, u32[]{:S(2)}) async-start(bf16[8,64,896]{2,1,0:T(8,128)(2,1)} %copy.20), calls=%async_computation | async-start | bytes 1835008 | tf_op jit(solution)/shard_map/all_to_all | solution.py:86
  10.5 0.0 copy-done.2
  10.5 0.6 fusion.29
  12.4 9.2 %fusion.18 = bf16[896,512]{1,0:T(8,128)(2,1)S(1)} fusion(s32[]{:T(128)} %bitcast, s32[896]{0:T(1024)S(1)} %add_multiply_fusion), kind=kLoop, calls=%fused_computation.24 | loop fusion | flops 16056320 | bytes 921092 | tf_op jit(solution)/shard_map/convert_element_type | solution.py:36
  21.6 12.7 %all-to-all-done = bf16[8,64,896]{2,1,0:T(8,128)(2,1)S(1)} async-done(((bf16[8,64,896]{2,1,0:T(8,128)(2,1)}), bf16[8,64,896]{2,1,0:T(8,128)(2,1)S(1)}, u32[]{:S(2)}, u32[]{:S(2)}) %all-to-all-start) | async-done | bytes 917536 | tf_op jit(solution)/shard_map/all_to_all | solution.py:86
  34.3 0.3 fusion.23
  34.6 0.3 convolution_add_fusion.2
  34.9 0.3 convolution_add_fusion.1
  35.3 0.3 fusion.19
  35.6 40.4 %all-reduce.1 = bf16[128,512]{1,0:T(8,128)(2,1)S(1)} all-reduce(f32[128,512]{1,0:T(8,128)S(1)} %bitcast.54), channel_id=1, replica_groups=mesh['tensor'=4,'replica'=4,'fsdp'=2] {'tensor','fsdp','replica'}, use_global_device_ids=true, to_apply=%region_0.0 | all-reduce | flops 65536 | bytes 393216 | tf_op jit(solution)/shard_map/psum | solution.py:97
  76.0 1.2 %fusion.30 = f32[128,896]{1,0:T(8,128)} fusion(bf16[128,512]{1,0:T(8,128)(2,1)S(1)} %all-reduce.1, bf16[896,512]{1,0:T(8,128)(2,1)S(1)} %fusion.18), kind=kOutput, calls=%fused_computation.46 | convolution fusion | flops 117440512 | bytes 1507328 | tf_op jit(solution)/shard_map/dot_general | solution.py:100
  77.3 0.0 copy-start
  77.3 0.0 copy-start.1
  77.3 4.4 %all-to-all-start.1 = ((f32[8,16,896]{2,1,0:T(8,128)}), f32[8,16,896]{2,1,0:T(8,128)S(1)}, u32[]{:S(2)}, u32[]{:S(2)}) async-start(f32[8,16,896]{2,1,0:T(8,128)} %bitcast.10), calls=%async_computation.1 | async-start | bytes 917504 | tf_op jit(solution)/shard_map/all_to_all | solution.py:105
  82.3 12.4 %all-to-all-done.1 = f32[8,16,896]{2,1,0:T(8,128)S(1)} async-done(((f32[8,16,896]{2,1,0:T(8,128)}), f32[8,16,896]{2,1,0:T(8,128)S(1)}, u32[]{:S(2)}, u32[]{:S(2)}) %all-to-all-start.1) | async-done | bytes 458784 | tf_op jit(solution)/shard_map/all_to_all | solution.py:105
  94.8 0.0 copy-done
  94.8 0.0 copy-done.1
  94.8 1.2 %multiply_divide_fusion = (f32[16,7168]{1,0:T(8,128)}, f32[16,7168]{1,0:T(8,128)}, f32[16,7168]{1,0:T(8,128)}) fusion(f32[]{:T(128)} %bitcast.13, f32[]{:T(128)} %bitcast.12, f32[16,7168]{1,0:T(8,128)S(1)} %bitcast.52, f32[16,7168]{1,0:T(8,128)S(1)} %copy-done, f32[16,7168]{1,0:T(8,128)S(1)} %copy-done.1), kind=kLoop, calls=%fused_computation.36 | loop fusion | flops 1261568 | bytes 2752520 | tf_op jit(solution)/shard_map/div | solution.py:45
  (2 shorter events, 0.0 us)
Async XLA Ops:
  3.1 7.4 %copy-start.2 = (s32[2]{0:T(128)S(1)}, s32[2]{0:T(128)}, u32[]{:S(2)}) copy-start(s32[2]{0:T(128)} %param.6) | copy-start | bytes 28
  3.1 31.3 %all-to-all-start = ((bf16[8,64,896]{2,1,0:T(8,128)(2,1)}), bf16[8,64,896]{2,1,0:T(8,128)(2,1)S(1)}, u32[]{:S(2)}, u32[]{:S(2)}) async-start(bf16[8,64,896]{2,1,0:T(8,128)(2,1)} %copy.20), calls=%async_computation | async-start | bytes 1835008 | tf_op jit(solution)/shard_map/all_to_all | solution.py:86
  77.3 17.6 %copy-start = (f32[16,7168]{1,0:T(8,128)S(1)}, f32[16,7168]{1,0:T(8,128)}, u32[]{:S(2)}) copy-start(f32[16,7168]{1,0:T(8,128)} %param.9) | copy-start | bytes 1376260
  77.3 17.6 %copy-start.1 = (f32[16,7168]{1,0:T(8,128)S(1)}, f32[16,7168]{1,0:T(8,128)}, u32[]{:S(2)}) copy-start(f32[16,7168]{1,0:T(8,128)} %param.8) | copy-start | bytes 1376260
  77.3 17.5 %all-to-all-start.1 = ((f32[8,16,896]{2,1,0:T(8,128)}), f32[8,16,896]{2,1,0:T(8,128)S(1)}, u32[]{:S(2)}, u32[]{:S(2)}) async-start(f32[8,16,896]{2,1,0:T(8,128)} %bitcast.10), calls=%async_computation.1 | async-start | bytes 917504 | tf_op jit(solution)/shard_map/all_to_all | solution.py:105

commit v2 on v1

--- a/solution.py
+++ b/solution.py
@@ -68,6 +68,31 @@
     return adam(first_moment, second_moment, estimate, adam_step)
 
 
+def exchange_sum(value, axes):
+    steps = []
+    for axis in axes:
+        size = lax.axis_size(axis)
+        step = 1
+        while step < size:
+            steps.append((axis, step, [(i, i ^ step) for i in range(size)]))
+            step *= 2
+    bits = []
+    for axis, step, pairs in steps:
+        bit = (lax.axis_index(axis) // step) % 2
+        half = value.shape[0] // 2
+        lower, upper = value[:half], value[half:]
+        keep = jnp.where(bit == 0, lower, upper)
+        send = jnp.where(bit == 0, upper, lower)
+        value = keep + lax.ppermute(send, axis, pairs)
+        bits.append(bit)
+    for (axis, step, pairs), bit in zip(reversed(steps), reversed(bits)):
+        got = lax.ppermute(value, axis, pairs)
+        value = jnp.where(
+            bit == 0, jnp.concatenate([value, got], 0), jnp.concatenate([got, value], 0)
+        )
+    return value
+
+
 def per_device(gradients, seeds, adam_step, first_moment, second_moment):
     gradient = gradients[0]
     rows, columns = gradient.shape
@@ -94,7 +119,7 @@
         )
         partial_value = term if partial_value is None else partial_value + term
     partial_value = partial_value.reshape(n_fsdp * rows, RANK) * (1.0 / n_rep)
-    sketch = lax.psum(partial_value, ("tensor",) + GROUP)
+    sketch = exchange_sum(partial_value, ("tensor",) + GROUP)
     sketch_rounded = sketch.astype(jnp.bfloat16)
 
     estimate = lax.dot_general(

time: 96.5 us -> 92.2 us (0.955)
  blocking collectives: 40.4 us -> 0 us
  waiting for transfers between devices: 25.1 us -> 57.1 us
  starting transfers between devices: 11.8 us -> 15.8 us
    psum x1 -> x0, blocking collectives: 40.4 us -> none  [per_device(): sketch = lax.psum(partial_value, ('tensor',) + GROUP)]
    ppermute x0 -> x10, waiting for transfers between devices: none -> 30.6 us  [the longest x5 15.7 us: exchange_sum(): value = keep + lax.ppermute(send, axis, pairs)]
    ppermute x0 -> x10, starting transfers between devices: none -> 4.71 us  [the longest x5 2.39 us: exchange_sum(): value = keep + lax.ppermute(send, axis, pairs)]
    all_to_all x1, waiting for transfers between devices: 12.4 us -> 13.8 us  [per_device(): estimate = lax.all_to_all(estimate, GROUP, 0, 0, tiled=True)]
  transfers between devices with their start and end apart: 2 -> 12, of which waited for: 2 -> 12; matrix products, arithmetic and copies ran while one was open for 10% -> 11% of each run, Pallas kernels for 0% -> 0%
where the time goes in v2:
time: 92.2 us; the launch traced here: 91.9 us
  waiting for transfers between devices  57.1 us (62%)
  starting transfers between devices  15.8 us (17%)
  other arithmetic  10.6 us (11%)
  local copies, waits for them, and re-layouts  3.02 us (3%)
  between operations  2.94 us (3%)
  matrix products  2.47 us (3%)
    ppermute x5, waiting for transfers between devices, exchange_sum(): value = keep + lax.ppermute(send, axis, pairs)  15.7 us
    ppermute x5, waiting for transfers between devices, exchange_sum(): got = lax.ppermute(value, axis, pairs)  15 us
    all_to_all x1, waiting for transfers between devices, per_device(): estimate = lax.all_to_all(estimate, GROUP, 0, 0, tiled=True)  13.8 us
    all_to_all x1, waiting for transfers between devices, per_device(): held = lax.all_to_all(pieces, GROUP, 0, 0, tiled=True)  12.7 us
    convert_element_type x1, other arithmetic, projection_block(): return (gauss * rank ** (-0.5)).astype(jnp.bfloat16)  9.2 us
    all_to_all x1, starting transfers between devices, per_device(): held = lax.all_to_all(pieces, GROUP, 0, 0, tiled=True)  7.44 us
    all_to_all x1, starting transfers between devices, per_device(): estimate = lax.all_to_all(estimate, GROUP, 0, 0, tiled=True)  3.61 us
    ppermute x5, starting transfers between devices, exchange_sum(): value = keep + lax.ppermute(send, axis, pairs)  2.39 us
  transfers between devices with their start and end apart: 12, of which 12 were waited for; matrix products, arithmetic and copies ran while one was open for 11% of the time, Pallas kernels for 0%

profile of v2, /device:TPU:0, one launch (start us, length us, event | category | flops | bytes accessed | tf_op | source)
XLA Modules:
  0.0 91.9 jit_solution(7445819106544874915)
XLA Ops:
  0.6 1.3 %copy.31 = bf16[8,8,8,896]{3,2,1,0:T(8,128)(2,1)S(1)} copy(bf16[8,8,8,896]{3,1,2,0:T(8,128)(2,1)} %bitcast.56) | data formatting | bytes 1835008
  2.0 1.1 %copy.20 = bf16[8,64,896]{2,1,0:T(8,128)(2,1)} copy(bf16[8,64,896]{2,0,1:T(8,128)(2,1)S(1)} %bitcast.53) | data formatting | bytes 1835008 | tf_op jit(solution)/shard_map/transpose | solution.py:110
  3.0 7.4 %all-to-all-start = ((bf16[8,64,896]{2,1,0:T(8,128)(2,1)}), bf16[8,64,896]{2,1,0:T(8,128)(2,1)S(1)}, u32[]{:S(2)}, u32[]{:S(2)}) async-start(bf16[8,64,896]{2,1,0:T(8,128)(2,1)} %copy.20), calls=%async_computation | async-start | bytes 1835008 | tf_op jit(solution)/shard_map/all_to_all | solution.py:111
  10.5 0.6 fusion.33
  12.4 9.2 %fusion.18 = bf16[896,512]{1,0:T(8,128)(2,1)S(1)} fusion(s32[]{:T(128)} %bitcast, s32[896]{0:T(1024)S(1)} %add_multiply_fusion), kind=kLoop, calls=%fused_computation.24 | loop fusion | flops 16056320 | bytes 921092 | tf_op jit(solution)/shard_map/convert_element_type | solution.py:36
  21.6 12.7 %all-to-all-done = bf16[8,64,896]{2,1,0:T(8,128)(2,1)S(1)} async-done(((bf16[8,64,896]{2,1,0:T(8,128)(2,1)}), bf16[8,64,896]{2,1,0:T(8,128)(2,1)S(1)}, u32[]{:S(2)}, u32[]{:S(2)}) %all-to-all-start) | async-done | bytes 917536 | tf_op jit(solution)/shard_map/all_to_all | solution.py:111
  34.3 0.3 fusion.24
  34.6 0.3 convolution_add_fusion.2
  34.9 0.3 convolution_add_fusion.1
  35.2 0.3 fusion.20
  35.6 0.1 collective-permute-start
  35.7 1.3 %collective-permute-done = f32[64,512]{1,0:T(8,128)S(1)} collective-permute-done((f32[64,512]{1,0:T(8,128)S(1)}, f32[64,512]{1,0:T(8,128)S(1)}, u32[]{:S(2)}, u32[]{:S(2)}) %collective-permute-start) | collective-permute-done | bytes 131104 | tf_op jit(solution)/shard_map/ppermute | solution.py:86
  37.1 1.6 %collective-permute-start.1 = (f32[32,512]{1,0:T(8,128)S(1)}, f32[32,512]{1,0:T(8,128)S(1)}, u32[]{:S(2)}, u32[]{:S(2)}) collective-permute-start(f32[32,512]{1,0:T(8,128)S(1)} %slice_select_fusion), channel_id=1, source_target_pairs={{0,16},{8,24},{16,0},{24,8},{1,17},{9,25},{17,1},{25,9},{2,18},{10... | collective-permute-start | bytes 196616 | tf_op jit(solution)/shard_map/ppermute | solution.py:86
  38.6 2.8 %collective-permute-done.1 = f32[32,512]{1,0:T(8,128)S(1)} collective-permute-done((f32[32,512]{1,0:T(8,128)S(1)}, f32[32,512]{1,0:T(8,128)S(1)}, u32[]{:S(2)}, u32[]{:S(2)}) %collective-permute-start.1) | collective-permute-done | bytes 65568 | tf_op jit(solution)/shard_map/ppermute | solution.py:86
  41.4 0.6 collective-permute-start.2
  42.1 3.4 %collective-permute-done.2 = f32[16,512]{1,0:T(8,128)S(1)} collective-permute-done((f32[16,512]{1,0:T(8,128)S(1)}, f32[16,512]{1,0:T(8,128)S(1)}, u32[]{:S(2)}, u32[]{:S(2)}) %collective-permute-start.2) | collective-permute-done | bytes 32800 | tf_op jit(solution)/shard_map/ppermute | solution.py:86
  45.5 3.7 %collective-permute-done.3 = f32[8,512]{1,0:T(8,128)S(1)} collective-permute-done((f32[8,512]{1,0:T(8,128)S(1)}, f32[8,512]{1,0:T(8,128)S(1)}, u32[]{:S(2)}, u32[]{:S(2)}) %collective-permute-start.3) | collective-permute-done | bytes 16416 | tf_op jit(solution)/shard_map/ppermute | solution.py:86
  49.3 0.1 collective-permute-start.4
  49.3 4.5 %collective-permute-done.4 = f32[4,512]{1,0:T(4,128)S(1)} collective-permute-done((f32[4,512]{1,0:T(4,128)S(1)}, f32[4,512]{1,0:T(4,128)S(1)}, u32[]{:S(2)}, u32[]{:S(2)}) %collective-permute-start.4) | collective-permute-done | bytes 8224 | tf_op jit(solution)/shard_map/ppermute | solution.py:86
  53.9 4.5 %collective-permute-done.5 = bf16[4,512]{1,0:T(4,128)(2,1)S(1)} collective-permute-done((bf16[4,512]{1,0:T(4,128)(2,1)S(1)}, bf16[4,512]{1,0:T(4,128)(2,1)S(1)}, u32[]{:S(2)}, u32[]{:S(2)}) %collective-permute-start.5) | collective-permute-done | bytes 4128 | tf_op jit(solution)/shard_map/ppermute | solution.py:89
  58.5 0.1 collective-permute-start.6
  58.5 3.6 %collective-permute-done.6 = bf16[8,512]{1,0:T(8,128)(2,1)S(1)} collective-permute-done((bf16[8,512]{1,0:T(8,128)(2,1)S(1)}, bf16[8,512]{1,0:T(8,128)(2,1)S(1)}, u32[]{:S(2)}, u32[]{:S(2)}) %collective-permute-start.6) | collective-permute-done | bytes 8224 | tf_op jit(solution)/shard_map/ppermute | solution.py:89
  62.2 0.6 collective-permute-start.7
  62.7 3.2 %collective-permute-done.7 = bf16[16,512]{1,0:T(8,128)(2,1)S(1)} collective-permute-done((bf16[16,512]{1,0:T(8,128)(2,1)S(1)}, bf16[16,512]{1,0:T(8,128)(2,1)S(1)}, u32[]{:S(2)}, u32[]{:S(2)}) %collective-permute-start.7) | collective-permute-done | bytes 16416 | tf_op jit(solution)/shard_map/ppermute | solution.py:89
  65.9 1.6 %collective-permute-start.8 = (bf16[32,512]{1,0:T(8,128)(2,1)S(1)}, bf16[32,512]{1,0:T(8,128)(2,1)S(1)}, u32[]{:S(2)}, u32[]{:S(2)}) collective-permute-start(bf16[32,512]{1,0:T(8,128)(2,1)S(1)} %maximum_select_fusion.2), channel_id=1, source_target_pairs={{0,16},{8,24},{16,0},{24,8},{1,17},{9,25},{17,1},{25,9},{2,18},{10... | collective-permute-start | bytes 98312 | tf_op jit(solution)/shard_map/ppermute | solution.py:89
  67.5 2.4 %collective-permute-done.8 = bf16[32,512]{1,0:T(8,128)(2,1)S(1)} collective-permute-done((bf16[32,512]{1,0:T(8,128)(2,1)S(1)}, bf16[32,512]{1,0:T(8,128)(2,1)S(1)}, u32[]{:S(2)}, u32[]{:S(2)}) %collective-permute-start.8) | collective-permute-done | bytes 32800 | tf_op jit(solution)/shard_map/ppermute | solution.py:89
  69.9 0.1 collective-permute-start.9
  70.0 1.2 %collective-permute-done.9 = bf16[64,512]{1,0:T(8,128)(2,1)S(1)} collective-permute-done((bf16[64,512]{1,0:T(8,128)(2,1)S(1)}, bf16[64,512]{1,0:T(8,128)(2,1)S(1)}, u32[]{:S(2)}, u32[]{:S(2)}) %collective-permute-start.9) | collective-permute-done | bytes 65568 | tf_op jit(solution)/shard_map/ppermute | solution.py:89
  71.2 1.2 %fusion.28 = f32[128,896]{1,0:T(8,128)} fusion(bf16[896,512]{1,0:T(8,128)(2,1)S(1)} %fusion.18, bf16[64,512]{1,0:T(8,128)(2,1)S(1)} %collective-permute-done.9, bf16[64,512]{1,0:T(8,128)(2,1)S(1)} %maximum_select_fusion.1, pred[]{:T(512)S(6)} %eq.16), kind=kOutput, calls=%fused_computation.45 | convolution fusion | flops 118030336 | bytes 1507329 | tf_op jit(solution)/shard_map/dot_general | solution.py:125
  72.5 3.6 %all-to-all-start.1 = ((f32[8,16,896]{2,1,0:T(8,128)}), f32[8,16,896]{2,1,0:T(8,128)S(1)}, u32[]{:S(2)}, u32[]{:S(2)}) async-start(f32[8,16,896]{2,1,0:T(8,128)} %bitcast.11), calls=%async_computation.1 | async-start | bytes 917504 | tf_op jit(solution)/shard_map/all_to_all | solution.py:130
  76.8 13.8 %all-to-all-done.1 = f32[8,16,896]{2,1,0:T(8,128)S(1)} async-done(((f32[8,16,896]{2,1,0:T(8,128)}), f32[8,16,896]{2,1,0:T(8,128)S(1)}, u32[]{:S(2)}, u32[]{:S(2)}) %all-to-all-start.1) | async-done | bytes 458784 | tf_op jit(solution)/shard_map/all_to_all | solution.py:130
  90.7 1.2 %multiply_divide_fusion = (f32[16,7168]{1,0:T(8,128)}, f32[16,7168]{1,0:T(8,128)}, f32[16,7168]{1,0:T(8,128)}) fusion(f32[]{:T(128)} %bitcast.14, f32[]{:T(128)} %bitcast.13, f32[16,7168]{1,0:T(8,128)S(1)} %bitcast.54, f32[16,7168]{1,0:T(8,128)S(1)} %copy-done, f32[16,7168]{1,0:T(8,128)S(1)} %copy-done.1), kind=kLoop, calls=%fused_computation.37 | loop fusion | flops 1261568 | bytes 2752520 | tf_op jit(solution)/shard_map/div | solution.py:45
  (24 shorter events, 0.3 us)
Async XLA Ops:
  3.0 7.4 %copy-start.2 = (s32[2]{0:T(128)S(1)}, s32[2]{0:T(128)}, u32[]{:S(2)}) copy-start(s32[2]{0:T(128)} %param.6) | copy-start | bytes 28
  3.0 31.3 %all-to-all-start = ((bf16[8,64,896]{2,1,0:T(8,128)(2,1)}), bf16[8,64,896]{2,1,0:T(8,128)(2,1)S(1)}, u32[]{:S(2)}, u32[]{:S(2)}) async-start(bf16[8,64,896]{2,1,0:T(8,128)(2,1)} %copy.20), calls=%async_computation | async-start | bytes 1835008 | tf_op jit(solution)/shard_map/all_to_all | solution.py:111
  35.6 1.4 %collective-permute-start = (f32[64,512]{1,0:T(8,128)S(1)}, f32[64,512]{1,0:T(8,128)S(1)}, u32[]{:S(2)}, u32[]{:S(2)}) collective-permute-start(f32[64,512]{1,0:T(8,128)S(1)} %select_bitcast_fusion), channel_id=1, source_target_pairs={{0,8},{8,0},{16,24},{24,16},{1,9},{9,1},{17,25},{25,17},{2,10},{10... | collective-permute-start | bytes 393224 | tf_op jit(solution)/shard_map/ppermute | solution.py:86
  37.1 4.3 %collective-permute-start.1 = (f32[32,512]{1,0:T(8,128)S(1)}, f32[32,512]{1,0:T(8,128)S(1)}, u32[]{:S(2)}, u32[]{:S(2)}) collective-permute-start(f32[32,512]{1,0:T(8,128)S(1)} %slice_select_fusion), channel_id=1, source_target_pairs={{0,16},{8,24},{16,0},{24,8},{1,17},{9,25},{17,1},{25,9},{2,18},{10... | collective-permute-start | bytes 196616 | tf_op jit(solution)/shard_map/ppermute | solution.py:86
  41.4 4.0 %collective-permute-start.2 = (f32[16,512]{1,0:T(8,128)S(1)}, f32[16,512]{1,0:T(8,128)S(1)}, u32[]{:S(2)}, u32[]{:S(2)}) collective-permute-start(f32[16,512]{1,0:T(8,128)S(1)} %slice_select_fusion.1), channel_id=1, source_target_pairs={{0,1},{1,0},{2,3},{3,2},{4,5},{5,4},{6,7},{7,6},{8,9},{9,8},{10,11... | collective-permute-start | bytes 98312 | tf_op jit(solution)/shard_map/ppermute | solution.py:86
  45.4 3.8 %collective-permute-start.3 = (f32[8,512]{1,0:T(8,128)S(1)}, f32[8,512]{1,0:T(8,128)S(1)}, u32[]{:S(2)}, u32[]{:S(2)}) collective-permute-start(f32[8,512]{1,0:T(8,128)S(1)} %slice_select_fusion.2), channel_id=1, source_target_pairs={{0,2},{2,0},{4,6},{6,4},{1,3},{3,1},{5,7},{7,5},{8,10},{10,8},{12,... | collective-permute-start | bytes 49160 | tf_op jit(solution)/shard_map/ppermute | solution.py:86
  49.3 4.6 %collective-permute-start.4 = (f32[4,512]{1,0:T(4,128)S(1)}, f32[4,512]{1,0:T(4,128)S(1)}, u32[]{:S(2)}, u32[]{:S(2)}) collective-permute-start(f32[4,512]{1,0:T(4,128)S(1)} %slice_select_fusion.3), channel_id=1, source_target_pairs={{0,4},{2,6},{4,0},{6,2},{1,5},{3,7},{5,1},{7,3},{8,12},{10,14},{12... | collective-permute-start | bytes 24584 | tf_op jit(solution)/shard_map/ppermute | solution.py:86
  53.9 4.6 %collective-permute-start.5 = (bf16[4,512]{1,0:T(4,128)(2,1)S(1)}, bf16[4,512]{1,0:T(4,128)(2,1)S(1)}, u32[]{:S(2)}, u32[]{:S(2)}) collective-permute-start(bf16[4,512]{1,0:T(4,128)(2,1)S(1)} %select_add_fusion.3), channel_id=1, source_target_pairs={{0,4},{2,6},{4,0},{6,2},{1,5},{3,7},{5,1},{7,3},{8,12},{10,14},{12... | collective-permute-start | bytes 12296 | tf_op jit(solution)/shard_map/ppermute | solution.py:89
  58.5 3.7 %collective-permute-start.6 = (bf16[8,512]{1,0:T(8,128)(2,1)S(1)}, bf16[8,512]{1,0:T(8,128)(2,1)S(1)}, u32[]{:S(2)}, u32[]{:S(2)}) collective-permute-start(bf16[8,512]{1,0:T(8,128)(2,1)S(1)} %maximum_select_fusion.4), channel_id=1, source_target_pairs={{0,2},{2,0},{4,6},{6,4},{1,3},{3,1},{5,7},{7,5},{8,10},{10,8},{12,... | collective-permute-start | bytes 24584 | tf_op jit(solution)/shard_map/ppermute | solution.py:89
  62.2 3.7 %collective-permute-start.7 = (bf16[16,512]{1,0:T(8,128)(2,1)S(1)}, bf16[16,512]{1,0:T(8,128)(2,1)S(1)}, u32[]{:S(2)}, u32[]{:S(2)}) collective-permute-start(bf16[16,512]{1,0:T(8,128)(2,1)S(1)} %maximum_select_fusion.3), channel_id=1, source_target_pairs={{0,1},{1,0},{2,3},{3,2},{4,5},{5,4},{6,7},{7,6},{8,9},{9,8},{10,11... | collective-permute-start | bytes 49160 | tf_op jit(solution)/shard_map/ppermute | solution.py:89
  65.9 4.0 %collective-permute-start.8 = (bf16[32,512]{1,0:T(8,128)(2,1)S(1)}, bf16[32,512]{1,0:T(8,128)(2,1)S(1)}, u32[]{:S(2)}, u32[]{:S(2)}) collective-permute-start(bf16[32,512]{1,0:T(8,128)(2,1)S(1)} %maximum_select_fusion.2), channel_id=1, source_target_pairs={{0,16},{8,24},{16,0},{24,8},{1,17},{9,25},{17,1},{25,9},{2,18},{10... | collective-permute-start | bytes 98312 | tf_op jit(solution)/shard_map/ppermute | solution.py:89
  69.9 1.3 %collective-permute-start.9 = (bf16[64,512]{1,0:T(8,128)(2,1)S(1)}, bf16[64,512]{1,0:T(8,128)(2,1)S(1)}, u32[]{:S(2)}, u32[]{:S(2)}) collective-permute-start(bf16[64,512]{1,0:T(8,128)(2,1)S(1)} %maximum_select_fusion.1), channel_id=1, source_target_pairs={{0,8},{8,0},{16,24},{24,16},{1,9},{9,1},{17,25},{25,17},{2,10},{10... | collective-permute-start | bytes 196616 | tf_op jit(solution)/shard_map/ppermute | solution.py:89
  72.5 18.2 %copy-start = (f32[16,7168]{1,0:T(8,128)S(1)}, f32[16,7168]{1,0:T(8,128)}, u32[]{:S(2)}) copy-start(f32[16,7168]{1,0:T(8,128)} %param.9) | copy-start | bytes 1376260
  72.5 18.2 %copy-start.1 = (f32[16,7168]{1,0:T(8,128)S(1)}, f32[16,7168]{1,0:T(8,128)}, u32[]{:S(2)}) copy-start(f32[16,7168]{1,0:T(8,128)} %param.8) | copy-start | bytes 1376260
  72.5 18.1 %all-to-all-start.1 = ((f32[8,16,896]{2,1,0:T(8,128)}), f32[8,16,896]{2,1,0:T(8,128)S(1)}, u32[]{:S(2)}, u32[]{:S(2)}) async-start(f32[8,16,896]{2,1,0:T(8,128)} %bitcast.11), calls=%async_computation.1 | async-start | bytes 917504 | tf_op jit(solution)/shard_map/all_to_all | solution.py:130

commit v3 on v1

--- a/solution.py
+++ b/solution.py
@@ -7,6 +7,7 @@
 
 RANK = 512
 GROUP = ("fsdp", "replica")
+MESH_GROUP = ("replica", "fsdp")
 
 
 def scramble(value):
@@ -68,6 +69,40 @@
     return adam(first_moment, second_moment, estimate, adam_step)
 
 
+def shifted(value_of, axis, size, place=lambda i: i):
+    got = [value_of(0)]
+    for k in range(1, size):
+        pairs = [(place(i), place((i + k) % size)) for i in range(size)]
+        got.append(lax.ppermute(value_of(k), axis, pairs))
+    return got
+
+
+def by_source(got, index, size):
+    order = (index - jnp.arange(size, dtype=jnp.int32)) % size
+    return jnp.take(jnp.stack(got), order, axis=0)
+
+
+def exchange_sum(value, axes):
+    plan = []
+    for axis in axes:
+        size = lax.axis_size(axis)
+        index = lax.axis_index(axis)
+        parts = value.reshape(size, value.shape[0] // size, *value.shape[1:])
+
+        def block(k, parts=parts, index=index, size=size):
+            return lax.dynamic_index_in_dim(parts, (index + k) % size, 0, keepdims=False)
+
+        got = shifted(block, axis, size)
+        value = got[0]
+        for term in got[1:]:
+            value = value + term
+        plan.append((axis, size, index))
+    for axis, size, index in reversed(plan):
+        got = shifted(lambda k, value=value: value, axis, size)
+        value = by_source(got, index, size).reshape(-1, *value.shape[1:])
+    return value
+
+
 def per_device(gradients, seeds, adam_step, first_moment, second_moment):
     gradient = gradients[0]
     rows, columns = gradient.shape
@@ -85,6 +120,7 @@
     pieces = gradient.reshape(rows, n_group, width).transpose(1, 0, 2)
     held = lax.all_to_all(pieces, GROUP, 0, 0, tiled=True)
     held = held.reshape(n_fsdp, n_rep, rows, width)
+    place = lambda i: (i % n_rep) * n_fsdp + i // n_rep
 
     partial_value = None
     for r in range(n_rep):
@@ -94,7 +130,7 @@
         )
         partial_value = term if partial_value is None else partial_value + term
     partial_value = partial_value.reshape(n_fsdp * rows, RANK) * (1.0 / n_rep)
-    sketch = lax.psum(partial_value, ("tensor",) + GROUP)
+    sketch = exchange_sum(partial_value, ("tensor",) + GROUP)
     sketch_rounded = sketch.astype(jnp.bfloat16)
 
     estimate = lax.dot_general(
@@ -102,8 +138,8 @@
     )
     out_rows = first_moment.shape[0]
     estimate = estimate.reshape(n_group, out_rows, width)
-    estimate = lax.all_to_all(estimate, GROUP, 0, 0, tiled=True)
-    estimate = estimate.transpose(1, 0, 2).reshape(out_rows, columns)
+    got = shifted(lambda k: estimate[(member + k) % n_group], MESH_GROUP, n_group, place)
+    estimate = by_source(got, member, n_group).transpose(1, 0, 2).reshape(out_rows, columns)
     return adam(first_moment, second_moment, estimate, adam_step)
 
 

time: 96.5 us -> 86.4 us (0.90)
  blocking collectives: 40.4 us -> 0 us
  starting transfers between devices: 11.8 us -> 27.1 us
  waiting for transfers between devices: 25.1 us -> 36.2 us
  local copies, waits for them, and re-layouts: 3.04 us -> 6.95 us
    psum x1 -> x0, blocking collectives: 40.4 us -> none  [per_device(): sketch = lax.psum(partial_value, ('tensor',) + GROUP)]
    ppermute x0 -> x21, waiting for transfers between devices: none -> 23.7 us  [shifted(): got.append(lax.ppermute(value_of(k), axis, pairs))]
    ppermute x0 -> x21, starting transfers between devices: none -> 19.6 us  [shifted(): got.append(lax.ppermute(value_of(k), axis, pairs))]
    all_to_all x1 -> x0, waiting for transfers between devices: 12.4 us -> none  [per_device(): estimate = lax.all_to_all(estimate, GROUP, 0, 0, tiled=True)]
    all_to_all x1 -> x0, starting transfers between devices: 4.35 us -> none  [per_device(): estimate = lax.all_to_all(estimate, GROUP, 0, 0, tiled=True)]
    gather x0 -> x6, local copies, waits for them, and re-layouts: none -> 2.28 us  [by_source(): return jnp.take(jnp.stack(got), order, axis=0)]
    unnamed x7 -> x13, local copies, waits for them, and re-layouts: 1.33 us -> 2.36 us
  transfers between devices with their start and end apart: 2 -> 22, of which waited for: 2 -> 17; matrix products, arithmetic and copies ran while one was open for 10% -> 12% of each run, Pallas kernels for 0% -> 0%
where the time goes in v3:
time: 86.4 us; the launch traced here: 86.1 us
  waiting for transfers between devices  36.2 us (42%)
  starting transfers between devices  27.1 us (31%)
  other arithmetic  11 us (13%)
  local copies, waits for them, and re-layouts  6.95 us (8%)
  between operations  3.14 us (4%)
  matrix products  1.7 us (2%)
    ppermute x21, waiting for transfers between devices, shifted(): got.append(lax.ppermute(value_of(k), axis, pairs))  23.7 us
    ppermute x21, starting transfers between devices, shifted(): got.append(lax.ppermute(value_of(k), axis, pairs))  19.6 us
    all_to_all x1, waiting for transfers between devices, per_device(): held = lax.all_to_all(pieces, GROUP, 0, 0, tiled=True)  12.6 us
    convert_element_type x1, other arithmetic, projection_block(): return (gauss * rank ** (-0.5)).astype(jnp.bfloat16)  9.2 us
    all_to_all x1, starting transfers between devices, per_device(): held = lax.all_to_all(pieces, GROUP, 0, 0, tiled=True)  7.44 us
    unnamed x13, local copies, waits for them, and re-layouts  2.36 us
    gather x6, local copies, waits for them, and re-layouts, by_source(): return jnp.take(jnp.stack(got), order, axis=0)  2.28 us
  transfers between devices with their start and end apart: 22, of which 17 were waited for; matrix products, arithmetic and copies ran while one was open for 12% of the time, Pallas kernels for 0%

profile of v3, /device:TPU:0, one launch (start us, length us, event | category | flops | bytes accessed | tf_op | source)
XLA Modules:
  0.0 86.1 jit_solution(4028208217268858261)
XLA Ops:
  0.6 1.3 %copy.30 = bf16[8,8,8,896]{3,2,1,0:T(8,128)(2,1)S(1)} copy(bf16[8,8,8,896]{3,1,2,0:T(8,128)(2,1)} %bitcast.134) | data formatting | bytes 1835008
  2.0 1.1 %copy.19 = bf16[8,64,896]{2,1,0:T(8,128)(2,1)} copy(bf16[8,64,896]{2,0,1:T(8,128)(2,1)S(1)} %bitcast.130) | data formatting | bytes 1835008 | tf_op jit(solution)/shard_map/transpose | solution.py:120
  3.0 7.4 %all-to-all-start = ((bf16[8,64,896]{2,1,0:T(8,128)(2,1)}), bf16[8,64,896]{2,1,0:T(8,128)(2,1)S(1)}, u32[]{:S(2)}, u32[]{:S(2)}) async-start(bf16[8,64,896]{2,1,0:T(8,128)(2,1)} %copy.19), calls=%async_computation | async-start | bytes 1835008 | tf_op jit(solution)/shard_map/all_to_all | solution.py:121
  10.5 0.6 fusion.48
  12.4 9.2 %fusion.18 = bf16[896,512]{1,0:T(8,128)(2,1)S(1)} fusion(s32[]{:T(128)} %bitcast, s32[896]{0:T(1024)S(1)} %add_multiply_fusion), kind=kLoop, calls=%fused_computation.28 | loop fusion | flops 16056320 | bytes 921092 | tf_op jit(solution)/shard_map/convert_element_type | solution.py:37
  21.7 12.6 %all-to-all-done = bf16[8,64,896]{2,1,0:T(8,128)(2,1)S(1)} async-done(((bf16[8,64,896]{2,1,0:T(8,128)(2,1)}), bf16[8,64,896]{2,1,0:T(8,128)(2,1)S(1)}, u32[]{:S(2)}, u32[]{:S(2)}) %all-to-all-start) | async-done | bytes 917536 | tf_op jit(solution)/shard_map/all_to_all | solution.py:121
  35.7 1.6 %collective-permute-start.1 = (f32[32,512]{1,0:T(8,128)S(1)}, f32[32,512]{1,0:T(8,128)S(1)}, u32[]{:S(2)}, u32[]{:S(2)}) collective-permute-start(f32[32,512]{1,0:T(8,128)S(1)} %get-tuple-element.16), channel_id=1, source_target_pairs={{0,16},{8,24},{16,0},{24,8},{1,17},{9,25},{17,1},{25,9},{2,18},{10... | collective-permute-start | bytes 196616 | tf_op jit(solution)/shard_map/ppermute | solution.py:76
  37.6 3.8 %collective-permute-done.1 = f32[32,512]{1,0:T(8,128)S(1)} collective-permute-done((f32[32,512]{1,0:T(8,128)S(1)}, f32[32,512]{1,0:T(8,128)S(1)}, u32[]{:S(2)}, u32[]{:S(2)}) %collective-permute-start.1) | collective-permute-done | bytes 65568 | tf_op jit(solution)/shard_map/ppermute | solution.py:76
  41.5 0.6 collective-permute-start.3
  42.2 3.3 %collective-permute-done.3 = f32[16,512]{1,0:T(8,128)S(1)} collective-permute-done((f32[16,512]{1,0:T(8,128)S(1)}, f32[16,512]{1,0:T(8,128)S(1)}, u32[]{:S(2)}, u32[]{:S(2)}) %collective-permute-start.3) | collective-permute-done | bytes 32800 | tf_op jit(solution)/shard_map/ppermute | solution.py:76
  45.7 1.9 %collective-permute-start.4 = (f32[4,512]{1,0:T(4,128)S(1)}, f32[4,512]{1,0:T(4,128)S(1)}, u32[]{:S(2)}, u32[]{:S(2)}) collective-permute-start(f32[4,512]{1,0:T(4,128)S(1)} %get-tuple-element.17), channel_id=1, source_target_pairs={{0,2},{2,4},{4,6},{6,0},{1,3},{3,5},{5,7},{7,1},{8,10},{10,12},{12... | collective-permute-start | bytes 24584 | tf_op jit(solution)/shard_map/ppermute | solution.py:76
  47.7 1.5 %collective-permute-done.6 = f32[4,512]{1,0:T(4,128)S(1)} collective-permute-done((f32[4,512]{1,0:T(4,128)S(1)}, f32[4,512]{1,0:T(4,128)S(1)}, u32[]{:S(2)}, u32[]{:S(2)}) %collective-permute-start.6) | collective-permute-done | bytes 8224 | tf_op jit(solution)/shard_map/ppermute | solution.py:76
  49.3 1.0 %collective-permute-done.5 = f32[4,512]{1,0:T(4,128)S(1)} collective-permute-done((f32[4,512]{1,0:T(4,128)S(1)}, f32[4,512]{1,0:T(4,128)S(1)}, u32[]{:S(2)}, u32[]{:S(2)}) %collective-permute-start.5) | collective-permute-done | bytes 8224 | tf_op jit(solution)/shard_map/ppermute | solution.py:76
  50.3 1.5 %collective-permute-done.4 = f32[4,512]{1,0:T(4,128)S(1)} collective-permute-done((f32[4,512]{1,0:T(4,128)S(1)}, f32[4,512]{1,0:T(4,128)S(1)}, u32[]{:S(2)}, u32[]{:S(2)}) %collective-permute-start.4) | collective-permute-done | bytes 8224 | tf_op jit(solution)/shard_map/ppermute | solution.py:76
  51.7 2.0 %collective-permute-start.9 = (bf16[4,512]{1,0:T(4,128)(2,1)S(1)}, bf16[4,512]{1,0:T(4,128)(2,1)S(1)}, u32[]{:S(2)}, u32[]{:S(2)}) collective-permute-start(bf16[4,512]{1,0:T(4,128)(2,1)S(1)} %fusion.33), channel_id=1, source_target_pairs={{0,6},{2,0},{4,2},{6,4},{1,7},{3,1},{5,3},{7,5},{8,14},{10,8},{12,... | collective-permute-start | bytes 12296 | tf_op jit(solution)/shard_map/ppermute | solution.py:76
  53.7 0.6 collective-permute-start.7
  55.6 2.6 %collective-permute-done.8 = bf16[4,512]{1,0:T(4,128)(2,1)S(1)} collective-permute-done((bf16[4,512]{1,0:T(4,128)(2,1)S(1)}, bf16[4,512]{1,0:T(4,128)(2,1)S(1)}, u32[]{:S(2)}, u32[]{:S(2)}) %collective-permute-start.8) | collective-permute-done | bytes 4128 | tf_op jit(solution)/shard_map/ppermute | solution.py:76
  58.2 0.9 %collective-permute-done.7 = bf16[4,512]{1,0:T(4,128)(2,1)S(1)} collective-permute-done((bf16[4,512]{1,0:T(4,128)(2,1)S(1)}, bf16[4,512]{1,0:T(4,128)(2,1)S(1)}, u32[]{:S(2)}, u32[]{:S(2)}) %collective-permute-start.7) | collective-permute-done | bytes 4128 | tf_op jit(solution)/shard_map/ppermute | solution.py:76
  59.2 0.6 gather_fusion
  60.5 3.1 %collective-permute-done.10 = bf16[16,512]{1,0:T(8,128)(2,1)S(1)} collective-permute-done((bf16[16,512]{1,0:T(8,128)(2,1)S(1)}, bf16[16,512]{1,0:T(8,128)(2,1)S(1)}, u32[]{:S(2)}, u32[]{:S(2)}) %collective-permute-start.10) | collective-permute-done | bytes 16416 | tf_op jit(solution)/shard_map/ppermute | solution.py:76
  64.2 0.9 %collective-permute-start.12 = (bf16[32,512]{1,0:T(8,128)(2,1)S(1)}, bf16[32,512]{1,0:T(8,128)(2,1)S(1)}, u32[]{:S(2)}, u32[]{:S(2)}) collective-permute-start(bf16[32,512]{1,0:T(8,128)(2,1)S(1)} %bitcast_select_fusion), channel_id=1, source_target_pairs={{0,16},{8,24},{16,0},{24,8},{1,17},{9,25},{17,1},{25,9},{2,18},{10... | collective-permute-start | bytes 98312 | tf_op jit(solution)/shard_map/ppermute | solution.py:76
  65.8 2.5 %collective-permute-done.12 = bf16[32,512]{1,0:T(8,128)(2,1)S(1)} collective-permute-done((bf16[32,512]{1,0:T(8,128)(2,1)S(1)}, bf16[32,512]{1,0:T(8,128)(2,1)S(1)}, u32[]{:S(2)}, u32[]{:S(2)}) %collective-permute-start.12) | collective-permute-done | bytes 32800 | tf_op jit(solution)/shard_map/ppermute | solution.py:76
  69.8 1.2 %collective-permute-start.15 = (f32[16,896]{1,0:T(8,128)S(1)}, f32[16,896]{1,0:T(8,128)S(1)}, u32[]{:S(2)}, u32[]{:S(2)}) collective-permute-start(f32[16,896]{1,0:T(8,128)S(1)} %get-tuple-element.11), channel_id=1, source_target_pairs={{0,4},{2,6},{4,1},{6,3},{1,5},{3,7},{5,0},{7,2},{8,12},{10,14},{12... | collective-permute-start | bytes 172040 | tf_op jit(solution)/shard_map/ppermute | solution.py:76
  71.0 3.0 %collective-permute-start.16 = (f32[16,896]{1,0:T(8,128)S(1)}, f32[16,896]{1,0:T(8,128)S(1)}, u32[]{:S(2)}, u32[]{:S(2)}) collective-permute-start(f32[16,896]{1,0:T(8,128)S(1)} %get-tuple-element.10), channel_id=1, source_target_pairs={{0,6},{2,1},{4,3},{6,5},{1,7},{3,0},{5,2},{7,4},{8,14},{10,9},{12,... | collective-permute-start | bytes 172040 | tf_op jit(solution)/shard_map/ppermute | solution.py:76
  74.0 1.3 %collective-permute-start.17 = (f32[16,896]{1,0:T(8,128)S(1)}, f32[16,896]{1,0:T(8,128)S(1)}, u32[]{:S(2)}, u32[]{:S(2)}) collective-permute-start(f32[16,896]{1,0:T(8,128)S(1)} %get-tuple-element.9), channel_id=1, source_target_pairs={{0,1},{2,3},{4,5},{6,7},{1,0},{3,2},{5,4},{7,6},{8,9},{10,11},{12,... | collective-permute-start | bytes 172040 | tf_op jit(solution)/shard_map/ppermute | solution.py:76
  75.3 0.7 collective-permute-start.18
  76.0 0.7 collective-permute-done.14
  76.7 1.3 %collective-permute-start.19 = (f32[16,896]{1,0:T(8,128)S(1)}, f32[16,896]{1,0:T(8,128)S(1)}, u32[]{:S(2)}, u32[]{:S(2)}) collective-permute-start(f32[16,896]{1,0:T(8,128)S(1)} %get-tuple-element.7), channel_id=1, source_target_pairs={{0,5},{2,7},{4,0},{6,2},{1,4},{3,6},{5,1},{7,3},{8,13},{10,15},{12... | collective-permute-start | bytes 172040 | tf_op jit(solution)/shard_map/ppermute | solution.py:76
  78.0 3.3 %collective-permute-start.20 = (f32[16,896]{1,0:T(8,128)S(1)}, f32[16,896]{1,0:T(8,128)S(1)}, u32[]{:S(2)}, u32[]{:S(2)}) collective-permute-start(f32[16,896]{1,0:T(8,128)S(1)} %get-tuple-element.6), channel_id=1, source_target_pairs={{0,7},{2,0},{4,2},{6,4},{1,6},{3,1},{5,3},{7,5},{8,15},{10,8},{12,... | collective-permute-start | bytes 172040 | tf_op jit(solution)/shard_map/ppermute | solution.py:76
  82.0 1.2 %collective-permute-done.20 = f32[16,896]{1,0:T(8,128)S(1)} collective-permute-done((f32[16,896]{1,0:T(8,128)S(1)}, f32[16,896]{1,0:T(8,128)S(1)}, u32[]{:S(2)}, u32[]{:S(2)}) %collective-permute-start.20) | collective-permute-done | bytes 57376 | tf_op jit(solution)/shard_map/ppermute | solution.py:76
  83.9 0.9 copy-done
  84.9 1.2 %multiply_divide_fusion = (f32[16,7168]{1,0:T(8,128)}, f32[16,7168]{1,0:T(8,128)}, f32[16,7168]{1,0:T(8,128)}) fusion(f32[]{:T(128)} %bitcast.53, f32[]{:T(128)} %bitcast.52, f32[16,7168]{1,0:T(8,128)S(1)} %bitcast.131, f32[16,7168]{1,0:T(8,128)S(1)} %copy-done, f32[16,7168]{1,0:T(8,128)S(1)} %copy-done.1), kind=kLoop, calls=%fused_computation.42 | loop fusion | flops 1261568 | bytes 2752520 | tf_op jit(solution)/shard_map/div | solution.py:46
  (76 shorter events, 7.5 us)
Async XLA Ops:
  3.0 7.4 %copy-start.2 = (s32[2]{0:T(128)S(1)}, s32[2]{0:T(128)}, u32[]{:S(2)}) copy-start(s32[2]{0:T(128)} %param.6) | copy-start | bytes 28
  3.0 31.3 %all-to-all-start = ((bf16[8,64,896]{2,1,0:T(8,128)(2,1)}), bf16[8,64,896]{2,1,0:T(8,128)(2,1)S(1)}, u32[]{:S(2)}, u32[]{:S(2)}) async-start(bf16[8,64,896]{2,1,0:T(8,128)(2,1)} %copy.19), calls=%async_computation | async-start | bytes 1835008 | tf_op jit(solution)/shard_map/all_to_all | solution.py:121
  35.6 2.0 %collective-permute-start.2 = (f32[32,512]{1,0:T(8,128)S(1)}, f32[32,512]{1,0:T(8,128)S(1)}, u32[]{:S(2)}, u32[]{:S(2)}) collective-permute-start(f32[32,512]{1,0:T(8,128)S(1)} %get-tuple-element.15), channel_id=1, source_target_pairs={{0,24},{8,0},{16,8},{24,16},{1,25},{9,1},{17,9},{25,17},{2,26},{10... | collective-permute-start | bytes 196616 | tf_op jit(solution)/shard_map/ppermute | solution.py:76
  35.7 5.7 %collective-permute-start.1 = (f32[32,512]{1,0:T(8,128)S(1)}, f32[32,512]{1,0:T(8,128)S(1)}, u32[]{:S(2)}, u32[]{:S(2)}) collective-permute-start(f32[32,512]{1,0:T(8,128)S(1)} %get-tuple-element.16), channel_id=1, source_target_pairs={{0,16},{8,24},{16,0},{24,8},{1,17},{9,25},{17,1},{25,9},{2,18},{10... | collective-permute-start | bytes 196616 | tf_op jit(solution)/shard_map/ppermute | solution.py:76
  37.2 4.3 %collective-permute-start = (f32[32,512]{1,0:T(8,128)S(1)}, f32[32,512]{1,0:T(8,128)S(1)}, u32[]{:S(2)}, u32[]{:S(2)}) collective-permute-start(f32[32,512]{1,0:T(8,128)S(1)} %get-tuple-element.14), channel_id=1, source_target_pairs={{0,8},{8,16},{16,24},{24,0},{1,9},{9,17},{17,25},{25,1},{2,10},{10... | collective-permute-start | bytes 196616 | tf_op jit(solution)/shard_map/ppermute | solution.py:76
  41.5 4.0 %collective-permute-start.3 = (f32[16,512]{1,0:T(8,128)S(1)}, f32[16,512]{1,0:T(8,128)S(1)}, u32[]{:S(2)}, u32[]{:S(2)}) collective-permute-start(f32[16,512]{1,0:T(8,128)S(1)} %dynamic-slice_bitcast_fusion.10), channel_id=1, source_target_pairs={{0,1},{1,0},{2,3},{3,2},{4,5},{5,4},{6,7},{7,6},{8,9},{9,8},{10,11... | collective-permute-start | bytes 98312 | tf_op jit(solution)/shard_map/ppermute | solution.py:76
  45.6 3.7 %collective-permute-start.6 = (f32[4,512]{1,0:T(4,128)S(1)}, f32[4,512]{1,0:T(4,128)S(1)}, u32[]{:S(2)}, u32[]{:S(2)}) collective-permute-start(f32[4,512]{1,0:T(4,128)S(1)} %get-tuple-element.18), channel_id=1, source_target_pairs={{0,6},{2,0},{4,2},{6,4},{1,7},{3,1},{5,3},{7,5},{8,14},{10,8},{12,... | collective-permute-start | bytes 24584 | tf_op jit(solution)/shard_map/ppermute | solution.py:76
  45.6 4.6 %collective-permute-start.5 = (f32[4,512]{1,0:T(4,128)S(1)}, f32[4,512]{1,0:T(4,128)S(1)}, u32[]{:S(2)}, u32[]{:S(2)}) collective-permute-start(f32[4,512]{1,0:T(4,128)S(1)} %get-tuple-element.19), channel_id=1, source_target_pairs={{0,4},{2,6},{4,0},{6,2},{1,5},{3,7},{5,1},{7,3},{8,12},{10,14},{12... | collective-permute-start | bytes 24584 | tf_op jit(solution)/shard_map/ppermute | solution.py:76
  45.7 6.0 %collective-permute-start.4 = (f32[4,512]{1,0:T(4,128)S(1)}, f32[4,512]{1,0:T(4,128)S(1)}, u32[]{:S(2)}, u32[]{:S(2)}) collective-permute-start(f32[4,512]{1,0:T(4,128)S(1)} %get-tuple-element.17), channel_id=1, source_target_pairs={{0,2},{2,4},{4,6},{6,0},{1,3},{3,5},{5,7},{7,1},{8,10},{10,12},{12... | collective-permute-start | bytes 24584 | tf_op jit(solution)/shard_map/ppermute | solution.py:76
  51.7 3.9 %collective-permute-start.9 = (bf16[4,512]{1,0:T(4,128)(2,1)S(1)}, bf16[4,512]{1,0:T(4,128)(2,1)S(1)}, u32[]{:S(2)}, u32[]{:S(2)}) collective-permute-start(bf16[4,512]{1,0:T(4,128)(2,1)S(1)} %fusion.33), channel_id=1, source_target_pairs={{0,6},{2,0},{4,2},{6,4},{1,7},{3,1},{5,3},{7,5},{8,14},{10,8},{12,... | collective-permute-start | bytes 12296 | tf_op jit(solution)/shard_map/ppermute | solution.py:76
  53.7 4.5 %collective-permute-start.8 = (bf16[4,512]{1,0:T(4,128)(2,1)S(1)}, bf16[4,512]{1,0:T(4,128)(2,1)S(1)}, u32[]{:S(2)}, u32[]{:S(2)}) collective-permute-start(bf16[4,512]{1,0:T(4,128)(2,1)S(1)} %fusion.33), channel_id=1, source_target_pairs={{0,4},{2,6},{4,0},{6,2},{1,5},{3,7},{5,1},{7,3},{8,12},{10,14},{12... | collective-permute-start | bytes 12296 | tf_op jit(solution)/shard_map/ppermute | solution.py:76
  53.7 5.4 %collective-permute-start.7 = (bf16[4,512]{1,0:T(4,128)(2,1)S(1)}, bf16[4,512]{1,0:T(4,128)(2,1)S(1)}, u32[]{:S(2)}, u32[]{:S(2)}) collective-permute-start(bf16[4,512]{1,0:T(4,128)(2,1)S(1)} %fusion.33), channel_id=1, source_target_pairs={{0,2},{2,4},{4,6},{6,0},{1,3},{3,5},{5,7},{7,1},{8,10},{10,12},{12... | collective-permute-start | bytes 12296 | tf_op jit(solution)/shard_map/ppermute | solution.py:76
  59.8 3.7 %collective-permute-start.10 = (bf16[16,512]{1,0:T(8,128)(2,1)S(1)}, bf16[16,512]{1,0:T(8,128)(2,1)S(1)}, u32[]{:S(2)}, u32[]{:S(2)}) collective-permute-start(bf16[16,512]{1,0:T(8,128)(2,1)S(1)} %broadcast_select_fusion), channel_id=1, source_target_pairs={{0,1},{1,0},{2,3},{3,2},{4,5},{5,4},{6,7},{7,6},{8,9},{9,8},{10,11... | collective-permute-start | bytes 49160 | tf_op jit(solution)/shard_map/ppermute | solution.py:76
  64.2 1.6 %collective-permute-start.13 = (bf16[32,512]{1,0:T(8,128)(2,1)S(1)}, bf16[32,512]{1,0:T(8,128)(2,1)S(1)}, u32[]{:S(2)}, u32[]{:S(2)}) collective-permute-start(bf16[32,512]{1,0:T(8,128)(2,1)S(1)} %bitcast_select_fusion), channel_id=1, source_target_pairs={{0,24},{8,0},{16,8},{24,16},{1,25},{9,1},{17,9},{25,17},{2,26},{10... | collective-permute-start | bytes 98312 | tf_op jit(solution)/shard_map/ppermute | solution.py:76
  64.2 4.0 %collective-permute-start.12 = (bf16[32,512]{1,0:T(8,128)(2,1)S(1)}, bf16[32,512]{1,0:T(8,128)(2,1)S(1)}, u32[]{:S(2)}, u32[]{:S(2)}) collective-permute-start(bf16[32,512]{1,0:T(8,128)(2,1)S(1)} %bitcast_select_fusion), channel_id=1, source_target_pairs={{0,16},{8,24},{16,0},{24,8},{1,17},{9,25},{17,1},{25,9},{2,18},{10... | collective-permute-start | bytes 98312 | tf_op jit(solution)/shard_map/ppermute | solution.py:76
  65.2 3.4 %collective-permute-start.11 = (bf16[32,512]{1,0:T(8,128)(2,1)S(1)}, bf16[32,512]{1,0:T(8,128)(2,1)S(1)}, u32[]{:S(2)}, u32[]{:S(2)}) collective-permute-start(bf16[32,512]{1,0:T(8,128)(2,1)S(1)} %bitcast_select_fusion), channel_id=1, source_target_pairs={{0,8},{8,16},{16,24},{24,0},{1,9},{9,17},{17,25},{25,1},{2,10},{10... | collective-permute-start | bytes 98312 | tf_op jit(solution)/shard_map/ppermute | solution.py:76
  69.7 7.0 %collective-permute-start.14 = (f32[16,896]{1,0:T(8,128)S(1)}, f32[16,896]{1,0:T(8,128)S(1)}, u32[]{:S(2)}, u32[]{:S(2)}) collective-permute-start(f32[16,896]{1,0:T(8,128)S(1)} %get-tuple-element.12), channel_id=1, source_target_pairs={{0,2},{2,4},{4,6},{6,1},{1,3},{3,5},{5,7},{7,0},{8,10},{10,12},{12... | collective-permute-start | bytes 172040 | tf_op jit(solution)/shard_map/ppermute | solution.py:76
  69.8 8.3 %collective-permute-start.15 = (f32[16,896]{1,0:T(8,128)S(1)}, f32[16,896]{1,0:T(8,128)S(1)}, u32[]{:S(2)}, u32[]{:S(2)}) collective-permute-start(f32[16,896]{1,0:T(8,128)S(1)} %get-tuple-element.11), channel_id=1, source_target_pairs={{0,4},{2,6},{4,1},{6,3},{1,5},{3,7},{5,0},{7,2},{8,12},{10,14},{12... | collective-permute-start | bytes 172040 | tf_op jit(solution)/shard_map/ppermute | solution.py:76
  71.0 10.3 %collective-permute-start.16 = (f32[16,896]{1,0:T(8,128)S(1)}, f32[16,896]{1,0:T(8,128)S(1)}, u32[]{:S(2)}, u32[]{:S(2)}) collective-permute-start(f32[16,896]{1,0:T(8,128)S(1)} %get-tuple-element.10), channel_id=1, source_target_pairs={{0,6},{2,1},{4,3},{6,5},{1,7},{3,0},{5,2},{7,4},{8,14},{10,9},{12,... | collective-permute-start | bytes 172040 | tf_op jit(solution)/shard_map/ppermute | solution.py:76
  74.0 7.3 %collective-permute-start.17 = (f32[16,896]{1,0:T(8,128)S(1)}, f32[16,896]{1,0:T(8,128)S(1)}, u32[]{:S(2)}, u32[]{:S(2)}) collective-permute-start(f32[16,896]{1,0:T(8,128)S(1)} %get-tuple-element.9), channel_id=1, source_target_pairs={{0,1},{2,3},{4,5},{6,7},{1,0},{3,2},{5,4},{7,6},{8,9},{10,11},{12,... | collective-permute-start | bytes 172040 | tf_op jit(solution)/shard_map/ppermute | solution.py:76
  75.3 6.1 %collective-permute-start.18 = (f32[16,896]{1,0:T(8,128)S(1)}, f32[16,896]{1,0:T(8,128)S(1)}, u32[]{:S(2)}, u32[]{:S(2)}) collective-permute-start(f32[16,896]{1,0:T(8,128)S(1)} %get-tuple-element.8), channel_id=1, source_target_pairs={{0,3},{2,5},{4,7},{6,0},{1,2},{3,4},{5,6},{7,1},{8,11},{10,13},{12... | collective-permute-start | bytes 172040 | tf_op jit(solution)/shard_map/ppermute | solution.py:76
  76.7 5.3 %collective-permute-start.19 = (f32[16,896]{1,0:T(8,128)S(1)}, f32[16,896]{1,0:T(8,128)S(1)}, u32[]{:S(2)}, u32[]{:S(2)}) collective-permute-start(f32[16,896]{1,0:T(8,128)S(1)} %get-tuple-element.7), channel_id=1, source_target_pairs={{0,5},{2,7},{4,0},{6,2},{1,4},{3,6},{5,1},{7,3},{8,13},{10,15},{12... | collective-permute-start | bytes 172040 | tf_op jit(solution)/shard_map/ppermute | solution.py:76
  78.0 5.2 %collective-permute-start.20 = (f32[16,896]{1,0:T(8,128)S(1)}, f32[16,896]{1,0:T(8,128)S(1)}, u32[]{:S(2)}, u32[]{:S(2)}) collective-permute-start(f32[16,896]{1,0:T(8,128)S(1)} %get-tuple-element.6), channel_id=1, source_target_pairs={{0,7},{2,0},{4,2},{6,4},{1,6},{3,1},{5,3},{7,5},{8,15},{10,8},{12,... | collective-permute-start | bytes 172040 | tf_op jit(solution)/shard_map/ppermute | solution.py:76
  83.8 1.0 %copy-start = (f32[16,7168]{1,0:T(8,128)S(1)}, f32[16,7168]{1,0:T(8,128)}, u32[]{:S(2)}) copy-start(f32[16,7168]{1,0:T(8,128)} %param.9) | copy-start | bytes 1376260
  83.8 1.1 %copy-start.1 = (f32[16,7168]{1,0:T(8,128)S(1)}, f32[16,7168]{1,0:T(8,128)}, u32[]{:S(2)}) copy-start(f32[16,7168]{1,0:T(8,128)} %param.8) | copy-start | bytes 1376260

commit v4 on v3

--- a/solution.py
+++ b/solution.py
@@ -106,40 +106,33 @@
 def per_device(gradients, seeds, adam_step, first_moment, second_moment):
     gradient = gradients[0]
     rows, columns = gradient.shape
-    n_fsdp = lax.axis_size("fsdp")
     n_rep = lax.axis_size("replica")
-    n_group = n_fsdp * n_rep
-    width = columns // n_group
-    if columns % (n_group * 128) != 0:
+    width = columns // n_rep
+    if columns % (n_rep * 128) != 0 or rows % n_rep != 0:
         return per_device_whole(gradients, seeds, adam_step, first_moment, second_moment)
-    member = lax.axis_index(GROUP)
+    member = lax.axis_index("replica")
     first = lax.axis_index("tensor") * jnp.int32(columns) + member * jnp.int32(width)
 
     projection = lax.optimization_barrier(projection_block(first, width, RANK, seeds))
 
-    pieces = gradient.reshape(rows, n_group, width).transpose(1, 0, 2)
-    held = lax.all_to_all(pieces, GROUP, 0, 0, tiled=True)
-    held = held.reshape(n_fsdp, n_rep, rows, width)
-    place = lambda i: (i % n_rep) * n_fsdp + i // n_rep
+    pieces = gradient.reshape(rows, n_rep, width).transpose(1, 0, 2)
+    held = lax.all_to_all(pieces, "replica", 0, 0, tiled=True)
 
     partial_value = None
     for r in range(n_rep):
-        term = lax.dot_general(
-            held[:, r], projection, (((2,), (0,)), ((), ())),
-            preferred_element_type=jnp.float32,
-        )
+        term = jnp.dot(held[r], projection, preferred_element_type=jnp.float32)
         partial_value = term if partial_value is None else partial_value + term
-    partial_value = partial_value.reshape(n_fsdp * rows, RANK) * (1.0 / n_rep)
-    sketch = exchange_sum(partial_value, ("tensor",) + GROUP)
+    partial_value = partial_value * (1.0 / n_rep)
+    sketch = exchange_sum(partial_value, ("tensor", "replica"))
     sketch_rounded = sketch.astype(jnp.bfloat16)
 
     estimate = lax.dot_general(
         sketch_rounded, projection, (((1,), (1,)), ((), ())), preferred_element_type=jnp.float32
     )
     out_rows = first_moment.shape[0]
-    estimate = estimate.reshape(n_group, out_rows, width)
-    got = shifted(lambda k: estimate[(member + k) % n_group], MESH_GROUP, n_group, place)
-    estimate = by_source(got, member, n_group).transpose(1, 0, 2).reshape(out_rows, columns)
+    estimate = estimate.reshape(n_rep, out_rows, width)
+    got = shifted(lambda k: estimate[(member + k) % n_rep], "replica", n_rep)
+    estimate = by_source(got, member, n_rep).transpose(1, 0, 2).reshape(out_rows, columns)
     return adam(first_moment, second_moment, estimate, adam_step)
 
 

time: 86.4 us -> 76.6 us (0.89)
  waiting for transfers between devices: 36.2 us -> 24.4 us
  other arithmetic: 11 us -> 19.8 us
  starting transfers between devices: 27.1 us -> 20.6 us
    all_to_all x1, waiting for transfers between devices: 12.6 us -> 2.72 us  [per_device(): held = lax.all_to_all(pieces, 'replica', 0, 0, tiled=True)]
    convert_element_type x1, other arithmetic: 9.2 us -> 18.2 us  [projection_block(): return (gauss * rank ** (-0.5)).astype(jnp.bfloat16)]
    ppermute x21 -> x15, starting transfers between devices: 19.6 us -> 14.2 us  [shifted(): got.append(lax.ppermute(value_of(k), axis, pairs))]
    another operation x1, local copies, waits for them, and re-layouts: 0.01 us -> 2.16 us  [per_device(): pieces = gradient.reshape(rows, n_rep, width).transpose(1, 0, 2)]
    ppermute x21 -> x15, waiting for transfers between devices: 23.7 us -> 21.7 us  [shifted(): got.append(lax.ppermute(value_of(k), axis, pairs))]
    unnamed x13 -> x6, local copies, waits for them, and re-layouts: 2.36 us -> 0.4 us
    all_to_all x1, starting transfers between devices: 7.44 us -> 6.35 us  [per_device(): held = lax.all_to_all(pieces, 'replica', 0, 0, tiled=True)]
    gather x6 -> x5, local copies, waits for them, and re-layouts: 2.28 us -> 1.74 us  [by_source(): return jnp.take(jnp.stack(got), order, axis=0)]
  transfers between devices with their start and end apart: 22 -> 16, of which waited for: 17 -> 11; matrix products, arithmetic and copies ran while one was open for 12% -> 25% of each run, Pallas kernels for 0% -> 0%
where the time goes in v4:
time: 76.6 us; the launch traced here: 76.4 us
  waiting for transfers between devices  24.4 us (32%)
  starting transfers between devices  20.6 us (27%)
  other arithmetic  19.8 us (26%)
  local copies, waits for them, and re-layouts  6.19 us (8%)
  between operations  2.94 us (4%)
  matrix products  2.41 us (3%)
    ppermute x15, waiting for transfers between devices, shifted(): got.append(lax.ppermute(value_of(k), axis, pairs))  21.7 us
    convert_element_type x1, other arithmetic, projection_block(): return (gauss * rank ** (-0.5)).astype(jnp.bfloat16)  18.2 us
    ppermute x15, starting transfers between devices, shifted(): got.append(lax.ppermute(value_of(k), axis, pairs))  14.2 us
    all_to_all x1, starting transfers between devices, per_device(): held = lax.all_to_all(pieces, 'replica', 0, 0, tiled=True)  6.35 us
    all_to_all x1, waiting for transfers between devices, per_device(): held = lax.all_to_all(pieces, 'replica', 0, 0, tiled=True)  2.72 us
    another operation x1, local copies, waits for them, and re-layouts, per_device(): pieces = gradient.reshape(rows, n_rep, width).transpose(1, 0, 2)  2.16 us
    dot_general x4, matrix products, per_device(): term = jnp.dot(held[r], projection, preferred_element_type=jnp.float32)  1.74 us
    gather x5, local copies, waits for them, and re-layouts, by_source(): return jnp.take(jnp.stack(got), order, axis=0)  1.74 us
  transfers between devices with their start and end apart: 16, of which 11 were waited for; matrix products, arithmetic and copies ran while one was open for 25% of the time, Pallas kernels for 0%

profile of v4, /device:TPU:0, one launch (start us, length us, event | category | flops | bytes accessed | tf_op | source)
XLA Modules:
  0.0 76.4 jit_solution(9579002419927170056)
XLA Ops:
  0.6 2.2 %reshape_squeeze.3 = bf16[64,4,1792]{2,1,0:T(4,128)(2,1)S(1)} reshape(bf16[1,64,7168]{2,1,0:T(8,128)(2,1)} %param.5) | data formatting | bytes 1835008 | tf_op jit(solution)/shard_map/reshape;squeeze | solution.py:118
  2.8 1.0 %copy.10 = bf16[4,64,1792]{2,1,0:T(8,128)(2,1)} copy(bf16[4,64,1792]{2,0,1:T(4,128)(2,1)S(1)} %bitcast.74) | data formatting | bytes 1835008 | tf_op jit(solution)/shard_map/transpose | solution.py:118
  3.8 6.3 %all-to-all-start = ((bf16[4,64,1792]{2,1,0:T(8,128)(2,1)}), bf16[4,64,1792]{2,1,0:T(8,128)(2,1)S(1)}, u32[]{:S(2)}, u32[]{:S(2)}) async-start(bf16[4,64,1792]{2,1,0:T(8,128)(2,1)} %copy.10), calls=%async_computation | async-start | bytes 1835008 | tf_op jit(solution)/shard_map/all_to_all | solution.py:119
  10.2 0.6 fusion.38
  12.1 18.2 %fusion.18 = bf16[1792,512]{1,0:T(8,128)(2,1)S(1)} fusion(s32[]{:T(128)} %bitcast, s32[1792]{0:T(1024)S(1)} %add_multiply_fusion), kind=kLoop, calls=%fused_computation.27 | loop fusion | flops 32112640 | bytes 1842180 | tf_op jit(solution)/shard_map/convert_element_type | solution.py:37
  30.4 2.7 %all-to-all-done = bf16[4,64,1792]{2,1,0:T(8,128)(2,1)S(1)} async-done(((bf16[4,64,1792]{2,1,0:T(8,128)(2,1)}), bf16[4,64,1792]{2,1,0:T(8,128)(2,1)S(1)}, u32[]{:S(2)}, u32[]{:S(2)}) %all-to-all-start) | async-done | bytes 917536 | tf_op jit(solution)/shard_map/all_to_all | solution.py:119
  33.5 0.4 convolution_add_fusion.2
  34.0 0.4 convolution_add_fusion.1
  34.4 0.4 fusion.21
  35.0 1.7 %collective-permute-start.2 = (f32[16,512]{1,0:T(8,128)S(1)}, f32[16,512]{1,0:T(8,128)S(1)}, u32[]{:S(2)}, u32[]{:S(2)}) collective-permute-start(f32[16,512]{1,0:T(8,128)S(1)} %get-tuple-element.11), channel_id=1, source_target_pairs={{0,24},{8,0},{16,8},{24,16},{1,25},{9,1},{17,9},{25,17},{2,26},{10... | collective-permute-start | bytes 98312 | tf_op jit(solution)/shard_map/ppermute | solution.py:76
  36.7 1.5 %collective-permute-start.1 = (f32[16,512]{1,0:T(8,128)S(1)}, f32[16,512]{1,0:T(8,128)S(1)}, u32[]{:S(2)}, u32[]{:S(2)}) collective-permute-start(f32[16,512]{1,0:T(8,128)S(1)} %get-tuple-element.12), channel_id=1, source_target_pairs={{0,16},{8,24},{16,0},{24,8},{1,17},{9,25},{17,1},{25,9},{2,18},{10... | collective-permute-start | bytes 98312 | tf_op jit(solution)/shard_map/ppermute | solution.py:76
  38.3 2.3 %collective-permute-done.1 = f32[16,512]{1,0:T(8,128)S(1)} collective-permute-done((f32[16,512]{1,0:T(8,128)S(1)}, f32[16,512]{1,0:T(8,128)S(1)}, u32[]{:S(2)}, u32[]{:S(2)}) %collective-permute-start.1) | collective-permute-done | bytes 32800 | tf_op jit(solution)/shard_map/ppermute | solution.py:76
  40.7 3.8 %collective-permute-start.5 = (f32[4,512]{1,0:T(4,128)S(1)}, f32[4,512]{1,0:T(4,128)S(1)}, u32[]{:S(2)}, u32[]{:S(2)}) collective-permute-start(f32[4,512]{1,0:T(4,128)S(1)} %get-tuple-element.14), channel_id=1, source_target_pairs={{0,6},{2,0},{4,2},{6,4},{1,7},{3,1},{5,3},{7,5},{8,14},{10,8},{12,... | collective-permute-start | bytes 24584 | tf_op jit(solution)/shard_map/ppermute | solution.py:76
  44.6 1.6 %collective-permute-done.3 = f32[4,512]{1,0:T(4,128)S(1)} collective-permute-done((f32[4,512]{1,0:T(4,128)S(1)}, f32[4,512]{1,0:T(4,128)S(1)}, u32[]{:S(2)}, u32[]{:S(2)}) %collective-permute-start.3) | collective-permute-done | bytes 8224 | tf_op jit(solution)/shard_map/ppermute | solution.py:76
  46.2 2.9 %collective-permute-done.4 = f32[4,512]{1,0:T(4,128)S(1)} collective-permute-done((f32[4,512]{1,0:T(4,128)S(1)}, f32[4,512]{1,0:T(4,128)S(1)}, u32[]{:S(2)}, u32[]{:S(2)}) %collective-permute-start.4) | collective-permute-done | bytes 8224 | tf_op jit(solution)/shard_map/ppermute | solution.py:76
  49.1 1.0 %collective-permute-start.8 = (bf16[4,512]{1,0:T(4,128)(2,1)S(1)}, bf16[4,512]{1,0:T(4,128)(2,1)S(1)}, u32[]{:S(2)}, u32[]{:S(2)}) collective-permute-start(bf16[4,512]{1,0:T(4,128)(2,1)S(1)} %fusion.29), channel_id=1, source_target_pairs={{0,6},{2,0},{4,2},{6,4},{1,7},{3,1},{5,3},{7,5},{8,14},{10,8},{12,... | collective-permute-start | bytes 12296 | tf_op jit(solution)/shard_map/ppermute | solution.py:76
  50.1 1.2 %collective-permute-start.6 = (bf16[4,512]{1,0:T(4,128)(2,1)S(1)}, bf16[4,512]{1,0:T(4,128)(2,1)S(1)}, u32[]{:S(2)}, u32[]{:S(2)}) collective-permute-start(bf16[4,512]{1,0:T(4,128)(2,1)S(1)} %fusion.29), channel_id=1, source_target_pairs={{0,2},{2,4},{4,6},{6,0},{1,3},{3,5},{5,7},{7,1},{8,10},{10,12},{12... | collective-permute-start | bytes 12296 | tf_op jit(solution)/shard_map/ppermute | solution.py:76
  51.4 1.3 %collective-permute-done.8 = bf16[4,512]{1,0:T(4,128)(2,1)S(1)} collective-permute-done((bf16[4,512]{1,0:T(4,128)(2,1)S(1)}, bf16[4,512]{1,0:T(4,128)(2,1)S(1)}, u32[]{:S(2)}, u32[]{:S(2)}) %collective-permute-start.8) | collective-permute-done | bytes 4128 | tf_op jit(solution)/shard_map/ppermute | solution.py:76
  52.8 1.8 %collective-permute-done.7 = bf16[4,512]{1,0:T(4,128)(2,1)S(1)} collective-permute-done((bf16[4,512]{1,0:T(4,128)(2,1)S(1)}, bf16[4,512]{1,0:T(4,128)(2,1)S(1)}, u32[]{:S(2)}, u32[]{:S(2)}) %collective-permute-start.7) | collective-permute-done | bytes 4128 | tf_op jit(solution)/shard_map/ppermute | solution.py:76
  54.6 0.9 %collective-permute-done.6 = bf16[4,512]{1,0:T(4,128)(2,1)S(1)} collective-permute-done((bf16[4,512]{1,0:T(4,128)(2,1)S(1)}, bf16[4,512]{1,0:T(4,128)(2,1)S(1)}, u32[]{:S(2)}, u32[]{:S(2)}) %collective-permute-start.6) | collective-permute-done | bytes 4128 | tf_op jit(solution)/shard_map/ppermute | solution.py:76
  55.5 0.6 gather_fusion
  56.2 1.6 %collective-permute-start.10 = (bf16[16,512]{1,0:T(8,128)(2,1)S(1)}, bf16[16,512]{1,0:T(8,128)(2,1)S(1)}, u32[]{:S(2)}, u32[]{:S(2)}) collective-permute-start(bf16[16,512]{1,0:T(8,128)(2,1)S(1)} %broadcast_select_fusion), channel_id=1, source_target_pairs={{0,16},{8,24},{16,0},{24,8},{1,17},{9,25},{17,1},{25,9},{2,18},{10... | collective-permute-start | bytes 49160 | tf_op jit(solution)/shard_map/ppermute | solution.py:76
  58.0 2.0 %collective-permute-done.10 = bf16[16,512]{1,0:T(8,128)(2,1)S(1)} collective-permute-done((bf16[16,512]{1,0:T(8,128)(2,1)S(1)}, bf16[16,512]{1,0:T(8,128)(2,1)S(1)}, u32[]{:S(2)}, u32[]{:S(2)}) %collective-permute-start.10) | collective-permute-done | bytes 16416 | tf_op jit(solution)/shard_map/ppermute | solution.py:76
  60.0 0.9 %collective-permute-done.9 = bf16[16,512]{1,0:T(8,128)(2,1)S(1)} collective-permute-done((bf16[16,512]{1,0:T(8,128)(2,1)S(1)}, bf16[16,512]{1,0:T(8,128)(2,1)S(1)}, u32[]{:S(2)}, u32[]{:S(2)}) %collective-permute-start.9) | collective-permute-done | bytes 16416 | tf_op jit(solution)/shard_map/ppermute | solution.py:76
  60.9 0.6 gather_fusion.1
  61.5 0.7 fusion.19
  62.2 1.7 %collective-permute-start.14 = (f32[16,1792]{1,0:T(8,128)S(1)}, f32[16,1792]{1,0:T(8,128)S(1)}, u32[]{:S(2)}, u32[]{:S(2)}) collective-permute-start(f32[16,1792]{1,0:T(8,128)S(1)} %get-tuple-element.7), channel_id=1, source_target_pairs={{0,6},{2,0},{4,2},{6,4},{1,7},{3,1},{5,3},{7,5},{8,14},{10,8},{12,... | collective-permute-start | bytes 344072 | tf_op jit(solution)/shard_map/ppermute | solution.py:76
  63.9 1.5 %collective-permute-start.12 = (f32[16,1792]{1,0:T(8,128)S(1)}, f32[16,1792]{1,0:T(8,128)S(1)}, u32[]{:S(2)}, u32[]{:S(2)}) collective-permute-start(f32[16,1792]{1,0:T(8,128)S(1)} %get-tuple-element.9), channel_id=1, source_target_pairs={{0,2},{2,4},{4,6},{6,0},{1,3},{3,5},{5,7},{7,1},{8,10},{10,12},{12... | collective-permute-start | bytes 344072 | tf_op jit(solution)/shard_map/ppermute | solution.py:76
  66.1 1.8 %collective-permute-done.14 = f32[16,1792]{1,0:T(8,128)S(1)} collective-permute-done((f32[16,1792]{1,0:T(8,128)S(1)}, f32[16,1792]{1,0:T(8,128)S(1)}, u32[]{:S(2)}, u32[]{:S(2)}) %collective-permute-start.14) | collective-permute-done | bytes 114720 | tf_op jit(solution)/shard_map/ppermute | solution.py:76
  67.9 6.1 %collective-permute-done.13 = f32[16,1792]{1,0:T(8,128)S(1)} collective-permute-done((f32[16,1792]{1,0:T(8,128)S(1)}, f32[16,1792]{1,0:T(8,128)S(1)}, u32[]{:S(2)}, u32[]{:S(2)}) %collective-permute-start.13) | collective-permute-done | bytes 114720 | tf_op jit(solution)/shard_map/ppermute | solution.py:76
  74.0 0.6 gather_fusion.2
  75.2 1.2 %multiply_divide_fusion = (f32[16,7168]{1,0:T(8,128)}, f32[16,7168]{1,0:T(8,128)}, f32[16,7168]{1,0:T(8,128)}) fusion(f32[]{:T(128)} %bitcast.35, f32[]{:T(128)} %bitcast.34, f32[16,7168]{1,0:T(8,128)S(1)} %bitcast.75, f32[16,7168]{1,0:T(8,128)S(1)} %copy-done, f32[16,7168]{1,0:T(8,128)S(1)} %copy-done.1), kind=kLoop, calls=%fused_computation.37 | loop fusion | flops 1261568 | bytes 2752520 | tf_op jit(solution)/shard_map/div | solution.py:46
  (42 shorter events, 1.8 us)
Async XLA Ops:
  2.8 7.4 %copy-start.2 = (s32[2]{0:T(128)S(1)}, s32[2]{0:T(128)}, u32[]{:S(2)}) copy-start(s32[2]{0:T(128)} %param.6) | copy-start | bytes 28
  3.8 29.3 %all-to-all-start = ((bf16[4,64,1792]{2,1,0:T(8,128)(2,1)}), bf16[4,64,1792]{2,1,0:T(8,128)(2,1)S(1)}, u32[]{:S(2)}, u32[]{:S(2)}) async-start(bf16[4,64,1792]{2,1,0:T(8,128)(2,1)} %copy.10), calls=%async_computation | async-start | bytes 1835008 | tf_op jit(solution)/shard_map/all_to_all | solution.py:119
  34.9 3.4 %collective-permute-start = (f32[16,512]{1,0:T(8,128)S(1)}, f32[16,512]{1,0:T(8,128)S(1)}, u32[]{:S(2)}, u32[]{:S(2)}) collective-permute-start(f32[16,512]{1,0:T(8,128)S(1)} %get-tuple-element.10), channel_id=1, source_target_pairs={{0,8},{8,16},{16,24},{24,0},{1,9},{9,17},{17,25},{25,1},{2,10},{10... | collective-permute-start | bytes 98312 | tf_op jit(solution)/shard_map/ppermute | solution.py:76
  35.0 3.3 %collective-permute-start.2 = (f32[16,512]{1,0:T(8,128)S(1)}, f32[16,512]{1,0:T(8,128)S(1)}, u32[]{:S(2)}, u32[]{:S(2)}) collective-permute-start(f32[16,512]{1,0:T(8,128)S(1)} %get-tuple-element.11), channel_id=1, source_target_pairs={{0,24},{8,0},{16,8},{24,16},{1,25},{9,1},{17,9},{25,17},{2,26},{10... | collective-permute-start | bytes 98312 | tf_op jit(solution)/shard_map/ppermute | solution.py:76
  36.7 3.9 %collective-permute-start.1 = (f32[16,512]{1,0:T(8,128)S(1)}, f32[16,512]{1,0:T(8,128)S(1)}, u32[]{:S(2)}, u32[]{:S(2)}) collective-permute-start(f32[16,512]{1,0:T(8,128)S(1)} %get-tuple-element.12), channel_id=1, source_target_pairs={{0,16},{8,24},{16,0},{24,8},{1,17},{9,25},{17,1},{25,9},{2,18},{10... | collective-permute-start | bytes 98312 | tf_op jit(solution)/shard_map/ppermute | solution.py:76
  40.7 5.5 %collective-permute-start.3 = (f32[4,512]{1,0:T(4,128)S(1)}, f32[4,512]{1,0:T(4,128)S(1)}, u32[]{:S(2)}, u32[]{:S(2)}) collective-permute-start(f32[4,512]{1,0:T(4,128)S(1)} %get-tuple-element.13), channel_id=1, source_target_pairs={{0,2},{2,4},{4,6},{6,0},{1,3},{3,5},{5,7},{7,1},{8,10},{10,12},{12... | collective-permute-start | bytes 24584 | tf_op jit(solution)/shard_map/ppermute | solution.py:76
  40.7 5.4 %collective-permute-start.5 = (f32[4,512]{1,0:T(4,128)S(1)}, f32[4,512]{1,0:T(4,128)S(1)}, u32[]{:S(2)}, u32[]{:S(2)}) collective-permute-start(f32[4,512]{1,0:T(4,128)S(1)} %get-tuple-element.14), channel_id=1, source_target_pairs={{0,6},{2,0},{4,2},{6,4},{1,7},{3,1},{5,3},{7,5},{8,14},{10,8},{12,... | collective-permute-start | bytes 24584 | tf_op jit(solution)/shard_map/ppermute | solution.py:76
  44.5 4.5 %collective-permute-start.4 = (f32[4,512]{1,0:T(4,128)S(1)}, f32[4,512]{1,0:T(4,128)S(1)}, u32[]{:S(2)}, u32[]{:S(2)}) collective-permute-start(f32[4,512]{1,0:T(4,128)S(1)} %get-tuple-element.15), channel_id=1, source_target_pairs={{0,4},{2,6},{4,0},{6,2},{1,5},{3,7},{5,1},{7,3},{8,12},{10,14},{12... | collective-permute-start | bytes 24584 | tf_op jit(solution)/shard_map/ppermute | solution.py:76
  49.1 3.7 %collective-permute-start.8 = (bf16[4,512]{1,0:T(4,128)(2,1)S(1)}, bf16[4,512]{1,0:T(4,128)(2,1)S(1)}, u32[]{:S(2)}, u32[]{:S(2)}) collective-permute-start(bf16[4,512]{1,0:T(4,128)(2,1)S(1)} %fusion.29), channel_id=1, source_target_pairs={{0,6},{2,0},{4,2},{6,4},{1,7},{3,1},{5,3},{7,5},{8,14},{10,8},{12,... | collective-permute-start | bytes 12296 | tf_op jit(solution)/shard_map/ppermute | solution.py:76
  50.1 4.5 %collective-permute-start.7 = (bf16[4,512]{1,0:T(4,128)(2,1)S(1)}, bf16[4,512]{1,0:T(4,128)(2,1)S(1)}, u32[]{:S(2)}, u32[]{:S(2)}) collective-permute-start(bf16[4,512]{1,0:T(4,128)(2,1)S(1)} %fusion.29), channel_id=1, source_target_pairs={{0,4},{2,6},{4,0},{6,2},{1,5},{3,7},{5,1},{7,3},{8,12},{10,14},{12... | collective-permute-start | bytes 12296 | tf_op jit(solution)/shard_map/ppermute | solution.py:76
  50.1 5.4 %collective-permute-start.6 = (bf16[4,512]{1,0:T(4,128)(2,1)S(1)}, bf16[4,512]{1,0:T(4,128)(2,1)S(1)}, u32[]{:S(2)}, u32[]{:S(2)}) collective-permute-start(bf16[4,512]{1,0:T(4,128)(2,1)S(1)} %fusion.29), channel_id=1, source_target_pairs={{0,2},{2,4},{4,6},{6,0},{1,3},{3,5},{5,7},{7,1},{8,10},{10,12},{12... | collective-permute-start | bytes 12296 | tf_op jit(solution)/shard_map/ppermute | solution.py:76
  56.2 1.8 %collective-permute-start.11 = (bf16[16,512]{1,0:T(8,128)(2,1)S(1)}, bf16[16,512]{1,0:T(8,128)(2,1)S(1)}, u32[]{:S(2)}, u32[]{:S(2)}) collective-permute-start(bf16[16,512]{1,0:T(8,128)(2,1)S(1)} %broadcast_select_fusion), channel_id=1, source_target_pairs={{0,24},{8,0},{16,8},{24,16},{1,25},{9,1},{17,9},{25,17},{2,26},{10... | collective-permute-start | bytes 49160 | tf_op jit(solution)/shard_map/ppermute | solution.py:76
  56.2 3.8 %collective-permute-start.10 = (bf16[16,512]{1,0:T(8,128)(2,1)S(1)}, bf16[16,512]{1,0:T(8,128)(2,1)S(1)}, u32[]{:S(2)}, u32[]{:S(2)}) collective-permute-start(bf16[16,512]{1,0:T(8,128)(2,1)S(1)} %broadcast_select_fusion), channel_id=1, source_target_pairs={{0,16},{8,24},{16,0},{24,8},{1,17},{9,25},{17,1},{25,9},{2,18},{10... | collective-permute-start | bytes 49160 | tf_op jit(solution)/shard_map/ppermute | solution.py:76
  57.7 3.2 %collective-permute-start.9 = (bf16[16,512]{1,0:T(8,128)(2,1)S(1)}, bf16[16,512]{1,0:T(8,128)(2,1)S(1)}, u32[]{:S(2)}, u32[]{:S(2)}) collective-permute-start(bf16[16,512]{1,0:T(8,128)(2,1)S(1)} %broadcast_select_fusion), channel_id=1, source_target_pairs={{0,8},{8,16},{16,24},{24,0},{1,9},{9,17},{17,25},{25,1},{2,10},{10... | collective-permute-start | bytes 49160 | tf_op jit(solution)/shard_map/ppermute | solution.py:76
  62.2 5.7 %collective-permute-start.14 = (f32[16,1792]{1,0:T(8,128)S(1)}, f32[16,1792]{1,0:T(8,128)S(1)}, u32[]{:S(2)}, u32[]{:S(2)}) collective-permute-start(f32[16,1792]{1,0:T(8,128)S(1)} %get-tuple-element.7), channel_id=1, source_target_pairs={{0,6},{2,0},{4,2},{6,4},{1,7},{3,1},{5,3},{7,5},{8,14},{10,8},{12,... | collective-permute-start | bytes 344072 | tf_op jit(solution)/shard_map/ppermute | solution.py:76
  63.9 10.1 %collective-permute-start.13 = (f32[16,1792]{1,0:T(8,128)S(1)}, f32[16,1792]{1,0:T(8,128)S(1)}, u32[]{:S(2)}, u32[]{:S(2)}) collective-permute-start(f32[16,1792]{1,0:T(8,128)S(1)} %get-tuple-element.8), channel_id=1, source_target_pairs={{0,4},{2,6},{4,0},{6,2},{1,5},{3,7},{5,1},{7,3},{8,12},{10,14},{12... | collective-permute-start | bytes 344072 | tf_op jit(solution)/shard_map/ppermute | solution.py:76
  63.9 10.1 %collective-permute-start.12 = (f32[16,1792]{1,0:T(8,128)S(1)}, f32[16,1792]{1,0:T(8,128)S(1)}, u32[]{:S(2)}, u32[]{:S(2)}) collective-permute-start(f32[16,1792]{1,0:T(8,128)S(1)} %get-tuple-element.9), channel_id=1, source_target_pairs={{0,2},{2,4},{4,6},{6,0},{1,3},{3,5},{5,7},{7,1},{8,10},{10,12},{12... | collective-permute-start | bytes 344072 | tf_op jit(solution)/shard_map/ppermute | solution.py:76
  74.0 1.0 %copy-start = (f32[16,7168]{1,0:T(8,128)S(1)}, f32[16,7168]{1,0:T(8,128)}, u32[]{:S(2)}) copy-start(f32[16,7168]{1,0:T(8,128)} %param.9) | copy-start | bytes 1376260
  74.0 1.2 %copy-start.1 = (f32[16,7168]{1,0:T(8,128)S(1)}, f32[16,7168]{1,0:T(8,128)}, u32[]{:S(2)}) copy-start(f32[16,7168]{1,0:T(8,128)} %param.8) | copy-start | bytes 1376260

commit v5 on v4

--- a/solution.py
+++ b/solution.py
@@ -130,9 +130,10 @@
         sketch_rounded, projection, (((1,), (1,)), ((), ())), preferred_element_type=jnp.float32
     )
     out_rows = first_moment.shape[0]
-    estimate = estimate.reshape(n_rep, out_rows, width)
+    estimate = estimate.reshape(n_rep, out_rows, width).astype(jnp.bfloat16)
     got = shifted(lambda k: estimate[(member + k) % n_rep], "replica", n_rep)
     estimate = by_source(got, member, n_rep).transpose(1, 0, 2).reshape(out_rows, columns)
+    estimate = estimate.astype(jnp.float32)
     return adam(first_moment, second_moment, estimate, adam_step)
 
 

time: 76.6 us -> 72.3 us (0.944)
  waiting for transfers between devices: 24.4 us -> 20.4 us
    ppermute x15, waiting for transfers between devices: 21.7 us -> 17.7 us  [shifted(): got.append(lax.ppermute(value_of(k), axis, pairs))]
  transfers between devices with their start and end apart: 16 -> 16, of which waited for: 11 -> 12; matrix products, arithmetic and copies ran while one was open for 25% -> 27% of each run, Pallas kernels for 0% -> 0%
where the time goes in v5:
time: 72.3 us; the launch traced here: 72 us
  starting transfers between devices  20.6 us (28%)
  waiting for transfers between devices  20.4 us (28%)
  other arithmetic  19.8 us (27%)
  local copies, waits for them, and re-layouts  5.78 us (8%)
  between operations  2.97 us (4%)
  matrix products  2.42 us (3%)
    convert_element_type x1, other arithmetic, projection_block(): return (gauss * rank ** (-0.5)).astype(jnp.bfloat16)  18.2 us
    ppermute x15, waiting for transfers between devices, shifted(): got.append(lax.ppermute(value_of(k), axis, pairs))  17.7 us
    ppermute x15, starting transfers between devices, shifted(): got.append(lax.ppermute(value_of(k), axis, pairs))  14.2 us
    all_to_all x1, starting transfers between devices, per_device(): held = lax.all_to_all(pieces, 'replica', 0, 0, tiled=True)  6.35 us
    all_to_all x1, waiting for transfers between devices, per_device(): held = lax.all_to_all(pieces, 'replica', 0, 0, tiled=True)  2.72 us
    another operation x1, local copies, waits for them, and re-layouts, per_device(): pieces = gradient.reshape(rows, n_rep, width).transpose(1, 0, 2)  2.16 us
    dot_general x4, matrix products, per_device(): term = jnp.dot(held[r], projection, preferred_element_type=jnp.float32)  1.74 us
    gather x5, local copies, waits for them, and re-layouts, by_source(): return jnp.take(jnp.stack(got), order, axis=0)  1.72 us
  transfers between devices with their start and end apart: 16, of which 12 were waited for; matrix products, arithmetic and copies ran while one was open for 27% of the time, Pallas kernels for 0%

profile of v5, /device:TPU:0, one launch (start us, length us, event | category | flops | bytes accessed | tf_op | source)
XLA Modules:
  0.0 72.0 jit_solution(7753324114084015501)
XLA Ops:
  0.6 2.2 %reshape_squeeze.3 = bf16[64,4,1792]{2,1,0:T(4,128)(2,1)S(1)} reshape(bf16[1,64,7168]{2,1,0:T(8,128)(2,1)} %param.5) | data formatting | bytes 1835008 | tf_op jit(solution)/shard_map/reshape;squeeze | solution.py:118
  2.8 1.0 %copy.10 = bf16[4,64,1792]{2,1,0:T(8,128)(2,1)} copy(bf16[4,64,1792]{2,0,1:T(4,128)(2,1)S(1)} %bitcast.74) | data formatting | bytes 1835008 | tf_op jit(solution)/shard_map/transpose | solution.py:118
  3.8 6.3 %all-to-all-start = ((bf16[4,64,1792]{2,1,0:T(8,128)(2,1)}), bf16[4,64,1792]{2,1,0:T(8,128)(2,1)S(1)}, u32[]{:S(2)}, u32[]{:S(2)}) async-start(bf16[4,64,1792]{2,1,0:T(8,128)(2,1)} %copy.10), calls=%async_computation | async-start | bytes 1835008 | tf_op jit(solution)/shard_map/all_to_all | solution.py:119
  10.2 0.6 fusion.37
  12.1 18.2 %fusion.18 = bf16[1792,512]{1,0:T(8,128)(2,1)S(1)} fusion(s32[]{:T(128)} %bitcast, s32[1792]{0:T(1024)S(1)} %add_multiply_fusion), kind=kLoop, calls=%fused_computation.27 | loop fusion | flops 32112640 | bytes 1842180 | tf_op jit(solution)/shard_map/convert_element_type | solution.py:37
  30.4 2.7 %all-to-all-done = bf16[4,64,1792]{2,1,0:T(8,128)(2,1)S(1)} async-done(((bf16[4,64,1792]{2,1,0:T(8,128)(2,1)}), bf16[4,64,1792]{2,1,0:T(8,128)(2,1)S(1)}, u32[]{:S(2)}, u32[]{:S(2)}) %all-to-all-start) | async-done | bytes 917536 | tf_op jit(solution)/shard_map/all_to_all | solution.py:119
  33.5 0.4 convolution_add_fusion.2
  34.4 0.4 fusion.20
  35.0 1.7 %collective-permute-start.2 = (f32[16,512]{1,0:T(8,128)S(1)}, f32[16,512]{1,0:T(8,128)S(1)}, u32[]{:S(2)}, u32[]{:S(2)}) collective-permute-start(f32[16,512]{1,0:T(8,128)S(1)} %get-tuple-element.11), channel_id=1, source_target_pairs={{0,24},{8,0},{16,8},{24,16},{1,25},{9,1},{17,9},{25,17},{2,26},{10... | collective-permute-start | bytes 98312 | tf_op jit(solution)/shard_map/ppermute | solution.py:76
  36.7 1.5 %collective-permute-start.1 = (f32[16,512]{1,0:T(8,128)S(1)}, f32[16,512]{1,0:T(8,128)S(1)}, u32[]{:S(2)}, u32[]{:S(2)}) collective-permute-start(f32[16,512]{1,0:T(8,128)S(1)} %get-tuple-element.12), channel_id=1, source_target_pairs={{0,16},{8,24},{16,0},{24,8},{1,17},{9,25},{17,1},{25,9},{2,18},{10... | collective-permute-start | bytes 98312 | tf_op jit(solution)/shard_map/ppermute | solution.py:76
  38.3 2.3 %collective-permute-done.1 = f32[16,512]{1,0:T(8,128)S(1)} collective-permute-done((f32[16,512]{1,0:T(8,128)S(1)}, f32[16,512]{1,0:T(8,128)S(1)}, u32[]{:S(2)}, u32[]{:S(2)}) %collective-permute-start.1) | collective-permute-done | bytes 32800 | tf_op jit(solution)/shard_map/ppermute | solution.py:76
  40.7 3.8 %collective-permute-start.5 = (f32[4,512]{1,0:T(4,128)S(1)}, f32[4,512]{1,0:T(4,128)S(1)}, u32[]{:S(2)}, u32[]{:S(2)}) collective-permute-start(f32[4,512]{1,0:T(4,128)S(1)} %get-tuple-element.14), channel_id=1, source_target_pairs={{0,6},{2,0},{4,2},{6,4},{1,7},{3,1},{5,3},{7,5},{8,14},{10,8},{12,... | collective-permute-start | bytes 24584 | tf_op jit(solution)/shard_map/ppermute | solution.py:76
  44.6 1.6 %collective-permute-done.3 = f32[4,512]{1,0:T(4,128)S(1)} collective-permute-done((f32[4,512]{1,0:T(4,128)S(1)}, f32[4,512]{1,0:T(4,128)S(1)}, u32[]{:S(2)}, u32[]{:S(2)}) %collective-permute-start.3) | collective-permute-done | bytes 8224 | tf_op jit(solution)/shard_map/ppermute | solution.py:76
  46.2 2.9 %collective-permute-done.4 = f32[4,512]{1,0:T(4,128)S(1)} collective-permute-done((f32[4,512]{1,0:T(4,128)S(1)}, f32[4,512]{1,0:T(4,128)S(1)}, u32[]{:S(2)}, u32[]{:S(2)}) %collective-permute-start.4) | collective-permute-done | bytes 8224 | tf_op jit(solution)/shard_map/ppermute | solution.py:76
  49.1 1.0 %collective-permute-start.8 = (bf16[4,512]{1,0:T(4,128)(2,1)S(1)}, bf16[4,512]{1,0:T(4,128)(2,1)S(1)}, u32[]{:S(2)}, u32[]{:S(2)}) collective-permute-start(bf16[4,512]{1,0:T(4,128)(2,1)S(1)} %fusion.28), channel_id=1, source_target_pairs={{0,6},{2,0},{4,2},{6,4},{1,7},{3,1},{5,3},{7,5},{8,14},{10,8},{12,... | collective-permute-start | bytes 12296 | tf_op jit(solution)/shard_map/ppermute | solution.py:76
  50.1 1.2 %collective-permute-start.6 = (bf16[4,512]{1,0:T(4,128)(2,1)S(1)}, bf16[4,512]{1,0:T(4,128)(2,1)S(1)}, u32[]{:S(2)}, u32[]{:S(2)}) collective-permute-start(bf16[4,512]{1,0:T(4,128)(2,1)S(1)} %fusion.28), channel_id=1, source_target_pairs={{0,2},{2,4},{4,6},{6,0},{1,3},{3,5},{5,7},{7,1},{8,10},{10,12},{12... | collective-permute-start | bytes 12296 | tf_op jit(solution)/shard_map/ppermute | solution.py:76
  51.4 1.3 %collective-permute-done.8 = bf16[4,512]{1,0:T(4,128)(2,1)S(1)} collective-permute-done((bf16[4,512]{1,0:T(4,128)(2,1)S(1)}, bf16[4,512]{1,0:T(4,128)(2,1)S(1)}, u32[]{:S(2)}, u32[]{:S(2)}) %collective-permute-start.8) | collective-permute-done | bytes 4128 | tf_op jit(solution)/shard_map/ppermute | solution.py:76
  52.8 1.8 %collective-permute-done.7 = bf16[4,512]{1,0:T(4,128)(2,1)S(1)} collective-permute-done((bf16[4,512]{1,0:T(4,128)(2,1)S(1)}, bf16[4,512]{1,0:T(4,128)(2,1)S(1)}, u32[]{:S(2)}, u32[]{:S(2)}) %collective-permute-start.7) | collective-permute-done | bytes 4128 | tf_op jit(solution)/shard_map/ppermute | solution.py:76
  54.6 0.9 %collective-permute-done.6 = bf16[4,512]{1,0:T(4,128)(2,1)S(1)} collective-permute-done((bf16[4,512]{1,0:T(4,128)(2,1)S(1)}, bf16[4,512]{1,0:T(4,128)(2,1)S(1)}, u32[]{:S(2)}, u32[]{:S(2)}) %collective-permute-start.6) | collective-permute-done | bytes 4128 | tf_op jit(solution)/shard_map/ppermute | solution.py:76
  55.5 0.6 gather_fusion
  56.2 1.6 %collective-permute-start.10 = (bf16[16,512]{1,0:T(8,128)(2,1)S(1)}, bf16[16,512]{1,0:T(8,128)(2,1)S(1)}, u32[]{:S(2)}, u32[]{:S(2)}) collective-permute-start(bf16[16,512]{1,0:T(8,128)(2,1)S(1)} %broadcast_select_fusion), channel_id=1, source_target_pairs={{0,16},{8,24},{16,0},{24,8},{1,17},{9,25},{17,1},{25,9},{2,18},{10... | collective-permute-start | bytes 49160 | tf_op jit(solution)/shard_map/ppermute | solution.py:76
  58.0 2.0 %collective-permute-done.10 = bf16[16,512]{1,0:T(8,128)(2,1)S(1)} collective-permute-done((bf16[16,512]{1,0:T(8,128)(2,1)S(1)}, bf16[16,512]{1,0:T(8,128)(2,1)S(1)}, u32[]{:S(2)}, u32[]{:S(2)}) %collective-permute-start.10) | collective-permute-done | bytes 16416 | tf_op jit(solution)/shard_map/ppermute | solution.py:76
  60.0 0.9 %collective-permute-done.9 = bf16[16,512]{1,0:T(8,128)(2,1)S(1)} collective-permute-done((bf16[16,512]{1,0:T(8,128)(2,1)S(1)}, bf16[16,512]{1,0:T(8,128)(2,1)S(1)}, u32[]{:S(2)}, u32[]{:S(2)}) %collective-permute-start.9) | collective-permute-done | bytes 16416 | tf_op jit(solution)/shard_map/ppermute | solution.py:76
  60.9 0.6 gather_fusion.1
  61.5 0.7 convolution_convert_fusion
  62.2 1.7 %collective-permute-start.14 = (bf16[16,1792]{1,0:T(8,128)(2,1)S(1)}, bf16[16,1792]{1,0:T(8,128)(2,1)S(1)}, u32[]{:S(2)}, u32[]{:S(2)}) collective-permute-start(bf16[16,1792]{1,0:T(8,128)(2,1)S(1)} %get-tuple-element.7), channel_id=1, source_target_pairs={{0,6},{2,0},{4,2},{6,4},{1,7},{3,1},{5,3},{7,5},{8,14},{10,8},{12,... | collective-permute-start | bytes 172040 | tf_op jit(solution)/shard_map/ppermute | solution.py:76
  64.0 1.5 %collective-permute-start.12 = (bf16[16,1792]{1,0:T(8,128)(2,1)S(1)}, bf16[16,1792]{1,0:T(8,128)(2,1)S(1)}, u32[]{:S(2)}, u32[]{:S(2)}) collective-permute-start(bf16[16,1792]{1,0:T(8,128)(2,1)S(1)} %get-tuple-element.9), channel_id=1, source_target_pairs={{0,2},{2,4},{4,6},{6,0},{1,3},{3,5},{5,7},{7,1},{8,10},{10,12},{12... | collective-permute-start | bytes 172040 | tf_op jit(solution)/shard_map/ppermute | solution.py:76
  66.1 0.9 %collective-permute-done.14 = bf16[16,1792]{1,0:T(8,128)(2,1)S(1)} collective-permute-done((bf16[16,1792]{1,0:T(8,128)(2,1)S(1)}, bf16[16,1792]{1,0:T(8,128)(2,1)S(1)}, u32[]{:S(2)}, u32[]{:S(2)}) %collective-permute-start.14) | collective-permute-done | bytes 57376 | tf_op jit(solution)/shard_map/ppermute | solution.py:76
  67.1 2.4 %collective-permute-done.13 = bf16[16,1792]{1,0:T(8,128)(2,1)S(1)} collective-permute-done((bf16[16,1792]{1,0:T(8,128)(2,1)S(1)}, bf16[16,1792]{1,0:T(8,128)(2,1)S(1)}, u32[]{:S(2)}, u32[]{:S(2)}) %collective-permute-start.13) | collective-permute-done | bytes 57376 | tf_op jit(solution)/shard_map/ppermute | solution.py:76
  69.4 0.6 collective-permute-done.12
  70.1 0.6 gather_fusion.2
  70.8 1.2 %multiply_divide_fusion = (f32[16,7168]{1,0:T(8,128)}, f32[16,7168]{1,0:T(8,128)}, f32[16,7168]{1,0:T(8,128)}) fusion(f32[]{:T(128)} %bitcast.35, f32[]{:T(128)} %bitcast.34, f32[16,7168]{1,0:T(8,128)S(1)} %bitcast.75, f32[16,7168]{1,0:T(8,128)S(1)} %copy-done, f32[16,7168]{1,0:T(8,128)S(1)} %copy-done.1), kind=kLoop, calls=%fused_computation.37 | loop fusion | flops 1261568 | bytes 2752520 | tf_op jit(solution)/shard_map/div | solution.py:46
  (42 shorter events, 1.9 us)
Async XLA Ops:
  2.8 7.4 %copy-start.2 = (s32[2]{0:T(128)S(1)}, s32[2]{0:T(128)}, u32[]{:S(2)}) copy-start(s32[2]{0:T(128)} %param.6) | copy-start | bytes 28
  3.8 29.3 %all-to-all-start = ((bf16[4,64,1792]{2,1,0:T(8,128)(2,1)}), bf16[4,64,1792]{2,1,0:T(8,128)(2,1)S(1)}, u32[]{:S(2)}, u32[]{:S(2)}) async-start(bf16[4,64,1792]{2,1,0:T(8,128)(2,1)} %copy.10), calls=%async_computation | async-start | bytes 1835008 | tf_op jit(solution)/shard_map/all_to_all | solution.py:119
  34.9 3.4 %collective-permute-start = (f32[16,512]{1,0:T(8,128)S(1)}, f32[16,512]{1,0:T(8,128)S(1)}, u32[]{:S(2)}, u32[]{:S(2)}) collective-permute-start(f32[16,512]{1,0:T(8,128)S(1)} %get-tuple-element.10), channel_id=1, source_target_pairs={{0,8},{8,16},{16,24},{24,0},{1,9},{9,17},{17,25},{25,1},{2,10},{10... | collective-permute-start | bytes 98312 | tf_op jit(solution)/shard_map/ppermute | solution.py:76
  35.0 3.3 %collective-permute-start.2 = (f32[16,512]{1,0:T(8,128)S(1)}, f32[16,512]{1,0:T(8,128)S(1)}, u32[]{:S(2)}, u32[]{:S(2)}) collective-permute-start(f32[16,512]{1,0:T(8,128)S(1)} %get-tuple-element.11), channel_id=1, source_target_pairs={{0,24},{8,0},{16,8},{24,16},{1,25},{9,1},{17,9},{25,17},{2,26},{10... | collective-permute-start | bytes 98312 | tf_op jit(solution)/shard_map/ppermute | solution.py:76
  36.7 3.9 %collective-permute-start.1 = (f32[16,512]{1,0:T(8,128)S(1)}, f32[16,512]{1,0:T(8,128)S(1)}, u32[]{:S(2)}, u32[]{:S(2)}) collective-permute-start(f32[16,512]{1,0:T(8,128)S(1)} %get-tuple-element.12), channel_id=1, source_target_pairs={{0,16},{8,24},{16,0},{24,8},{1,17},{9,25},{17,1},{25,9},{2,18},{10... | collective-permute-start | bytes 98312 | tf_op jit(solution)/shard_map/ppermute | solution.py:76
  40.7 5.5 %collective-permute-start.3 = (f32[4,512]{1,0:T(4,128)S(1)}, f32[4,512]{1,0:T(4,128)S(1)}, u32[]{:S(2)}, u32[]{:S(2)}) collective-permute-start(f32[4,512]{1,0:T(4,128)S(1)} %get-tuple-element.13), channel_id=1, source_target_pairs={{0,2},{2,4},{4,6},{6,0},{1,3},{3,5},{5,7},{7,1},{8,10},{10,12},{12... | collective-permute-start | bytes 24584 | tf_op jit(solution)/shard_map/ppermute | solution.py:76
  40.7 5.4 %collective-permute-start.5 = (f32[4,512]{1,0:T(4,128)S(1)}, f32[4,512]{1,0:T(4,128)S(1)}, u32[]{:S(2)}, u32[]{:S(2)}) collective-permute-start(f32[4,512]{1,0:T(4,128)S(1)} %get-tuple-element.14), channel_id=1, source_target_pairs={{0,6},{2,0},{4,2},{6,4},{1,7},{3,1},{5,3},{7,5},{8,14},{10,8},{12,... | collective-permute-start | bytes 24584 | tf_op jit(solution)/shard_map/ppermute | solution.py:76
  44.5 4.5 %collective-permute-start.4 = (f32[4,512]{1,0:T(4,128)S(1)}, f32[4,512]{1,0:T(4,128)S(1)}, u32[]{:S(2)}, u32[]{:S(2)}) collective-permute-start(f32[4,512]{1,0:T(4,128)S(1)} %get-tuple-element.15), channel_id=1, source_target_pairs={{0,4},{2,6},{4,0},{6,2},{1,5},{3,7},{5,1},{7,3},{8,12},{10,14},{12... | collective-permute-start | bytes 24584 | tf_op jit(solution)/shard_map/ppermute | solution.py:76
  49.1 3.7 %collective-permute-start.8 = (bf16[4,512]{1,0:T(4,128)(2,1)S(1)}, bf16[4,512]{1,0:T(4,128)(2,1)S(1)}, u32[]{:S(2)}, u32[]{:S(2)}) collective-permute-start(bf16[4,512]{1,0:T(4,128)(2,1)S(1)} %fusion.28), channel_id=1, source_target_pairs={{0,6},{2,0},{4,2},{6,4},{1,7},{3,1},{5,3},{7,5},{8,14},{10,8},{12,... | collective-permute-start | bytes 12296 | tf_op jit(solution)/shard_map/ppermute | solution.py:76
  50.1 4.5 %collective-permute-start.7 = (bf16[4,512]{1,0:T(4,128)(2,1)S(1)}, bf16[4,512]{1,0:T(4,128)(2,1)S(1)}, u32[]{:S(2)}, u32[]{:S(2)}) collective-permute-start(bf16[4,512]{1,0:T(4,128)(2,1)S(1)} %fusion.28), channel_id=1, source_target_pairs={{0,4},{2,6},{4,0},{6,2},{1,5},{3,7},{5,1},{7,3},{8,12},{10,14},{12... | collective-permute-start | bytes 12296 | tf_op jit(solution)/shard_map/ppermute | solution.py:76
  50.1 5.4 %collective-permute-start.6 = (bf16[4,512]{1,0:T(4,128)(2,1)S(1)}, bf16[4,512]{1,0:T(4,128)(2,1)S(1)}, u32[]{:S(2)}, u32[]{:S(2)}) collective-permute-start(bf16[4,512]{1,0:T(4,128)(2,1)S(1)} %fusion.28), channel_id=1, source_target_pairs={{0,2},{2,4},{4,6},{6,0},{1,3},{3,5},{5,7},{7,1},{8,10},{10,12},{12... | collective-permute-start | bytes 12296 | tf_op jit(solution)/shard_map/ppermute | solution.py:76
  56.2 1.8 %collective-permute-start.11 = (bf16[16,512]{1,0:T(8,128)(2,1)S(1)}, bf16[16,512]{1,0:T(8,128)(2,1)S(1)}, u32[]{:S(2)}, u32[]{:S(2)}) collective-permute-start(bf16[16,512]{1,0:T(8,128)(2,1)S(1)} %broadcast_select_fusion), channel_id=1, source_target_pairs={{0,24},{8,0},{16,8},{24,16},{1,25},{9,1},{17,9},{25,17},{2,26},{10... | collective-permute-start | bytes 49160 | tf_op jit(solution)/shard_map/ppermute | solution.py:76
  56.2 3.8 %collective-permute-start.10 = (bf16[16,512]{1,0:T(8,128)(2,1)S(1)}, bf16[16,512]{1,0:T(8,128)(2,1)S(1)}, u32[]{:S(2)}, u32[]{:S(2)}) collective-permute-start(bf16[16,512]{1,0:T(8,128)(2,1)S(1)} %broadcast_select_fusion), channel_id=1, source_target_pairs={{0,16},{8,24},{16,0},{24,8},{1,17},{9,25},{17,1},{25,9},{2,18},{10... | collective-permute-start | bytes 49160 | tf_op jit(solution)/shard_map/ppermute | solution.py:76
  57.7 3.2 %collective-permute-start.9 = (bf16[16,512]{1,0:T(8,128)(2,1)S(1)}, bf16[16,512]{1,0:T(8,128)(2,1)S(1)}, u32[]{:S(2)}, u32[]{:S(2)}) collective-permute-start(bf16[16,512]{1,0:T(8,128)(2,1)S(1)} %broadcast_select_fusion), channel_id=1, source_target_pairs={{0,8},{8,16},{16,24},{24,0},{1,9},{9,17},{17,25},{25,1},{2,10},{10... | collective-permute-start | bytes 49160 | tf_op jit(solution)/shard_map/ppermute | solution.py:76
  62.1 8.6 %copy-start = (f32[16,7168]{1,0:T(8,128)S(1)}, f32[16,7168]{1,0:T(8,128)}, u32[]{:S(2)}) copy-start(f32[16,7168]{1,0:T(8,128)} %param.9) | copy-start | bytes 1376260
  62.2 8.6 %copy-start.1 = (f32[16,7168]{1,0:T(8,128)S(1)}, f32[16,7168]{1,0:T(8,128)}, u32[]{:S(2)}) copy-start(f32[16,7168]{1,0:T(8,128)} %param.8) | copy-start | bytes 1376260
  62.2 4.9 %collective-permute-start.14 = (bf16[16,1792]{1,0:T(8,128)(2,1)S(1)}, bf16[16,1792]{1,0:T(8,128)(2,1)S(1)}, u32[]{:S(2)}, u32[]{:S(2)}) collective-permute-start(bf16[16,1792]{1,0:T(8,128)(2,1)S(1)} %get-tuple-element.7), channel_id=1, source_target_pairs={{0,6},{2,0},{4,2},{6,4},{1,7},{3,1},{5,3},{7,5},{8,14},{10,8},{12,... | collective-permute-start | bytes 172040 | tf_op jit(solution)/shard_map/ppermute | solution.py:76
  63.9 5.5 %collective-permute-start.13 = (bf16[16,1792]{1,0:T(8,128)(2,1)S(1)}, bf16[16,1792]{1,0:T(8,128)(2,1)S(1)}, u32[]{:S(2)}, u32[]{:S(2)}) collective-permute-start(bf16[16,1792]{1,0:T(8,128)(2,1)S(1)} %get-tuple-element.8), channel_id=1, source_target_pairs={{0,4},{2,6},{4,0},{6,2},{1,5},{3,7},{5,1},{7,3},{8,12},{10,14},{12... | collective-permute-start | bytes 172040 | tf_op jit(solution)/shard_map/ppermute | solution.py:76
  64.0 6.1 %collective-permute-start.12 = (bf16[16,1792]{1,0:T(8,128)(2,1)S(1)}, bf16[16,1792]{1,0:T(8,128)(2,1)S(1)}, u32[]{:S(2)}, u32[]{:S(2)}) collective-permute-start(bf16[16,1792]{1,0:T(8,128)(2,1)S(1)} %get-tuple-element.9), channel_id=1, source_target_pairs={{0,2},{2,4},{4,6},{6,0},{1,3},{3,5},{5,7},{7,1},{8,10},{10,12},{12... | collective-permute-start | bytes 172040 | tf_op jit(solution)/shard_map/ppermute | solution.py:76

commit v6 on v5

--- a/solution.py
+++ b/solution.py
@@ -115,7 +115,7 @@
 
     projection = lax.optimization_barrier(projection_block(first, width, RANK, seeds))
 
-    pieces = gradient.reshape(rows, n_rep, width).transpose(1, 0, 2)
+    pieces = jnp.stack([gradient[:, i * width : (i + 1) * width] for i in range(n_rep)])
     held = lax.all_to_all(pieces, "replica", 0, 0, tiled=True)
 
     partial_value = None

time: 72.3 us -> 71.5 us (0.989)
  local copies, waits for them, and re-layouts: 5.78 us -> 3.93 us
  other arithmetic: 19.8 us -> 20.9 us
    another operation x0 -> x1, other arithmetic: none -> 1.06 us  [per_device(): jnp.stack([gradient[:, i * width:(i + 1) * width] for i in range(n_rep)])]
    transpose x1 -> x0, local copies, waits for them, and re-layouts: 1.04 us -> none  [per_device(): pieces = gradient.reshape(rows, n_rep, width).transpose(1, 0, 2)]
    another operation x1, local copies, waits for them, and re-layouts: 2.16 us -> 1.34 us  [per_device(): jnp.stack([gradient[:, i * width:(i + 1) * width] for i in range(n_rep)])]
where the time goes in v6:
time: 71.5 us; the launch traced here: 71.2 us
  other arithmetic  20.9 us (29%)
  starting transfers between devices  20.6 us (29%)
  waiting for transfers between devices  20.4 us (29%)
  local copies, waits for them, and re-layouts  3.93 us (5%)
  between operations  2.97 us (4%)
  matrix products  2.41 us (3%)
    convert_element_type x1, other arithmetic, projection_block(): return (gauss * rank ** (-0.5)).astype(jnp.bfloat16)  18.2 us
    ppermute x15, waiting for transfers between devices, shifted(): got.append(lax.ppermute(value_of(k), axis, pairs))  17.7 us
    ppermute x15, starting transfers between devices, shifted(): got.append(lax.ppermute(value_of(k), axis, pairs))  14.3 us
    all_to_all x1, starting transfers between devices, per_device(): held = lax.all_to_all(pieces, 'replica', 0, 0, tiled=True)  6.35 us
    all_to_all x1, waiting for transfers between devices, per_device(): held = lax.all_to_all(pieces, 'replica', 0, 0, tiled=True)  2.72 us
    dot_general x4, matrix products, per_device(): term = jnp.dot(held[r], projection, preferred_element_type=jnp.float32)  1.73 us
    gather x5, local copies, waits for them, and re-layouts, by_source(): return jnp.take(jnp.stack(got), order, axis=0)  1.72 us
  transfers between devices with their start and end apart: 16, of which 12 were waited for; matrix products, arithmetic and copies ran while one was open for 27% of the time, Pallas kernels for 0%

profile of v6, /device:TPU:0, one launch (start us, length us, event | category | flops | bytes accessed | tf_op | source)
XLA Modules:
  0.0 71.2 jit_solution(5208341792968091787)
XLA Ops:
  0.6 1.3 %slice_bitcast_fusion.11 = (bf16[1,64,1792]{2,1,0:T(8,128)(2,1)S(1)}, bf16[1,64,1792]{2,1,0:T(8,128)(2,1)S(1)}, bf16[1,64,1792]{2,1,0:T(8,128)(2,1)S(1)}, bf16[1,64,1792]{2,1,0:T(8,128)(2,1)S(1)}) fusion(bf16[64,7168]{1,0:T(8,128)(2,1)} %bitcast.81), kind=kLoop, calls=%fused_computation.48 | loop fusion | bytes 1835008 | tf_op jit(solution)/shard_map/stack | solution.py:118
  2.0 1.1 %pad_maximum_fusion = bf16[4,64,1792]{2,1,0:T(8,128)(2,1)} fusion(bf16[1,64,1792]{2,1,0:T(8,128)(2,1)S(1)} %get-tuple-element.7, bf16[1,64,1792]{2,1,0:T(8,128)(2,1)S(1)} %get-tuple-element.8, bf16[1,64,1792]{2,1,0:T(8,128)(2,1)S(1)} %get-tuple-element.9, bf16[1,64,1792]{2,1,0:T(8,128)(2,1)S(1)} %get-tuple-element.6), kind=kLoop, calls=%fused_computation.34 | loop fusion | flops 1376256 | bytes 1835008 | tf_op jit(solution)/shard_map/stack | solution.py:118
  3.0 6.3 %all-to-all-start = ((bf16[4,64,1792]{2,1,0:T(8,128)(2,1)}), bf16[4,64,1792]{2,1,0:T(8,128)(2,1)S(1)}, u32[]{:S(2)}, u32[]{:S(2)}) async-start(bf16[4,64,1792]{2,1,0:T(8,128)(2,1)} %pad_maximum_fusion), calls=%async_computation | async-start | bytes 1835008 | tf_op jit(solution)/shard_map/all_to_all | solution.py:119
  9.4 0.6 fusion.37
  11.3 18.2 %fusion.18 = bf16[1792,512]{1,0:T(8,128)(2,1)S(1)} fusion(s32[]{:T(128)} %bitcast.6, s32[1792]{0:T(1024)S(1)} %add_multiply_fusion), kind=kLoop, calls=%fused_computation.27 | loop fusion | flops 32112640 | bytes 1842180 | tf_op jit(solution)/shard_map/convert_element_type | solution.py:37
  29.6 2.7 %all-to-all-done = bf16[4,64,1792]{2,1,0:T(8,128)(2,1)S(1)} async-done(((bf16[4,64,1792]{2,1,0:T(8,128)(2,1)}), bf16[4,64,1792]{2,1,0:T(8,128)(2,1)S(1)}, u32[]{:S(2)}, u32[]{:S(2)}) %all-to-all-start) | async-done | bytes 917536 | tf_op jit(solution)/shard_map/all_to_all | solution.py:119
  32.7 0.4 convolution_add_fusion.2
  33.6 0.4 fusion.20
  34.1 1.7 %collective-permute-start.2 = (f32[16,512]{1,0:T(8,128)S(1)}, f32[16,512]{1,0:T(8,128)S(1)}, u32[]{:S(2)}, u32[]{:S(2)}) collective-permute-start(f32[16,512]{1,0:T(8,128)S(1)} %get-tuple-element.15), channel_id=1, source_target_pairs={{0,24},{8,0},{16,8},{24,16},{1,25},{9,1},{17,9},{25,17},{2,26},{10... | collective-permute-start | bytes 98312 | tf_op jit(solution)/shard_map/ppermute | solution.py:76
  35.9 1.5 %collective-permute-start.1 = (f32[16,512]{1,0:T(8,128)S(1)}, f32[16,512]{1,0:T(8,128)S(1)}, u32[]{:S(2)}, u32[]{:S(2)}) collective-permute-start(f32[16,512]{1,0:T(8,128)S(1)} %get-tuple-element.16), channel_id=1, source_target_pairs={{0,16},{8,24},{16,0},{24,8},{1,17},{9,25},{17,1},{25,9},{2,18},{10... | collective-permute-start | bytes 98312 | tf_op jit(solution)/shard_map/ppermute | solution.py:76
  37.5 2.3 %collective-permute-done.1 = f32[16,512]{1,0:T(8,128)S(1)} collective-permute-done((f32[16,512]{1,0:T(8,128)S(1)}, f32[16,512]{1,0:T(8,128)S(1)}, u32[]{:S(2)}, u32[]{:S(2)}) %collective-permute-start.1) | collective-permute-done | bytes 32800 | tf_op jit(solution)/shard_map/ppermute | solution.py:76
  39.9 3.8 %collective-permute-start.5 = (f32[4,512]{1,0:T(4,128)S(1)}, f32[4,512]{1,0:T(4,128)S(1)}, u32[]{:S(2)}, u32[]{:S(2)}) collective-permute-start(f32[4,512]{1,0:T(4,128)S(1)} %get-tuple-element.18), channel_id=1, source_target_pairs={{0,6},{2,0},{4,2},{6,4},{1,7},{3,1},{5,3},{7,5},{8,14},{10,8},{12,... | collective-permute-start | bytes 24584 | tf_op jit(solution)/shard_map/ppermute | solution.py:76
  43.8 1.6 %collective-permute-done.3 = f32[4,512]{1,0:T(4,128)S(1)} collective-permute-done((f32[4,512]{1,0:T(4,128)S(1)}, f32[4,512]{1,0:T(4,128)S(1)}, u32[]{:S(2)}, u32[]{:S(2)}) %collective-permute-start.3) | collective-permute-done | bytes 8224 | tf_op jit(solution)/shard_map/ppermute | solution.py:76
  45.4 2.9 %collective-permute-done.4 = f32[4,512]{1,0:T(4,128)S(1)} collective-permute-done((f32[4,512]{1,0:T(4,128)S(1)}, f32[4,512]{1,0:T(4,128)S(1)}, u32[]{:S(2)}, u32[]{:S(2)}) %collective-permute-start.4) | collective-permute-done | bytes 8224 | tf_op jit(solution)/shard_map/ppermute | solution.py:76
  48.3 1.0 %collective-permute-start.8 = (bf16[4,512]{1,0:T(4,128)(2,1)S(1)}, bf16[4,512]{1,0:T(4,128)(2,1)S(1)}, u32[]{:S(2)}, u32[]{:S(2)}) collective-permute-start(bf16[4,512]{1,0:T(4,128)(2,1)S(1)} %fusion.28), channel_id=1, source_target_pairs={{0,6},{2,0},{4,2},{6,4},{1,7},{3,1},{5,3},{7,5},{8,14},{10,8},{12,... | collective-permute-start | bytes 12296 | tf_op jit(solution)/shard_map/ppermute | solution.py:76
  49.3 1.2 %collective-permute-start.6 = (bf16[4,512]{1,0:T(4,128)(2,1)S(1)}, bf16[4,512]{1,0:T(4,128)(2,1)S(1)}, u32[]{:S(2)}, u32[]{:S(2)}) collective-permute-start(bf16[4,512]{1,0:T(4,128)(2,1)S(1)} %fusion.28), channel_id=1, source_target_pairs={{0,2},{2,4},{4,6},{6,0},{1,3},{3,5},{5,7},{7,1},{8,10},{10,12},{12... | collective-permute-start | bytes 12296 | tf_op jit(solution)/shard_map/ppermute | solution.py:76
  50.6 1.3 %collective-permute-done.8 = bf16[4,512]{1,0:T(4,128)(2,1)S(1)} collective-permute-done((bf16[4,512]{1,0:T(4,128)(2,1)S(1)}, bf16[4,512]{1,0:T(4,128)(2,1)S(1)}, u32[]{:S(2)}, u32[]{:S(2)}) %collective-permute-start.8) | collective-permute-done | bytes 4128 | tf_op jit(solution)/shard_map/ppermute | solution.py:76
  52.0 1.8 %collective-permute-done.7 = bf16[4,512]{1,0:T(4,128)(2,1)S(1)} collective-permute-done((bf16[4,512]{1,0:T(4,128)(2,1)S(1)}, bf16[4,512]{1,0:T(4,128)(2,1)S(1)}, u32[]{:S(2)}, u32[]{:S(2)}) %collective-permute-start.7) | collective-permute-done | bytes 4128 | tf_op jit(solution)/shard_map/ppermute | solution.py:76
  53.8 0.9 %collective-permute-done.6 = bf16[4,512]{1,0:T(4,128)(2,1)S(1)} collective-permute-done((bf16[4,512]{1,0:T(4,128)(2,1)S(1)}, bf16[4,512]{1,0:T(4,128)(2,1)S(1)}, u32[]{:S(2)}, u32[]{:S(2)}) %collective-permute-start.6) | collective-permute-done | bytes 4128 | tf_op jit(solution)/shard_map/ppermute | solution.py:76
  54.7 0.6 gather_fusion
  55.4 1.6 %collective-permute-start.10 = (bf16[16,512]{1,0:T(8,128)(2,1)S(1)}, bf16[16,512]{1,0:T(8,128)(2,1)S(1)}, u32[]{:S(2)}, u32[]{:S(2)}) collective-permute-start(bf16[16,512]{1,0:T(8,128)(2,1)S(1)} %broadcast_select_fusion), channel_id=1, source_target_pairs={{0,16},{8,24},{16,0},{24,8},{1,17},{9,25},{17,1},{25,9},{2,18},{10... | collective-permute-start | bytes 49160 | tf_op jit(solution)/shard_map/ppermute | solution.py:76
  57.2 2.0 %collective-permute-done.10 = bf16[16,512]{1,0:T(8,128)(2,1)S(1)} collective-permute-done((bf16[16,512]{1,0:T(8,128)(2,1)S(1)}, bf16[16,512]{1,0:T(8,128)(2,1)S(1)}, u32[]{:S(2)}, u32[]{:S(2)}) %collective-permute-start.10) | collective-permute-done | bytes 16416 | tf_op jit(solution)/shard_map/ppermute | solution.py:76
  59.2 0.9 %collective-permute-done.9 = bf16[16,512]{1,0:T(8,128)(2,1)S(1)} collective-permute-done((bf16[16,512]{1,0:T(8,128)(2,1)S(1)}, bf16[16,512]{1,0:T(8,128)(2,1)S(1)}, u32[]{:S(2)}, u32[]{:S(2)}) %collective-permute-start.9) | collective-permute-done | bytes 16416 | tf_op jit(solution)/shard_map/ppermute | solution.py:76
  60.1 0.6 gather_fusion.1
  60.7 0.7 convolution_convert_fusion
  61.4 1.7 %collective-permute-start.14 = (bf16[16,1792]{1,0:T(8,128)(2,1)S(1)}, bf16[16,1792]{1,0:T(8,128)(2,1)S(1)}, u32[]{:S(2)}, u32[]{:S(2)}) collective-permute-start(bf16[16,1792]{1,0:T(8,128)(2,1)S(1)} %get-tuple-element.11), channel_id=1, source_target_pairs={{0,6},{2,0},{4,2},{6,4},{1,7},{3,1},{5,3},{7,5},{8,14},{10,8},{12,... | collective-permute-start | bytes 172040 | tf_op jit(solution)/shard_map/ppermute | solution.py:76
  63.2 1.5 %collective-permute-start.12 = (bf16[16,1792]{1,0:T(8,128)(2,1)S(1)}, bf16[16,1792]{1,0:T(8,128)(2,1)S(1)}, u32[]{:S(2)}, u32[]{:S(2)}) collective-permute-start(bf16[16,1792]{1,0:T(8,128)(2,1)S(1)} %get-tuple-element.13), channel_id=1, source_target_pairs={{0,2},{2,4},{4,6},{6,0},{1,3},{3,5},{5,7},{7,1},{8,10},{10,12},{12... | collective-permute-start | bytes 172040 | tf_op jit(solution)/shard_map/ppermute | solution.py:76
  65.4 0.9 %collective-permute-done.14 = bf16[16,1792]{1,0:T(8,128)(2,1)S(1)} collective-permute-done((bf16[16,1792]{1,0:T(8,128)(2,1)S(1)}, bf16[16,1792]{1,0:T(8,128)(2,1)S(1)}, u32[]{:S(2)}, u32[]{:S(2)}) %collective-permute-start.14) | collective-permute-done | bytes 57376 | tf_op jit(solution)/shard_map/ppermute | solution.py:76
  66.3 2.4 %collective-permute-done.13 = bf16[16,1792]{1,0:T(8,128)(2,1)S(1)} collective-permute-done((bf16[16,1792]{1,0:T(8,128)(2,1)S(1)}, bf16[16,1792]{1,0:T(8,128)(2,1)S(1)}, u32[]{:S(2)}, u32[]{:S(2)}) %collective-permute-start.13) | collective-permute-done | bytes 57376 | tf_op jit(solution)/shard_map/ppermute | solution.py:76
  68.6 0.6 collective-permute-done.12
  69.3 0.6 gather_fusion.2
  70.0 1.2 %multiply_divide_fusion = (f32[16,7168]{1,0:T(8,128)}, f32[16,7168]{1,0:T(8,128)}, f32[16,7168]{1,0:T(8,128)}) fusion(f32[]{:T(128)} %bitcast.37, f32[]{:T(128)} %bitcast.36, f32[16,7168]{1,0:T(8,128)S(1)} %bitcast.80, f32[16,7168]{1,0:T(8,128)S(1)} %copy-done, f32[16,7168]{1,0:T(8,128)S(1)} %copy-done.1), kind=kLoop, calls=%fused_computation.38 | loop fusion | flops 1261568 | bytes 2752520 | tf_op jit(solution)/shard_map/div | solution.py:46
  (42 shorter events, 1.9 us)
Async XLA Ops:
  2.0 7.4 %copy-start.2 = (s32[2]{0:T(128)S(1)}, s32[2]{0:T(128)}, u32[]{:S(2)}) copy-start(s32[2]{0:T(128)} %param.6) | copy-start | bytes 28
  3.0 29.3 %all-to-all-start = ((bf16[4,64,1792]{2,1,0:T(8,128)(2,1)}), bf16[4,64,1792]{2,1,0:T(8,128)(2,1)S(1)}, u32[]{:S(2)}, u32[]{:S(2)}) async-start(bf16[4,64,1792]{2,1,0:T(8,128)(2,1)} %pad_maximum_fusion), calls=%async_computation | async-start | bytes 1835008 | tf_op jit(solution)/shard_map/all_to_all | solution.py:119
  34.1 3.4 %collective-permute-start = (f32[16,512]{1,0:T(8,128)S(1)}, f32[16,512]{1,0:T(8,128)S(1)}, u32[]{:S(2)}, u32[]{:S(2)}) collective-permute-start(f32[16,512]{1,0:T(8,128)S(1)} %get-tuple-element.14), channel_id=1, source_target_pairs={{0,8},{8,16},{16,24},{24,0},{1,9},{9,17},{17,25},{25,1},{2,10},{10... | collective-permute-start | bytes 98312 | tf_op jit(solution)/shard_map/ppermute | solution.py:76
  34.1 3.3 %collective-permute-start.2 = (f32[16,512]{1,0:T(8,128)S(1)}, f32[16,512]{1,0:T(8,128)S(1)}, u32[]{:S(2)}, u32[]{:S(2)}) collective-permute-start(f32[16,512]{1,0:T(8,128)S(1)} %get-tuple-element.15), channel_id=1, source_target_pairs={{0,24},{8,0},{16,8},{24,16},{1,25},{9,1},{17,9},{25,17},{2,26},{10... | collective-permute-start | bytes 98312 | tf_op jit(solution)/shard_map/ppermute | solution.py:76
  35.9 3.9 %collective-permute-start.1 = (f32[16,512]{1,0:T(8,128)S(1)}, f32[16,512]{1,0:T(8,128)S(1)}, u32[]{:S(2)}, u32[]{:S(2)}) collective-permute-start(f32[16,512]{1,0:T(8,128)S(1)} %get-tuple-element.16), channel_id=1, source_target_pairs={{0,16},{8,24},{16,0},{24,8},{1,17},{9,25},{17,1},{25,9},{2,18},{10... | collective-permute-start | bytes 98312 | tf_op jit(solution)/shard_map/ppermute | solution.py:76
  39.9 5.5 %collective-permute-start.3 = (f32[4,512]{1,0:T(4,128)S(1)}, f32[4,512]{1,0:T(4,128)S(1)}, u32[]{:S(2)}, u32[]{:S(2)}) collective-permute-start(f32[4,512]{1,0:T(4,128)S(1)} %get-tuple-element.17), channel_id=1, source_target_pairs={{0,2},{2,4},{4,6},{6,0},{1,3},{3,5},{5,7},{7,1},{8,10},{10,12},{12... | collective-permute-start | bytes 24584 | tf_op jit(solution)/shard_map/ppermute | solution.py:76
  39.9 5.4 %collective-permute-start.5 = (f32[4,512]{1,0:T(4,128)S(1)}, f32[4,512]{1,0:T(4,128)S(1)}, u32[]{:S(2)}, u32[]{:S(2)}) collective-permute-start(f32[4,512]{1,0:T(4,128)S(1)} %get-tuple-element.18), channel_id=1, source_target_pairs={{0,6},{2,0},{4,2},{6,4},{1,7},{3,1},{5,3},{7,5},{8,14},{10,8},{12,... | collective-permute-start | bytes 24584 | tf_op jit(solution)/shard_map/ppermute | solution.py:76
  43.7 4.5 %collective-permute-start.4 = (f32[4,512]{1,0:T(4,128)S(1)}, f32[4,512]{1,0:T(4,128)S(1)}, u32[]{:S(2)}, u32[]{:S(2)}) collective-permute-start(f32[4,512]{1,0:T(4,128)S(1)} %get-tuple-element.19), channel_id=1, source_target_pairs={{0,4},{2,6},{4,0},{6,2},{1,5},{3,7},{5,1},{7,3},{8,12},{10,14},{12... | collective-permute-start | bytes 24584 | tf_op jit(solution)/shard_map/ppermute | solution.py:76
  48.3 3.7 %collective-permute-start.8 = (bf16[4,512]{1,0:T(4,128)(2,1)S(1)}, bf16[4,512]{1,0:T(4,128)(2,1)S(1)}, u32[]{:S(2)}, u32[]{:S(2)}) collective-permute-start(bf16[4,512]{1,0:T(4,128)(2,1)S(1)} %fusion.28), channel_id=1, source_target_pairs={{0,6},{2,0},{4,2},{6,4},{1,7},{3,1},{5,3},{7,5},{8,14},{10,8},{12,... | collective-permute-start | bytes 12296 | tf_op jit(solution)/shard_map/ppermute | solution.py:76
  49.3 4.5 %collective-permute-start.7 = (bf16[4,512]{1,0:T(4,128)(2,1)S(1)}, bf16[4,512]{1,0:T(4,128)(2,1)S(1)}, u32[]{:S(2)}, u32[]{:S(2)}) collective-permute-start(bf16[4,512]{1,0:T(4,128)(2,1)S(1)} %fusion.28), channel_id=1, source_target_pairs={{0,4},{2,6},{4,0},{6,2},{1,5},{3,7},{5,1},{7,3},{8,12},{10,14},{12... | collective-permute-start | bytes 12296 | tf_op jit(solution)/shard_map/ppermute | solution.py:76
  49.3 5.4 %collective-permute-start.6 = (bf16[4,512]{1,0:T(4,128)(2,1)S(1)}, bf16[4,512]{1,0:T(4,128)(2,1)S(1)}, u32[]{:S(2)}, u32[]{:S(2)}) collective-permute-start(bf16[4,512]{1,0:T(4,128)(2,1)S(1)} %fusion.28), channel_id=1, source_target_pairs={{0,2},{2,4},{4,6},{6,0},{1,3},{3,5},{5,7},{7,1},{8,10},{10,12},{12... | collective-permute-start | bytes 12296 | tf_op jit(solution)/shard_map/ppermute | solution.py:76
  55.4 1.8 %collective-permute-start.11 = (bf16[16,512]{1,0:T(8,128)(2,1)S(1)}, bf16[16,512]{1,0:T(8,128)(2,1)S(1)}, u32[]{:S(2)}, u32[]{:S(2)}) collective-permute-start(bf16[16,512]{1,0:T(8,128)(2,1)S(1)} %broadcast_select_fusion), channel_id=1, source_target_pairs={{0,24},{8,0},{16,8},{24,16},{1,25},{9,1},{17,9},{25,17},{2,26},{10... | collective-permute-start | bytes 49160 | tf_op jit(solution)/shard_map/ppermute | solution.py:76
  55.4 3.8 %collective-permute-start.10 = (bf16[16,512]{1,0:T(8,128)(2,1)S(1)}, bf16[16,512]{1,0:T(8,128)(2,1)S(1)}, u32[]{:S(2)}, u32[]{:S(2)}) collective-permute-start(bf16[16,512]{1,0:T(8,128)(2,1)S(1)} %broadcast_select_fusion), channel_id=1, source_target_pairs={{0,16},{8,24},{16,0},{24,8},{1,17},{9,25},{17,1},{25,9},{2,18},{10... | collective-permute-start | bytes 49160 | tf_op jit(solution)/shard_map/ppermute | solution.py:76
  56.9 3.2 %collective-permute-start.9 = (bf16[16,512]{1,0:T(8,128)(2,1)S(1)}, bf16[16,512]{1,0:T(8,128)(2,1)S(1)}, u32[]{:S(2)}, u32[]{:S(2)}) collective-permute-start(bf16[16,512]{1,0:T(8,128)(2,1)S(1)} %broadcast_select_fusion), channel_id=1, source_target_pairs={{0,8},{8,16},{16,24},{24,0},{1,9},{9,17},{17,25},{25,1},{2,10},{10... | collective-permute-start | bytes 49160 | tf_op jit(solution)/shard_map/ppermute | solution.py:76
  61.4 8.6 %copy-start = (f32[16,7168]{1,0:T(8,128)S(1)}, f32[16,7168]{1,0:T(8,128)}, u32[]{:S(2)}) copy-start(f32[16,7168]{1,0:T(8,128)} %param.9) | copy-start | bytes 1376260
  61.4 8.6 %copy-start.1 = (f32[16,7168]{1,0:T(8,128)S(1)}, f32[16,7168]{1,0:T(8,128)}, u32[]{:S(2)}) copy-start(f32[16,7168]{1,0:T(8,128)} %param.8) | copy-start | bytes 1376260
  61.4 4.9 %collective-permute-start.14 = (bf16[16,1792]{1,0:T(8,128)(2,1)S(1)}, bf16[16,1792]{1,0:T(8,128)(2,1)S(1)}, u32[]{:S(2)}, u32[]{:S(2)}) collective-permute-start(bf16[16,1792]{1,0:T(8,128)(2,1)S(1)} %get-tuple-element.11), channel_id=1, source_target_pairs={{0,6},{2,0},{4,2},{6,4},{1,7},{3,1},{5,3},{7,5},{8,14},{10,8},{12,... | collective-permute-start | bytes 172040 | tf_op jit(solution)/shard_map/ppermute | solution.py:76
  63.2 5.5 %collective-permute-start.13 = (bf16[16,1792]{1,0:T(8,128)(2,1)S(1)}, bf16[16,1792]{1,0:T(8,128)(2,1)S(1)}, u32[]{:S(2)}, u32[]{:S(2)}) collective-permute-start(bf16[16,1792]{1,0:T(8,128)(2,1)S(1)} %get-tuple-element.12), channel_id=1, source_target_pairs={{0,4},{2,6},{4,0},{6,2},{1,5},{3,7},{5,1},{7,3},{8,12},{10,14},{12... | collective-permute-start | bytes 172040 | tf_op jit(solution)/shard_map/ppermute | solution.py:76
  63.2 6.1 %collective-permute-start.12 = (bf16[16,1792]{1,0:T(8,128)(2,1)S(1)}, bf16[16,1792]{1,0:T(8,128)(2,1)S(1)}, u32[]{:S(2)}, u32[]{:S(2)}) collective-permute-start(bf16[16,1792]{1,0:T(8,128)(2,1)S(1)} %get-tuple-element.13), channel_id=1, source_target_pairs={{0,2},{2,4},{4,6},{6,0},{1,3},{3,5},{5,7},{7,1},{8,10},{10,12},{12... | collective-permute-start | bytes 172040 | tf_op jit(solution)/shard_map/ppermute | solution.py:76

commit v7 on v6

--- a/solution.py
+++ b/solution.py
@@ -78,8 +78,7 @@
 
 
 def by_source(got, index, size):
-    order = (index - jnp.arange(size, dtype=jnp.int32)) % size
-    return jnp.take(jnp.stack(got), order, axis=0)
+    return jnp.stack([lax.select_n((index - p) % size, *got) for p in range(size)])
 
 
 def exchange_sum(value, axes):

time: 71.5 us -> 69.7 us (0.975)
  local copies, waits for them, and re-layouts: 3.93 us -> 2.06 us
    gather x5 -> x0, local copies, waits for them, and re-layouts: 1.72 us -> none  [by_source(): return jnp.take(jnp.stack(got), order, axis=0)]
  transfers between devices with their start and end apart: 16 -> 16, of which waited for: 12 -> 13; matrix products, arithmetic and copies ran while one was open for 27% -> 27% of each run, Pallas kernels for 0% -> 0%
where the time goes in v7:
time: 69.7 us; the launch traced here: 69.5 us
  waiting for transfers between devices  20.8 us (30%)
  other arithmetic  20.7 us (30%)
  starting transfers between devices  20.6 us (30%)
  between operations  2.86 us (4%)
  matrix products  2.41 us (3%)
  local copies, waits for them, and re-layouts  2.06 us (3%)
    convert_element_type x1, other arithmetic, projection_block(): return (gauss * rank ** (-0.5)).astype(jnp.bfloat16)  18.2 us
    ppermute x15, waiting for transfers between devices, shifted(): got.append(lax.ppermute(value_of(k), axis, pairs))  18.1 us
    ppermute x15, starting transfers between devices, shifted(): got.append(lax.ppermute(value_of(k), axis, pairs))  14.3 us
    all_to_all x1, starting transfers between devices, per_device(): held = lax.all_to_all(pieces, 'replica', 0, 0, tiled=True)  6.35 us
    all_to_all x1, waiting for transfers between devices, per_device(): held = lax.all_to_all(pieces, 'replica', 0, 0, tiled=True)  2.75 us
    dot_general x4, matrix products, per_device(): term = jnp.dot(held[r], projection, preferred_element_type=jnp.float32)  1.73 us
  transfers between devices with their start and end apart: 16, of which 13 were waited for; matrix products, arithmetic and copies ran while one was open for 27% of the time, Pallas kernels for 0%

profile of v7, /device:TPU:0, one launch (start us, length us, event | category | flops | bytes accessed | tf_op | source)
XLA Modules:
  0.0 69.5 jit_solution(6241637880655681980)
XLA Ops:
  0.6 1.3 %slice_bitcast_fusion.11 = (bf16[1,64,1792]{2,1,0:T(8,128)(2,1)S(1)}, bf16[1,64,1792]{2,1,0:T(8,128)(2,1)S(1)}, bf16[1,64,1792]{2,1,0:T(8,128)(2,1)S(1)}, bf16[1,64,1792]{2,1,0:T(8,128)(2,1)S(1)}) fusion(bf16[64,7168]{1,0:T(8,128)(2,1)} %bitcast.112), kind=kLoop, calls=%fused_computation.45 | loop fusion | bytes 1835008 | tf_op jit(solution)/shard_map/stack | solution.py:117
  2.0 1.1 %pad_maximum_fusion = bf16[4,64,1792]{2,1,0:T(8,128)(2,1)} fusion(bf16[1,64,1792]{2,1,0:T(8,128)(2,1)S(1)} %get-tuple-element.7, bf16[1,64,1792]{2,1,0:T(8,128)(2,1)S(1)} %get-tuple-element.8, bf16[1,64,1792]{2,1,0:T(8,128)(2,1)S(1)} %get-tuple-element.9, bf16[1,64,1792]{2,1,0:T(8,128)(2,1)S(1)} %get-tuple-element.6), kind=kLoop, calls=%fused_computation.31 | loop fusion | flops 1376256 | bytes 1835008 | tf_op jit(solution)/shard_map/stack | solution.py:117
  3.1 6.3 %all-to-all-start = ((bf16[4,64,1792]{2,1,0:T(8,128)(2,1)}), bf16[4,64,1792]{2,1,0:T(8,128)(2,1)S(1)}, u32[]{:S(2)}, u32[]{:S(2)}) async-start(bf16[4,64,1792]{2,1,0:T(8,128)(2,1)} %pad_maximum_fusion), calls=%async_computation | async-start | bytes 1835008 | tf_op jit(solution)/shard_map/all_to_all | solution.py:118
  9.4 0.6 fusion.48
  11.3 18.2 %fusion.18 = bf16[1792,512]{1,0:T(8,128)(2,1)S(1)} fusion(s32[]{:T(128)} %bitcast.6, s32[1792]{0:T(1024)S(1)} %add_multiply_fusion), kind=kLoop, calls=%fused_computation.24 | loop fusion | flops 32112640 | bytes 1842180 | tf_op jit(solution)/shard_map/convert_element_type | solution.py:37
  29.6 2.8 %all-to-all-done = bf16[4,64,1792]{2,1,0:T(8,128)(2,1)S(1)} async-done(((bf16[4,64,1792]{2,1,0:T(8,128)(2,1)}), bf16[4,64,1792]{2,1,0:T(8,128)(2,1)S(1)}, u32[]{:S(2)}, u32[]{:S(2)}) %all-to-all-start) | async-done | bytes 917536 | tf_op jit(solution)/shard_map/all_to_all | solution.py:118
  32.3 0.4 fusion.22
  32.8 0.4 convolution_add_fusion.2
  33.2 0.4 convolution_add_fusion.1
  33.6 0.4 fusion.20
  34.2 1.7 %collective-permute-start.2 = (f32[16,512]{1,0:T(8,128)S(1)}, f32[16,512]{1,0:T(8,128)S(1)}, u32[]{:S(2)}, u32[]{:S(2)}) collective-permute-start(f32[16,512]{1,0:T(8,128)S(1)} %get-tuple-element.18), channel_id=1, source_target_pairs={{0,24},{8,0},{16,8},{24,16},{1,25},{9,1},{17,9},{25,17},{2,26},{10... | collective-permute-start | bytes 98312 | tf_op jit(solution)/shard_map/ppermute | solution.py:76
  35.9 1.5 %collective-permute-start.1 = (f32[16,512]{1,0:T(8,128)S(1)}, f32[16,512]{1,0:T(8,128)S(1)}, u32[]{:S(2)}, u32[]{:S(2)}) collective-permute-start(f32[16,512]{1,0:T(8,128)S(1)} %get-tuple-element.19), channel_id=1, source_target_pairs={{0,16},{8,24},{16,0},{24,8},{1,17},{9,25},{17,1},{25,9},{2,18},{10... | collective-permute-start | bytes 98312 | tf_op jit(solution)/shard_map/ppermute | solution.py:76
  37.5 2.3 %collective-permute-done.1 = f32[16,512]{1,0:T(8,128)S(1)} collective-permute-done((f32[16,512]{1,0:T(8,128)S(1)}, f32[16,512]{1,0:T(8,128)S(1)}, u32[]{:S(2)}, u32[]{:S(2)}) %collective-permute-start.1) | collective-permute-done | bytes 32800 | tf_op jit(solution)/shard_map/ppermute | solution.py:76
  39.9 3.8 %collective-permute-start.5 = (f32[4,512]{1,0:T(4,128)S(1)}, f32[4,512]{1,0:T(4,128)S(1)}, u32[]{:S(2)}, u32[]{:S(2)}) collective-permute-start(f32[4,512]{1,0:T(4,128)S(1)} %get-tuple-element.25), channel_id=1, source_target_pairs={{0,6},{2,0},{4,2},{6,4},{1,7},{3,1},{5,3},{7,5},{8,14},{10,8},{12,... | collective-permute-start | bytes 24584 | tf_op jit(solution)/shard_map/ppermute | solution.py:76
  43.8 1.6 %collective-permute-done.3 = f32[4,512]{1,0:T(4,128)S(1)} collective-permute-done((f32[4,512]{1,0:T(4,128)S(1)}, f32[4,512]{1,0:T(4,128)S(1)}, u32[]{:S(2)}, u32[]{:S(2)}) %collective-permute-start.3) | collective-permute-done | bytes 8224 | tf_op jit(solution)/shard_map/ppermute | solution.py:76
  45.4 2.9 %collective-permute-done.4 = f32[4,512]{1,0:T(4,128)S(1)} collective-permute-done((f32[4,512]{1,0:T(4,128)S(1)}, f32[4,512]{1,0:T(4,128)S(1)}, u32[]{:S(2)}, u32[]{:S(2)}) %collective-permute-start.4) | collective-permute-done | bytes 8224 | tf_op jit(solution)/shard_map/ppermute | solution.py:76
  48.3 1.0 %collective-permute-start.8 = (bf16[4,512]{1,0:T(4,128)(2,1)S(1)}, bf16[4,512]{1,0:T(4,128)(2,1)S(1)}, u32[]{:S(2)}, u32[]{:S(2)}) collective-permute-start(bf16[4,512]{1,0:T(4,128)(2,1)S(1)} %fusion.45), channel_id=1, source_target_pairs={{0,6},{2,0},{4,2},{6,4},{1,7},{3,1},{5,3},{7,5},{8,14},{10,8},{12,... | collective-permute-start | bytes 12296 | tf_op jit(solution)/shard_map/ppermute | solution.py:76
  49.3 1.2 %collective-permute-start.6 = (bf16[4,512]{1,0:T(4,128)(2,1)S(1)}, bf16[4,512]{1,0:T(4,128)(2,1)S(1)}, u32[]{:S(2)}, u32[]{:S(2)}) collective-permute-start(bf16[4,512]{1,0:T(4,128)(2,1)S(1)} %fusion.45), channel_id=1, source_target_pairs={{0,2},{2,4},{4,6},{6,0},{1,3},{3,5},{5,7},{7,1},{8,10},{10,12},{12... | collective-permute-start | bytes 12296 | tf_op jit(solution)/shard_map/ppermute | solution.py:76
  50.5 1.5 %collective-permute-done.8 = bf16[4,512]{1,0:T(4,128)(2,1)S(1)} collective-permute-done((bf16[4,512]{1,0:T(4,128)(2,1)S(1)}, bf16[4,512]{1,0:T(4,128)(2,1)S(1)}, u32[]{:S(2)}, u32[]{:S(2)}) %collective-permute-start.8) | collective-permute-done | bytes 4128 | tf_op jit(solution)/shard_map/ppermute | solution.py:76
  52.0 1.8 %collective-permute-done.7 = bf16[4,512]{1,0:T(4,128)(2,1)S(1)} collective-permute-done((bf16[4,512]{1,0:T(4,128)(2,1)S(1)}, bf16[4,512]{1,0:T(4,128)(2,1)S(1)}, u32[]{:S(2)}, u32[]{:S(2)}) %collective-permute-start.7) | collective-permute-done | bytes 4128 | tf_op jit(solution)/shard_map/ppermute | solution.py:76
  53.8 0.9 %collective-permute-done.6 = bf16[4,512]{1,0:T(4,128)(2,1)S(1)} collective-permute-done((bf16[4,512]{1,0:T(4,128)(2,1)S(1)}, bf16[4,512]{1,0:T(4,128)(2,1)S(1)}, u32[]{:S(2)}, u32[]{:S(2)}) %collective-permute-start.6) | collective-permute-done | bytes 4128 | tf_op jit(solution)/shard_map/ppermute | solution.py:76
  54.8 1.6 %collective-permute-start.10 = (bf16[16,512]{1,0:T(8,128)(2,1)S(1)}, bf16[16,512]{1,0:T(8,128)(2,1)S(1)}, u32[]{:S(2)}, u32[]{:S(2)}) collective-permute-start(bf16[16,512]{1,0:T(8,128)(2,1)S(1)} %reshape.35), channel_id=1, source_target_pairs={{0,16},{8,24},{16,0},{24,8},{1,17},{9,25},{17,1},{25,9},{2,18},{10... | collective-permute-start | bytes 49160 | tf_op jit(solution)/shard_map/ppermute | solution.py:76
  56.4 0.2 collective-permute-start.9
  56.5 2.1 %collective-permute-done.10 = bf16[16,512]{1,0:T(8,128)(2,1)S(1)} collective-permute-done((bf16[16,512]{1,0:T(8,128)(2,1)S(1)}, bf16[16,512]{1,0:T(8,128)(2,1)S(1)}, u32[]{:S(2)}, u32[]{:S(2)}) %collective-permute-start.10) | collective-permute-done | bytes 16416 | tf_op jit(solution)/shard_map/ppermute | solution.py:76
  58.6 0.9 %collective-permute-done.9 = bf16[16,512]{1,0:T(8,128)(2,1)S(1)} collective-permute-done((bf16[16,512]{1,0:T(8,128)(2,1)S(1)}, bf16[16,512]{1,0:T(8,128)(2,1)S(1)}, u32[]{:S(2)}, u32[]{:S(2)}) %collective-permute-start.9) | collective-permute-done | bytes 16416 | tf_op jit(solution)/shard_map/ppermute | solution.py:76
  59.6 0.7 convolution_convert_fusion
  60.3 1.7 %collective-permute-start.14 = (bf16[16,1792]{1,0:T(8,128)(2,1)S(1)}, bf16[16,1792]{1,0:T(8,128)(2,1)S(1)}, u32[]{:S(2)}, u32[]{:S(2)}) collective-permute-start(bf16[16,1792]{1,0:T(8,128)(2,1)S(1)} %get-tuple-element.14), channel_id=1, source_target_pairs={{0,6},{2,0},{4,2},{6,4},{1,7},{3,1},{5,3},{7,5},{8,14},{10,8},{12,... | collective-permute-start | bytes 172040 | tf_op jit(solution)/shard_map/ppermute | solution.py:76
  62.0 1.5 %collective-permute-start.12 = (bf16[16,1792]{1,0:T(8,128)(2,1)S(1)}, bf16[16,1792]{1,0:T(8,128)(2,1)S(1)}, u32[]{:S(2)}, u32[]{:S(2)}) collective-permute-start(bf16[16,1792]{1,0:T(8,128)(2,1)S(1)} %get-tuple-element.16), channel_id=1, source_target_pairs={{0,2},{2,4},{4,6},{6,0},{1,3},{3,5},{5,7},{7,1},{8,10},{10,12},{12... | collective-permute-start | bytes 172040 | tf_op jit(solution)/shard_map/ppermute | solution.py:76
  64.2 0.9 %collective-permute-done.14 = bf16[16,1792]{1,0:T(8,128)(2,1)S(1)} collective-permute-done((bf16[16,1792]{1,0:T(8,128)(2,1)S(1)}, bf16[16,1792]{1,0:T(8,128)(2,1)S(1)}, u32[]{:S(2)}, u32[]{:S(2)}) %collective-permute-start.14) | collective-permute-done | bytes 57376 | tf_op jit(solution)/shard_map/ppermute | solution.py:76
  65.1 2.4 %collective-permute-done.13 = bf16[16,1792]{1,0:T(8,128)(2,1)S(1)} collective-permute-done((bf16[16,1792]{1,0:T(8,128)(2,1)S(1)}, bf16[16,1792]{1,0:T(8,128)(2,1)S(1)}, u32[]{:S(2)}, u32[]{:S(2)}) %collective-permute-start.13) | collective-permute-done | bytes 57376 | tf_op jit(solution)/shard_map/ppermute | solution.py:76
  67.5 0.6 collective-permute-done.12
  68.2 1.2 %multiply_divide_fusion = (f32[16,7168]{1,0:T(8,128)}, f32[16,7168]{1,0:T(8,128)}, f32[16,7168]{1,0:T(8,128)}) fusion(f32[]{:T(128)} %bitcast.38, f32[]{:T(128)} %bitcast.37, f32[16,7168]{1,0:T(8,128)S(1)} %bitcast.111, f32[16,7168]{1,0:T(8,128)S(1)} %copy-done, f32[16,7168]{1,0:T(8,128)S(1)} %copy-done.1), kind=kLoop, calls=%fused_computation.35 | loop fusion | flops 1261568 | bytes 2752520 | tf_op jit(solution)/shard_map/div | solution.py:46
  (30 shorter events, 0.6 us)
Async XLA Ops:
  2.0 7.4 %copy-start.2 = (s32[2]{0:T(128)S(1)}, s32[2]{0:T(128)}, u32[]{:S(2)}) copy-start(s32[2]{0:T(128)} %param.6) | copy-start | bytes 28
  3.1 29.3 %all-to-all-start = ((bf16[4,64,1792]{2,1,0:T(8,128)(2,1)}), bf16[4,64,1792]{2,1,0:T(8,128)(2,1)S(1)}, u32[]{:S(2)}, u32[]{:S(2)}) async-start(bf16[4,64,1792]{2,1,0:T(8,128)(2,1)} %pad_maximum_fusion), calls=%async_computation | async-start | bytes 1835008 | tf_op jit(solution)/shard_map/all_to_all | solution.py:118
  34.1 3.4 %collective-permute-start = (f32[16,512]{1,0:T(8,128)S(1)}, f32[16,512]{1,0:T(8,128)S(1)}, u32[]{:S(2)}, u32[]{:S(2)}) collective-permute-start(f32[16,512]{1,0:T(8,128)S(1)} %get-tuple-element.17), channel_id=1, source_target_pairs={{0,8},{8,16},{16,24},{24,0},{1,9},{9,17},{17,25},{25,1},{2,10},{10... | collective-permute-start | bytes 98312 | tf_op jit(solution)/shard_map/ppermute | solution.py:76
  34.2 3.3 %collective-permute-start.2 = (f32[16,512]{1,0:T(8,128)S(1)}, f32[16,512]{1,0:T(8,128)S(1)}, u32[]{:S(2)}, u32[]{:S(2)}) collective-permute-start(f32[16,512]{1,0:T(8,128)S(1)} %get-tuple-element.18), channel_id=1, source_target_pairs={{0,24},{8,0},{16,8},{24,16},{1,25},{9,1},{17,9},{25,17},{2,26},{10... | collective-permute-start | bytes 98312 | tf_op jit(solution)/shard_map/ppermute | solution.py:76
  35.9 3.9 %collective-permute-start.1 = (f32[16,512]{1,0:T(8,128)S(1)}, f32[16,512]{1,0:T(8,128)S(1)}, u32[]{:S(2)}, u32[]{:S(2)}) collective-permute-start(f32[16,512]{1,0:T(8,128)S(1)} %get-tuple-element.19), channel_id=1, source_target_pairs={{0,16},{8,24},{16,0},{24,8},{1,17},{9,25},{17,1},{25,9},{2,18},{10... | collective-permute-start | bytes 98312 | tf_op jit(solution)/shard_map/ppermute | solution.py:76
  39.9 5.5 %collective-permute-start.3 = (f32[4,512]{1,0:T(4,128)S(1)}, f32[4,512]{1,0:T(4,128)S(1)}, u32[]{:S(2)}, u32[]{:S(2)}) collective-permute-start(f32[4,512]{1,0:T(4,128)S(1)} %get-tuple-element.24), channel_id=1, source_target_pairs={{0,2},{2,4},{4,6},{6,0},{1,3},{3,5},{5,7},{7,1},{8,10},{10,12},{12... | collective-permute-start | bytes 24584 | tf_op jit(solution)/shard_map/ppermute | solution.py:76
  39.9 5.4 %collective-permute-start.5 = (f32[4,512]{1,0:T(4,128)S(1)}, f32[4,512]{1,0:T(4,128)S(1)}, u32[]{:S(2)}, u32[]{:S(2)}) collective-permute-start(f32[4,512]{1,0:T(4,128)S(1)} %get-tuple-element.25), channel_id=1, source_target_pairs={{0,6},{2,0},{4,2},{6,4},{1,7},{3,1},{5,3},{7,5},{8,14},{10,8},{12,... | collective-permute-start | bytes 24584 | tf_op jit(solution)/shard_map/ppermute | solution.py:76
  43.7 4.5 %collective-permute-start.4 = (f32[4,512]{1,0:T(4,128)S(1)}, f32[4,512]{1,0:T(4,128)S(1)}, u32[]{:S(2)}, u32[]{:S(2)}) collective-permute-start(f32[4,512]{1,0:T(4,128)S(1)} %get-tuple-element.26), channel_id=1, source_target_pairs={{0,4},{2,6},{4,0},{6,2},{1,5},{3,7},{5,1},{7,3},{8,12},{10,14},{12... | collective-permute-start | bytes 24584 | tf_op jit(solution)/shard_map/ppermute | solution.py:76
  48.3 3.7 %collective-permute-start.8 = (bf16[4,512]{1,0:T(4,128)(2,1)S(1)}, bf16[4,512]{1,0:T(4,128)(2,1)S(1)}, u32[]{:S(2)}, u32[]{:S(2)}) collective-permute-start(bf16[4,512]{1,0:T(4,128)(2,1)S(1)} %fusion.45), channel_id=1, source_target_pairs={{0,6},{2,0},{4,2},{6,4},{1,7},{3,1},{5,3},{7,5},{8,14},{10,8},{12,... | collective-permute-start | bytes 12296 | tf_op jit(solution)/shard_map/ppermute | solution.py:76
  49.3 4.5 %collective-permute-start.7 = (bf16[4,512]{1,0:T(4,128)(2,1)S(1)}, bf16[4,512]{1,0:T(4,128)(2,1)S(1)}, u32[]{:S(2)}, u32[]{:S(2)}) collective-permute-start(bf16[4,512]{1,0:T(4,128)(2,1)S(1)} %fusion.45), channel_id=1, source_target_pairs={{0,4},{2,6},{4,0},{6,2},{1,5},{3,7},{5,1},{7,3},{8,12},{10,14},{12... | collective-permute-start | bytes 12296 | tf_op jit(solution)/shard_map/ppermute | solution.py:76
  49.3 5.4 %collective-permute-start.6 = (bf16[4,512]{1,0:T(4,128)(2,1)S(1)}, bf16[4,512]{1,0:T(4,128)(2,1)S(1)}, u32[]{:S(2)}, u32[]{:S(2)}) collective-permute-start(bf16[4,512]{1,0:T(4,128)(2,1)S(1)} %fusion.45), channel_id=1, source_target_pairs={{0,2},{2,4},{4,6},{6,0},{1,3},{3,5},{5,7},{7,1},{8,10},{10,12},{12... | collective-permute-start | bytes 12296 | tf_op jit(solution)/shard_map/ppermute | solution.py:76
  54.7 1.8 %collective-permute-start.11 = (bf16[16,512]{1,0:T(8,128)(2,1)S(1)}, bf16[16,512]{1,0:T(8,128)(2,1)S(1)}, u32[]{:S(2)}, u32[]{:S(2)}) collective-permute-start(bf16[16,512]{1,0:T(8,128)(2,1)S(1)} %reshape.35), channel_id=1, source_target_pairs={{0,24},{8,0},{16,8},{24,16},{1,25},{9,1},{17,9},{25,17},{2,26},{10... | collective-permute-start | bytes 49160 | tf_op jit(solution)/shard_map/ppermute | solution.py:76
  54.8 3.8 %collective-permute-start.10 = (bf16[16,512]{1,0:T(8,128)(2,1)S(1)}, bf16[16,512]{1,0:T(8,128)(2,1)S(1)}, u32[]{:S(2)}, u32[]{:S(2)}) collective-permute-start(bf16[16,512]{1,0:T(8,128)(2,1)S(1)} %reshape.35), channel_id=1, source_target_pairs={{0,16},{8,24},{16,0},{24,8},{1,17},{9,25},{17,1},{25,9},{2,18},{10... | collective-permute-start | bytes 49160 | tf_op jit(solution)/shard_map/ppermute | solution.py:76
  56.4 3.2 %collective-permute-start.9 = (bf16[16,512]{1,0:T(8,128)(2,1)S(1)}, bf16[16,512]{1,0:T(8,128)(2,1)S(1)}, u32[]{:S(2)}, u32[]{:S(2)}) collective-permute-start(bf16[16,512]{1,0:T(8,128)(2,1)S(1)} %reshape.35), channel_id=1, source_target_pairs={{0,8},{8,16},{16,24},{24,0},{1,9},{9,17},{17,25},{25,1},{2,10},{10... | collective-permute-start | bytes 49160 | tf_op jit(solution)/shard_map/ppermute | solution.py:76
  59.5 8.7 %copy-start = (f32[16,7168]{1,0:T(8,128)S(1)}, f32[16,7168]{1,0:T(8,128)}, u32[]{:S(2)}) copy-start(f32[16,7168]{1,0:T(8,128)} %param.9) | copy-start | bytes 1376260
  59.6 8.7 %copy-start.1 = (f32[16,7168]{1,0:T(8,128)S(1)}, f32[16,7168]{1,0:T(8,128)}, u32[]{:S(2)}) copy-start(f32[16,7168]{1,0:T(8,128)} %param.8) | copy-start | bytes 1376260
  60.3 4.9 %collective-permute-start.14 = (bf16[16,1792]{1,0:T(8,128)(2,1)S(1)}, bf16[16,1792]{1,0:T(8,128)(2,1)S(1)}, u32[]{:S(2)}, u32[]{:S(2)}) collective-permute-start(bf16[16,1792]{1,0:T(8,128)(2,1)S(1)} %get-tuple-element.14), channel_id=1, source_target_pairs={{0,6},{2,0},{4,2},{6,4},{1,7},{3,1},{5,3},{7,5},{8,14},{10,8},{12,... | collective-permute-start | bytes 172040 | tf_op jit(solution)/shard_map/ppermute | solution.py:76
  62.0 5.5 %collective-permute-start.13 = (bf16[16,1792]{1,0:T(8,128)(2,1)S(1)}, bf16[16,1792]{1,0:T(8,128)(2,1)S(1)}, u32[]{:S(2)}, u32[]{:S(2)}) collective-permute-start(bf16[16,1792]{1,0:T(8,128)(2,1)S(1)} %get-tuple-element.15), channel_id=1, source_target_pairs={{0,4},{2,6},{4,0},{6,2},{1,5},{3,7},{5,1},{7,3},{8,12},{10,14},{12... | collective-permute-start | bytes 172040 | tf_op jit(solution)/shard_map/ppermute | solution.py:76
  62.0 6.1 %collective-permute-start.12 = (bf16[16,1792]{1,0:T(8,128)(2,1)S(1)}, bf16[16,1792]{1,0:T(8,128)(2,1)S(1)}, u32[]{:S(2)}, u32[]{:S(2)}) collective-permute-start(bf16[16,1792]{1,0:T(8,128)(2,1)S(1)} %get-tuple-element.16), channel_id=1, source_target_pairs={{0,2},{2,4},{4,6},{6,0},{1,3},{3,5},{5,7},{7,1},{8,10},{10,12},{12... | collective-permute-start | bytes 172040 | tf_op jit(solution)/shard_map/ppermute | solution.py:76

commit v8 on v7

--- a/solution.py
+++ b/solution.py
@@ -117,10 +117,12 @@
     pieces = jnp.stack([gradient[:, i * width : (i + 1) * width] for i in range(n_rep)])
     held = lax.all_to_all(pieces, "replica", 0, 0, tiled=True)
 
-    partial_value = None
-    for r in range(n_rep):
-        term = jnp.dot(held[r], projection, preferred_element_type=jnp.float32)
-        partial_value = term if partial_value is None else partial_value + term
+    terms = jnp.dot(
+        held.reshape(n_rep * rows, width), projection, preferred_element_type=jnp.float32
+    ).reshape(n_rep, rows, RANK)
+    partial_value = terms[0]
+    for r in range(1, n_rep):
+        partial_value = partial_value + terms[r]
     partial_value = partial_value * (1.0 / n_rep)
     sketch = exchange_sum(partial_value, ("tensor", "replica"))
     sketch_rounded = sketch.astype(jnp.bfloat16)

time: 69.7 us -> 68.6 us (0.984)
  matrix products: 2.41 us -> 1.31 us
    dot_general x4 -> x1, matrix products: 1.73 us -> 0.63 us  [per_device(): jnp.dot(held.reshape(n_rep * rows, width), projection, preferred_element_...]
  transfers between devices with their start and end apart: 16 -> 16, of which waited for: 13 -> 13; matrix products, arithmetic and copies ran while one was open for 27% -> 28% of each run, Pallas kernels for 0% -> 0%
where the time goes in v8:
time: 68.6 us; the launch traced here: 68.4 us
  waiting for transfers between devices  20.8 us (30%)
  other arithmetic  20.7 us (30%)
  starting transfers between devices  20.6 us (30%)
  between operations  2.86 us (4%)
  local copies, waits for them, and re-layouts  2.06 us (3%)
  matrix products  1.31 us (2%)
    convert_element_type x1, other arithmetic, projection_block(): return (gauss * rank ** (-0.5)).astype(jnp.bfloat16)  18.2 us
    ppermute x15, waiting for transfers between devices, shifted(): got.append(lax.ppermute(value_of(k), axis, pairs))  18.1 us
    ppermute x15, starting transfers between devices, shifted(): got.append(lax.ppermute(value_of(k), axis, pairs))  14.3 us
    all_to_all x1, starting transfers between devices, per_device(): held = lax.all_to_all(pieces, 'replica', 0, 0, tiled=True)  6.35 us
    all_to_all x1, waiting for transfers between devices, per_device(): held = lax.all_to_all(pieces, 'replica', 0, 0, tiled=True)  2.75 us
  transfers between devices with their start and end apart: 16, of which 13 were waited for; matrix products, arithmetic and copies ran while one was open for 28% of the time, Pallas kernels for 0%

profile of v8, /device:TPU:0, one launch (start us, length us, event | category | flops | bytes accessed | tf_op | source)
XLA Modules:
  0.0 68.4 jit_solution(912939037480880983)
XLA Ops:
  0.6 1.3 %slice_bitcast_fusion.3 = (bf16[1,64,1792]{2,1,0:T(8,128)(2,1)S(1)}, bf16[1,64,1792]{2,1,0:T(8,128)(2,1)S(1)}, bf16[1,64,1792]{2,1,0:T(8,128)(2,1)S(1)}, bf16[1,64,1792]{2,1,0:T(8,128)(2,1)S(1)}) fusion(bf16[64,7168]{1,0:T(8,128)(2,1)} %bitcast.100), kind=kLoop, calls=%fused_computation.36 | loop fusion | bytes 1835008 | tf_op jit(solution)/shard_map/stack | solution.py:117
  2.0 1.1 %pad_maximum_fusion = bf16[4,64,1792]{2,1,0:T(8,128)(2,1)} fusion(bf16[1,64,1792]{2,1,0:T(8,128)(2,1)S(1)} %get-tuple-element.7, bf16[1,64,1792]{2,1,0:T(8,128)(2,1)S(1)} %get-tuple-element.8, bf16[1,64,1792]{2,1,0:T(8,128)(2,1)S(1)} %get-tuple-element.9, bf16[1,64,1792]{2,1,0:T(8,128)(2,1)S(1)} %get-tuple-element.6), kind=kLoop, calls=%fused_computation.27 | loop fusion | flops 1376256 | bytes 1835008 | tf_op jit(solution)/shard_map/stack | solution.py:117
  3.1 6.3 %all-to-all-start = ((bf16[4,64,1792]{2,1,0:T(8,128)(2,1)}), bf16[4,64,1792]{2,1,0:T(8,128)(2,1)S(1)}, u32[]{:S(2)}, u32[]{:S(2)}) async-start(bf16[4,64,1792]{2,1,0:T(8,128)(2,1)} %pad_maximum_fusion), calls=%async_computation | async-start | bytes 1835008 | tf_op jit(solution)/shard_map/all_to_all | solution.py:118
  9.4 0.6 fusion.47
  11.3 18.2 %fusion.18 = bf16[1792,512]{1,0:T(8,128)(2,1)S(1)} fusion(s32[]{:T(128)} %bitcast.6, s32[1792]{0:T(1024)S(1)} %add_multiply_fusion), kind=kLoop, calls=%fused_computation.24 | loop fusion | flops 32112640 | bytes 1842180 | tf_op jit(solution)/shard_map/convert_element_type | solution.py:37
  29.6 2.8 %all-to-all-done = bf16[4,64,1792]{2,1,0:T(8,128)(2,1)S(1)} async-done(((bf16[4,64,1792]{2,1,0:T(8,128)(2,1)}), bf16[4,64,1792]{2,1,0:T(8,128)(2,1)S(1)}, u32[]{:S(2)}, u32[]{:S(2)}) %all-to-all-start) | async-done | bytes 917536 | tf_op jit(solution)/shard_map/all_to_all | solution.py:118
  32.3 0.6 fusion.48
  33.1 1.7 %collective-permute-start.2 = (f32[16,512]{1,0:T(8,128)S(1)}, f32[16,512]{1,0:T(8,128)S(1)}, u32[]{:S(2)}, u32[]{:S(2)}) collective-permute-start(f32[16,512]{1,0:T(8,128)S(1)} %get-tuple-element.18), channel_id=1, source_target_pairs={{0,24},{8,0},{16,8},{24,16},{1,25},{9,1},{17,9},{25,17},{2,26},{10... | collective-permute-start | bytes 98312 | tf_op jit(solution)/shard_map/ppermute | solution.py:76
  34.8 1.5 %collective-permute-start.1 = (f32[16,512]{1,0:T(8,128)S(1)}, f32[16,512]{1,0:T(8,128)S(1)}, u32[]{:S(2)}, u32[]{:S(2)}) collective-permute-start(f32[16,512]{1,0:T(8,128)S(1)} %get-tuple-element.19), channel_id=1, source_target_pairs={{0,16},{8,24},{16,0},{24,8},{1,17},{9,25},{17,1},{25,9},{2,18},{10... | collective-permute-start | bytes 98312 | tf_op jit(solution)/shard_map/ppermute | solution.py:76
  36.3 0.1 collective-permute-done
  36.4 2.3 %collective-permute-done.1 = f32[16,512]{1,0:T(8,128)S(1)} collective-permute-done((f32[16,512]{1,0:T(8,128)S(1)}, f32[16,512]{1,0:T(8,128)S(1)}, u32[]{:S(2)}, u32[]{:S(2)}) %collective-permute-start.1) | collective-permute-done | bytes 32800 | tf_op jit(solution)/shard_map/ppermute | solution.py:76
  38.8 0.1 collective-permute-start.3
  38.9 3.8 %collective-permute-start.5 = (f32[4,512]{1,0:T(4,128)S(1)}, f32[4,512]{1,0:T(4,128)S(1)}, u32[]{:S(2)}, u32[]{:S(2)}) collective-permute-start(f32[4,512]{1,0:T(4,128)S(1)} %get-tuple-element.25), channel_id=1, source_target_pairs={{0,6},{2,0},{4,2},{6,4},{1,7},{3,1},{5,3},{7,5},{8,14},{10,8},{12,... | collective-permute-start | bytes 24584 | tf_op jit(solution)/shard_map/ppermute | solution.py:76
  42.7 1.6 %collective-permute-done.3 = f32[4,512]{1,0:T(4,128)S(1)} collective-permute-done((f32[4,512]{1,0:T(4,128)S(1)}, f32[4,512]{1,0:T(4,128)S(1)}, u32[]{:S(2)}, u32[]{:S(2)}) %collective-permute-start.3) | collective-permute-done | bytes 8224 | tf_op jit(solution)/shard_map/ppermute | solution.py:76
  44.3 2.9 %collective-permute-done.4 = f32[4,512]{1,0:T(4,128)S(1)} collective-permute-done((f32[4,512]{1,0:T(4,128)S(1)}, f32[4,512]{1,0:T(4,128)S(1)}, u32[]{:S(2)}, u32[]{:S(2)}) %collective-permute-start.4) | collective-permute-done | bytes 8224 | tf_op jit(solution)/shard_map/ppermute | solution.py:76
  47.2 1.0 %collective-permute-start.8 = (bf16[4,512]{1,0:T(4,128)(2,1)S(1)}, bf16[4,512]{1,0:T(4,128)(2,1)S(1)}, u32[]{:S(2)}, u32[]{:S(2)}) collective-permute-start(bf16[4,512]{1,0:T(4,128)(2,1)S(1)} %fusion.44), channel_id=1, source_target_pairs={{0,6},{2,0},{4,2},{6,4},{1,7},{3,1},{5,3},{7,5},{8,14},{10,8},{12,... | collective-permute-start | bytes 12296 | tf_op jit(solution)/shard_map/ppermute | solution.py:76
  48.2 1.2 %collective-permute-start.6 = (bf16[4,512]{1,0:T(4,128)(2,1)S(1)}, bf16[4,512]{1,0:T(4,128)(2,1)S(1)}, u32[]{:S(2)}, u32[]{:S(2)}) collective-permute-start(bf16[4,512]{1,0:T(4,128)(2,1)S(1)} %fusion.44), channel_id=1, source_target_pairs={{0,2},{2,4},{4,6},{6,0},{1,3},{3,5},{5,7},{7,1},{8,10},{10,12},{12... | collective-permute-start | bytes 12296 | tf_op jit(solution)/shard_map/ppermute | solution.py:76
  49.4 1.5 %collective-permute-done.8 = bf16[4,512]{1,0:T(4,128)(2,1)S(1)} collective-permute-done((bf16[4,512]{1,0:T(4,128)(2,1)S(1)}, bf16[4,512]{1,0:T(4,128)(2,1)S(1)}, u32[]{:S(2)}, u32[]{:S(2)}) %collective-permute-start.8) | collective-permute-done | bytes 4128 | tf_op jit(solution)/shard_map/ppermute | solution.py:76
  50.9 1.8 %collective-permute-done.7 = bf16[4,512]{1,0:T(4,128)(2,1)S(1)} collective-permute-done((bf16[4,512]{1,0:T(4,128)(2,1)S(1)}, bf16[4,512]{1,0:T(4,128)(2,1)S(1)}, u32[]{:S(2)}, u32[]{:S(2)}) %collective-permute-start.7) | collective-permute-done | bytes 4128 | tf_op jit(solution)/shard_map/ppermute | solution.py:76
  52.7 0.9 %collective-permute-done.6 = bf16[4,512]{1,0:T(4,128)(2,1)S(1)} collective-permute-done((bf16[4,512]{1,0:T(4,128)(2,1)S(1)}, bf16[4,512]{1,0:T(4,128)(2,1)S(1)}, u32[]{:S(2)}, u32[]{:S(2)}) %collective-permute-start.6) | collective-permute-done | bytes 4128 | tf_op jit(solution)/shard_map/ppermute | solution.py:76
  53.7 0.1 collective-permute-start.11
  53.7 1.6 %collective-permute-start.10 = (bf16[16,512]{1,0:T(8,128)(2,1)S(1)}, bf16[16,512]{1,0:T(8,128)(2,1)S(1)}, u32[]{:S(2)}, u32[]{:S(2)}) collective-permute-start(bf16[16,512]{1,0:T(8,128)(2,1)S(1)} %reshape.54), channel_id=1, source_target_pairs={{0,16},{8,24},{16,0},{24,8},{1,17},{9,25},{17,1},{25,9},{2,18},{10... | collective-permute-start | bytes 49160 | tf_op jit(solution)/shard_map/ppermute | solution.py:76
  55.3 0.2 collective-permute-start.9
  55.5 2.1 %collective-permute-done.10 = bf16[16,512]{1,0:T(8,128)(2,1)S(1)} collective-permute-done((bf16[16,512]{1,0:T(8,128)(2,1)S(1)}, bf16[16,512]{1,0:T(8,128)(2,1)S(1)}, u32[]{:S(2)}, u32[]{:S(2)}) %collective-permute-start.10) | collective-permute-done | bytes 16416 | tf_op jit(solution)/shard_map/ppermute | solution.py:76
  57.5 0.9 %collective-permute-done.9 = bf16[16,512]{1,0:T(8,128)(2,1)S(1)} collective-permute-done((bf16[16,512]{1,0:T(8,128)(2,1)S(1)}, bf16[16,512]{1,0:T(8,128)(2,1)S(1)}, u32[]{:S(2)}, u32[]{:S(2)}) %collective-permute-start.9) | collective-permute-done | bytes 16416 | tf_op jit(solution)/shard_map/ppermute | solution.py:76
  58.5 0.7 convolution_convert_fusion
  59.2 1.7 %collective-permute-start.14 = (bf16[16,1792]{1,0:T(8,128)(2,1)S(1)}, bf16[16,1792]{1,0:T(8,128)(2,1)S(1)}, u32[]{:S(2)}, u32[]{:S(2)}) collective-permute-start(bf16[16,1792]{1,0:T(8,128)(2,1)S(1)} %get-tuple-element.14), channel_id=1, source_target_pairs={{0,6},{2,0},{4,2},{6,4},{1,7},{3,1},{5,3},{7,5},{8,14},{10,8},{12,... | collective-permute-start | bytes 172040 | tf_op jit(solution)/shard_map/ppermute | solution.py:76
  61.0 1.5 %collective-permute-start.12 = (bf16[16,1792]{1,0:T(8,128)(2,1)S(1)}, bf16[16,1792]{1,0:T(8,128)(2,1)S(1)}, u32[]{:S(2)}, u32[]{:S(2)}) collective-permute-start(bf16[16,1792]{1,0:T(8,128)(2,1)S(1)} %get-tuple-element.16), channel_id=1, source_target_pairs={{0,2},{2,4},{4,6},{6,0},{1,3},{3,5},{5,7},{7,1},{8,10},{10,12},{12... | collective-permute-start | bytes 172040 | tf_op jit(solution)/shard_map/ppermute | solution.py:76
  63.2 0.9 %collective-permute-done.14 = bf16[16,1792]{1,0:T(8,128)(2,1)S(1)} collective-permute-done((bf16[16,1792]{1,0:T(8,128)(2,1)S(1)}, bf16[16,1792]{1,0:T(8,128)(2,1)S(1)}, u32[]{:S(2)}, u32[]{:S(2)}) %collective-permute-start.14) | collective-permute-done | bytes 57376 | tf_op jit(solution)/shard_map/ppermute | solution.py:76
  64.1 2.3 %collective-permute-done.13 = bf16[16,1792]{1,0:T(8,128)(2,1)S(1)} collective-permute-done((bf16[16,1792]{1,0:T(8,128)(2,1)S(1)}, bf16[16,1792]{1,0:T(8,128)(2,1)S(1)}, u32[]{:S(2)}, u32[]{:S(2)}) %collective-permute-start.13) | collective-permute-done | bytes 57376 | tf_op jit(solution)/shard_map/ppermute | solution.py:76
  66.4 0.6 collective-permute-done.12
  67.2 1.2 %multiply_divide_fusion = (f32[16,7168]{1,0:T(8,128)}, f32[16,7168]{1,0:T(8,128)}, f32[16,7168]{1,0:T(8,128)}) fusion(f32[]{:T(128)} %bitcast.35, f32[]{:T(128)} %bitcast.34, f32[16,7168]{1,0:T(8,128)S(1)} %bitcast.99, f32[16,7168]{1,0:T(8,128)S(1)} %copy-done, f32[16,7168]{1,0:T(8,128)S(1)} %copy-done.1), kind=kLoop, calls=%fused_computation.31 | loop fusion | flops 1261568 | bytes 2752520 | tf_op jit(solution)/shard_map/div | solution.py:46
  (28 shorter events, 0.4 us)
Async XLA Ops:
  2.0 7.4 %copy-start.2 = (s32[2]{0:T(128)S(1)}, s32[2]{0:T(128)}, u32[]{:S(2)}) copy-start(s32[2]{0:T(128)} %param.6) | copy-start | bytes 28
  3.1 29.3 %all-to-all-start = ((bf16[4,64,1792]{2,1,0:T(8,128)(2,1)}), bf16[4,64,1792]{2,1,0:T(8,128)(2,1)S(1)}, u32[]{:S(2)}, u32[]{:S(2)}) async-start(bf16[4,64,1792]{2,1,0:T(8,128)(2,1)} %pad_maximum_fusion), calls=%async_computation | async-start | bytes 1835008 | tf_op jit(solution)/shard_map/all_to_all | solution.py:118
  33.0 3.4 %collective-permute-start = (f32[16,512]{1,0:T(8,128)S(1)}, f32[16,512]{1,0:T(8,128)S(1)}, u32[]{:S(2)}, u32[]{:S(2)}) collective-permute-start(f32[16,512]{1,0:T(8,128)S(1)} %get-tuple-element.17), channel_id=1, source_target_pairs={{0,8},{8,16},{16,24},{24,0},{1,9},{9,17},{17,25},{25,1},{2,10},{10... | collective-permute-start | bytes 98312 | tf_op jit(solution)/shard_map/ppermute | solution.py:76
  33.1 3.3 %collective-permute-start.2 = (f32[16,512]{1,0:T(8,128)S(1)}, f32[16,512]{1,0:T(8,128)S(1)}, u32[]{:S(2)}, u32[]{:S(2)}) collective-permute-start(f32[16,512]{1,0:T(8,128)S(1)} %get-tuple-element.18), channel_id=1, source_target_pairs={{0,24},{8,0},{16,8},{24,16},{1,25},{9,1},{17,9},{25,17},{2,26},{10... | collective-permute-start | bytes 98312 | tf_op jit(solution)/shard_map/ppermute | solution.py:76
  34.8 3.9 %collective-permute-start.1 = (f32[16,512]{1,0:T(8,128)S(1)}, f32[16,512]{1,0:T(8,128)S(1)}, u32[]{:S(2)}, u32[]{:S(2)}) collective-permute-start(f32[16,512]{1,0:T(8,128)S(1)} %get-tuple-element.19), channel_id=1, source_target_pairs={{0,16},{8,24},{16,0},{24,8},{1,17},{9,25},{17,1},{25,9},{2,18},{10... | collective-permute-start | bytes 98312 | tf_op jit(solution)/shard_map/ppermute | solution.py:76
  38.8 5.5 %collective-permute-start.3 = (f32[4,512]{1,0:T(4,128)S(1)}, f32[4,512]{1,0:T(4,128)S(1)}, u32[]{:S(2)}, u32[]{:S(2)}) collective-permute-start(f32[4,512]{1,0:T(4,128)S(1)} %get-tuple-element.24), channel_id=1, source_target_pairs={{0,2},{2,4},{4,6},{6,0},{1,3},{3,5},{5,7},{7,1},{8,10},{10,12},{12... | collective-permute-start | bytes 24584 | tf_op jit(solution)/shard_map/ppermute | solution.py:76
  38.9 5.4 %collective-permute-start.5 = (f32[4,512]{1,0:T(4,128)S(1)}, f32[4,512]{1,0:T(4,128)S(1)}, u32[]{:S(2)}, u32[]{:S(2)}) collective-permute-start(f32[4,512]{1,0:T(4,128)S(1)} %get-tuple-element.25), channel_id=1, source_target_pairs={{0,6},{2,0},{4,2},{6,4},{1,7},{3,1},{5,3},{7,5},{8,14},{10,8},{12,... | collective-permute-start | bytes 24584 | tf_op jit(solution)/shard_map/ppermute | solution.py:76
  42.7 4.5 %collective-permute-start.4 = (f32[4,512]{1,0:T(4,128)S(1)}, f32[4,512]{1,0:T(4,128)S(1)}, u32[]{:S(2)}, u32[]{:S(2)}) collective-permute-start(f32[4,512]{1,0:T(4,128)S(1)} %get-tuple-element.26), channel_id=1, source_target_pairs={{0,4},{2,6},{4,0},{6,2},{1,5},{3,7},{5,1},{7,3},{8,12},{10,14},{12... | collective-permute-start | bytes 24584 | tf_op jit(solution)/shard_map/ppermute | solution.py:76
  47.2 3.7 %collective-permute-start.8 = (bf16[4,512]{1,0:T(4,128)(2,1)S(1)}, bf16[4,512]{1,0:T(4,128)(2,1)S(1)}, u32[]{:S(2)}, u32[]{:S(2)}) collective-permute-start(bf16[4,512]{1,0:T(4,128)(2,1)S(1)} %fusion.44), channel_id=1, source_target_pairs={{0,6},{2,0},{4,2},{6,4},{1,7},{3,1},{5,3},{7,5},{8,14},{10,8},{12,... | collective-permute-start | bytes 12296 | tf_op jit(solution)/shard_map/ppermute | solution.py:76
  48.2 4.5 %collective-permute-start.7 = (bf16[4,512]{1,0:T(4,128)(2,1)S(1)}, bf16[4,512]{1,0:T(4,128)(2,1)S(1)}, u32[]{:S(2)}, u32[]{:S(2)}) collective-permute-start(bf16[4,512]{1,0:T(4,128)(2,1)S(1)} %fusion.44), channel_id=1, source_target_pairs={{0,4},{2,6},{4,0},{6,2},{1,5},{3,7},{5,1},{7,3},{8,12},{10,14},{12... | collective-permute-start | bytes 12296 | tf_op jit(solution)/shard_map/ppermute | solution.py:76
  48.2 5.4 %collective-permute-start.6 = (bf16[4,512]{1,0:T(4,128)(2,1)S(1)}, bf16[4,512]{1,0:T(4,128)(2,1)S(1)}, u32[]{:S(2)}, u32[]{:S(2)}) collective-permute-start(bf16[4,512]{1,0:T(4,128)(2,1)S(1)} %fusion.44), channel_id=1, source_target_pairs={{0,2},{2,4},{4,6},{6,0},{1,3},{3,5},{5,7},{7,1},{8,10},{10,12},{12... | collective-permute-start | bytes 12296 | tf_op jit(solution)/shard_map/ppermute | solution.py:76
  53.7 1.8 %collective-permute-start.11 = (bf16[16,512]{1,0:T(8,128)(2,1)S(1)}, bf16[16,512]{1,0:T(8,128)(2,1)S(1)}, u32[]{:S(2)}, u32[]{:S(2)}) collective-permute-start(bf16[16,512]{1,0:T(8,128)(2,1)S(1)} %reshape.54), channel_id=1, source_target_pairs={{0,24},{8,0},{16,8},{24,16},{1,25},{9,1},{17,9},{25,17},{2,26},{10... | collective-permute-start | bytes 49160 | tf_op jit(solution)/shard_map/ppermute | solution.py:76
  53.7 3.8 %collective-permute-start.10 = (bf16[16,512]{1,0:T(8,128)(2,1)S(1)}, bf16[16,512]{1,0:T(8,128)(2,1)S(1)}, u32[]{:S(2)}, u32[]{:S(2)}) collective-permute-start(bf16[16,512]{1,0:T(8,128)(2,1)S(1)} %reshape.54), channel_id=1, source_target_pairs={{0,16},{8,24},{16,0},{24,8},{1,17},{9,25},{17,1},{25,9},{2,18},{10... | collective-permute-start | bytes 49160 | tf_op jit(solution)/shard_map/ppermute | solution.py:76
  55.3 3.2 %collective-permute-start.9 = (bf16[16,512]{1,0:T(8,128)(2,1)S(1)}, bf16[16,512]{1,0:T(8,128)(2,1)S(1)}, u32[]{:S(2)}, u32[]{:S(2)}) collective-permute-start(bf16[16,512]{1,0:T(8,128)(2,1)S(1)} %reshape.54), channel_id=1, source_target_pairs={{0,8},{8,16},{16,24},{24,0},{1,9},{9,17},{17,25},{25,1},{2,10},{10... | collective-permute-start | bytes 49160 | tf_op jit(solution)/shard_map/ppermute | solution.py:76
  58.5 8.7 %copy-start = (f32[16,7168]{1,0:T(8,128)S(1)}, f32[16,7168]{1,0:T(8,128)}, u32[]{:S(2)}) copy-start(f32[16,7168]{1,0:T(8,128)} %param.9) | copy-start | bytes 1376260
  58.5 8.7 %copy-start.1 = (f32[16,7168]{1,0:T(8,128)S(1)}, f32[16,7168]{1,0:T(8,128)}, u32[]{:S(2)}) copy-start(f32[16,7168]{1,0:T(8,128)} %param.8) | copy-start | bytes 1376260
  59.2 4.9 %collective-permute-start.14 = (bf16[16,1792]{1,0:T(8,128)(2,1)S(1)}, bf16[16,1792]{1,0:T(8,128)(2,1)S(1)}, u32[]{:S(2)}, u32[]{:S(2)}) collective-permute-start(bf16[16,1792]{1,0:T(8,128)(2,1)S(1)} %get-tuple-element.14), channel_id=1, source_target_pairs={{0,6},{2,0},{4,2},{6,4},{1,7},{3,1},{5,3},{7,5},{8,14},{10,8},{12,... | collective-permute-start | bytes 172040 | tf_op jit(solution)/shard_map/ppermute | solution.py:76
  61.0 5.5 %collective-permute-start.13 = (bf16[16,1792]{1,0:T(8,128)(2,1)S(1)}, bf16[16,1792]{1,0:T(8,128)(2,1)S(1)}, u32[]{:S(2)}, u32[]{:S(2)}) collective-permute-start(bf16[16,1792]{1,0:T(8,128)(2,1)S(1)} %get-tuple-element.15), channel_id=1, source_target_pairs={{0,4},{2,6},{4,0},{6,2},{1,5},{3,7},{5,1},{7,3},{8,12},{10,14},{12... | collective-permute-start | bytes 172040 | tf_op jit(solution)/shard_map/ppermute | solution.py:76
  61.0 6.1 %collective-permute-start.12 = (bf16[16,1792]{1,0:T(8,128)(2,1)S(1)}, bf16[16,1792]{1,0:T(8,128)(2,1)S(1)}, u32[]{:S(2)}, u32[]{:S(2)}) collective-permute-start(bf16[16,1792]{1,0:T(8,128)(2,1)S(1)} %get-tuple-element.16), channel_id=1, source_target_pairs={{0,2},{2,4},{4,6},{6,0},{1,3},{3,5},{5,7},{7,1},{8,10},{10,12},{12... | collective-permute-start | bytes 172040 | tf_op jit(solution)/shard_map/ppermute | solution.py:76

commit v9 on v8

--- a/solution.py
+++ b/solution.py
@@ -114,8 +114,12 @@
 
     projection = lax.optimization_barrier(projection_block(first, width, RANK, seeds))
 
-    pieces = jnp.stack([gradient[:, i * width : (i + 1) * width] for i in range(n_rep)])
-    held = lax.all_to_all(pieces, "replica", 0, 0, tiled=True)
+    got = shifted(
+        lambda k: lax.dynamic_slice_in_dim(gradient, ((member + k) % n_rep) * width, width, 1),
+        "replica",
+        n_rep,
+    )
+    held = by_source(got, member, n_rep)
 
     terms = jnp.dot(
         held.reshape(n_rep * rows, width), projection, preferred_element_type=jnp.float32

time: 68.6 us -> 67.2 us (0.980)
  waiting for transfers between devices: 20.8 us -> 14.2 us
  starting transfers between devices: 20.6 us -> 24.7 us
    ppermute x15 -> x18, starting transfers between devices: 14.3 us -> 24.7 us  [shifted(): got.append(lax.ppermute(value_of(k), axis, pairs))]
    all_to_all x1 -> x0, starting transfers between devices: 6.35 us -> none  [per_device(): held = lax.all_to_all(pieces, 'replica', 0, 0, tiled=True)]
    ppermute x15 -> x18, waiting for transfers between devices: 18.1 us -> 14.2 us  [shifted(): got.append(lax.ppermute(value_of(k), axis, pairs))]
    all_to_all x1 -> x0, waiting for transfers between devices: 2.75 us -> none  [per_device(): held = lax.all_to_all(pieces, 'replica', 0, 0, tiled=True)]
    another operation x1 -> x0, local copies, waits for them, and re-layouts: 1.34 us -> none  [per_device(): jnp.stack([gradient[:, i * width:(i + 1) * width] for i in range(n_rep)])]
    another operation x4 -> x6, other arithmetic: 0.09 us -> 1.43 us  [by_source(): jnp.stack([lax.select_n((index - p) % size, *got) for p in range(size)])]
    dynamic_slice x0 -> x1, local copies, waits for them, and re-layouts: none -> 1.21 us  [per_device(): lax.dynamic_slice_in_dim(gradient, (member + k) % n_rep * width, width, 1)]
    another operation x1 -> x0, other arithmetic: 1.07 us -> none  [per_device(): jnp.stack([gradient[:, i * width:(i + 1) * width] for i in range(n_rep)])]
  transfers between devices with their start and end apart: 16 -> 18, of which waited for: 13 -> 12; matrix products, arithmetic and copies ran while one was open for 28% -> 29% of each run, Pallas kernels for 0% -> 0%
where the time goes in v9:
time: 67.2 us; the launch traced here: 67 us
  starting transfers between devices  24.7 us (37%)
  other arithmetic  21 us (31%)
  waiting for transfers between devices  14.2 us (21%)
  between operations  3.05 us (5%)
  local copies, waits for them, and re-layouts  2.66 us (4%)
  matrix products  1.3 us (2%)
    ppermute x18, starting transfers between devices, shifted(): got.append(lax.ppermute(value_of(k), axis, pairs))  24.7 us
    convert_element_type x1, other arithmetic, projection_block(): return (gauss * rank ** (-0.5)).astype(jnp.bfloat16)  18.2 us
    ppermute x18, waiting for transfers between devices, shifted(): got.append(lax.ppermute(value_of(k), axis, pairs))  14.2 us
    another operation x6, other arithmetic, by_source(): jnp.stack([lax.select_n((index - p) % size, *got) for p in range(size)])  1.43 us
  transfers between devices with their start and end apart: 18, of which 12 were waited for; matrix products, arithmetic and copies ran while one was open for 29% of the time, Pallas kernels for 0%

profile of v9, /device:TPU:0, one launch (start us, length us, event | category | flops | bytes accessed | tf_op | source)
XLA Modules:
  0.0 67.0 jit_solution(17131713166350896976)
XLA Ops:
  0.7 1.2 %dynamic-slice_bitcast_fusion = (bf16[64,1792]{1,0:T(8,128)(2,1)S(1)}, bf16[64,1792]{1,0:T(8,128)(2,1)S(1)}, bf16[64,1792]{1,0:T(8,128)(2,1)S(1)}) fusion(bf16[1,64,7168]{2,1,0:T(8,128)(2,1)} %param.5, s32[]{:T(128)S(6)} %select_n.544, s32[]{:T(128)S(6)} %select_n.537, s32[]{:T(128)S(6)} %select_n.542), kind=kLoop, calls=%fused_computation.45 | loop fusion | bytes 1376268 | tf_op jit(solution)/shard_map/dynamic_slice | solution.py:118
  1.9 3.1 %collective-permute-start = (bf16[64,1792]{1,0:T(8,128)(2,1)S(1)}, bf16[64,1792]{1,0:T(8,128)(2,1)S(1)}, u32[]{:S(2)}, u32[]{:S(2)}) collective-permute-start(bf16[64,1792]{1,0:T(8,128)(2,1)S(1)} %get-tuple-element.11), channel_id=1, source_target_pairs={{0,2},{2,4},{4,6},{6,0},{1,3},{3,5},{5,7},{7,1},{8,10},{10,12},{12... | collective-permute-start | bytes 688136 | tf_op jit(solution)/shard_map/ppermute | solution.py:76
  5.0 2.6 %collective-permute-start.1 = (bf16[64,1792]{1,0:T(8,128)(2,1)S(1)}, bf16[64,1792]{1,0:T(8,128)(2,1)S(1)}, u32[]{:S(2)}, u32[]{:S(2)}) collective-permute-start(bf16[64,1792]{1,0:T(8,128)(2,1)S(1)} %get-tuple-element.12), channel_id=1, source_target_pairs={{0,4},{2,6},{4,0},{6,2},{1,5},{3,7},{5,1},{7,3},{8,12},{10,14},{12... | collective-permute-start | bytes 688136 | tf_op jit(solution)/shard_map/ppermute | solution.py:76
  7.6 1.3 %collective-permute-start.2 = (bf16[64,1792]{1,0:T(8,128)(2,1)S(1)}, bf16[64,1792]{1,0:T(8,128)(2,1)S(1)}, u32[]{:S(2)}, u32[]{:S(2)}) collective-permute-start(bf16[64,1792]{1,0:T(8,128)(2,1)S(1)} %get-tuple-element.10), channel_id=1, source_target_pairs={{0,6},{2,0},{4,2},{6,4},{1,7},{3,1},{5,3},{7,5},{8,14},{10,8},{12,... | collective-permute-start | bytes 688136 | tf_op jit(solution)/shard_map/ppermute | solution.py:76
  8.9 1.3 %fusion.55 = (s32[1]{0:T(128)}, s32[1]{0:T(128)}) fusion(s32[2]{0:T(128)} %param.6), kind=kLoop, calls=%fused_computation.101 | loop fusion | bytes 16 | tf_op jit(solution)/shard_map/slice | solution.py:23
  11.6 18.2 %fusion.18 = bf16[1792,512]{1,0:T(8,128)(2,1)S(1)} fusion(s32[]{:T(128)} %bitcast.9, s32[1792]{0:T(1024)S(1)} %add_multiply_fusion), kind=kLoop, calls=%fused_computation.24 | loop fusion | flops 32112640 | bytes 1842180 | tf_op jit(solution)/shard_map/convert_element_type | solution.py:37
  30.0 1.2 %fusion.22 = (bf16[1,64,1792]{2,1,0:T(8,128)(2,1)S(1)}, bf16[1,64,1792]{2,1,0:T(8,128)(2,1)S(1)}, bf16[1,64,1792]{2,1,0:T(8,128)(2,1)S(1)}, bf16[1,64,1792]{2,1,0:T(8,128)(2,1)S(1)}) fusion(bf16[64,1792]{1,0:T(8,128)(2,1)S(1)} %collective-permute-done, bf16[64,1792]{1,0:T(8,128)(2,1)S(1)} %collective-permute-done.1, ...), kind=kLoop, calls=%fused_computation.38 | loop fusion | flops 1376256 | bytes 1835024 | tf_op jit(solution)/shard_map/stack | solution.py:81
  31.3 0.6 fusion.56
  32.1 1.6 %collective-permute-start.4 = (f32[16,512]{1,0:T(8,128)S(1)}, f32[16,512]{1,0:T(8,128)S(1)}, u32[]{:S(2)}, u32[]{:S(2)}) collective-permute-start(f32[16,512]{1,0:T(8,128)S(1)} %get-tuple-element.22), channel_id=1, source_target_pairs={{0,16},{8,24},{16,0},{24,8},{1,17},{9,25},{17,1},{25,9},{2,18},{10... | collective-permute-start | bytes 98312 | tf_op jit(solution)/shard_map/ppermute | solution.py:76
  33.6 1.4 %collective-permute-start.5 = (f32[16,512]{1,0:T(8,128)S(1)}, f32[16,512]{1,0:T(8,128)S(1)}, u32[]{:S(2)}, u32[]{:S(2)}) collective-permute-start(f32[16,512]{1,0:T(8,128)S(1)} %get-tuple-element.21), channel_id=1, source_target_pairs={{0,24},{8,0},{16,8},{24,16},{1,25},{9,1},{17,9},{25,17},{2,26},{10... | collective-permute-start | bytes 98312 | tf_op jit(solution)/shard_map/ppermute | solution.py:76
  35.0 0.4 collective-permute-done.3
  35.4 0.7 collective-permute-done.4
  36.1 0.6 collective-permute-done.5
  36.7 0.7 %collective-permute-start.6 = (f32[4,512]{1,0:T(4,128)S(1)}, f32[4,512]{1,0:T(4,128)S(1)}, u32[]{:S(2)}, u32[]{:S(2)}) collective-permute-start(f32[4,512]{1,0:T(4,128)S(1)} %get-tuple-element.27), channel_id=1, source_target_pairs={{0,2},{2,4},{4,6},{6,0},{1,3},{3,5},{5,7},{7,1},{8,10},{10,12},{12... | collective-permute-start | bytes 24584 | tf_op jit(solution)/shard_map/ppermute | solution.py:76
  37.4 0.3 collective-permute-start.7
  37.8 2.8 %collective-permute-start.8 = (f32[4,512]{1,0:T(4,128)S(1)}, f32[4,512]{1,0:T(4,128)S(1)}, u32[]{:S(2)}, u32[]{:S(2)}) collective-permute-start(f32[4,512]{1,0:T(4,128)S(1)} %get-tuple-element.28), channel_id=1, source_target_pairs={{0,6},{2,0},{4,2},{6,4},{1,7},{3,1},{5,3},{7,5},{8,14},{10,8},{12,... | collective-permute-start | bytes 24584 | tf_op jit(solution)/shard_map/ppermute | solution.py:76
  40.6 1.7 %collective-permute-done.6 = f32[4,512]{1,0:T(4,128)S(1)} collective-permute-done((f32[4,512]{1,0:T(4,128)S(1)}, f32[4,512]{1,0:T(4,128)S(1)}, u32[]{:S(2)}, u32[]{:S(2)}) %collective-permute-start.6) | collective-permute-done | bytes 8224 | tf_op jit(solution)/shard_map/ppermute | solution.py:76
  42.2 0.5 collective-permute-done.8
  42.8 1.3 %collective-permute-start.10 = (bf16[4,512]{1,0:T(4,128)(2,1)S(1)}, bf16[4,512]{1,0:T(4,128)(2,1)S(1)}, u32[]{:S(2)}, u32[]{:S(2)}) collective-permute-start(bf16[4,512]{1,0:T(4,128)(2,1)S(1)} %fusion.52), channel_id=1, source_target_pairs={{0,4},{2,6},{4,0},{6,2},{1,5},{3,7},{5,1},{7,3},{8,12},{10,14},{12... | collective-permute-start | bytes 12296 | tf_op jit(solution)/shard_map/ppermute | solution.py:76
  44.1 3.1 %collective-permute-start.11 = (bf16[4,512]{1,0:T(4,128)(2,1)S(1)}, bf16[4,512]{1,0:T(4,128)(2,1)S(1)}, u32[]{:S(2)}, u32[]{:S(2)}) collective-permute-start(bf16[4,512]{1,0:T(4,128)(2,1)S(1)} %fusion.52), channel_id=1, source_target_pairs={{0,6},{2,0},{4,2},{6,4},{1,7},{3,1},{5,3},{7,5},{8,14},{10,8},{12,... | collective-permute-start | bytes 12296 | tf_op jit(solution)/shard_map/ppermute | solution.py:76
  47.3 1.2 %collective-permute-done.11 = bf16[4,512]{1,0:T(4,128)(2,1)S(1)} collective-permute-done((bf16[4,512]{1,0:T(4,128)(2,1)S(1)}, bf16[4,512]{1,0:T(4,128)(2,1)S(1)}, u32[]{:S(2)}, u32[]{:S(2)}) %collective-permute-start.11) | collective-permute-done | bytes 4128 | tf_op jit(solution)/shard_map/ppermute | solution.py:76
  48.5 4.1 %collective-permute-done.9 = bf16[4,512]{1,0:T(4,128)(2,1)S(1)} collective-permute-done((bf16[4,512]{1,0:T(4,128)(2,1)S(1)}, bf16[4,512]{1,0:T(4,128)(2,1)S(1)}, u32[]{:S(2)}, u32[]{:S(2)}) %collective-permute-start.9) | collective-permute-done | bytes 4128 | tf_op jit(solution)/shard_map/ppermute | solution.py:76
  52.8 1.0 %collective-permute-start.13 = (bf16[16,512]{1,0:T(8,128)(2,1)S(1)}, bf16[16,512]{1,0:T(8,128)(2,1)S(1)}, u32[]{:S(2)}, u32[]{:S(2)}) collective-permute-start(bf16[16,512]{1,0:T(8,128)(2,1)S(1)} %reshape.58), channel_id=1, source_target_pairs={{0,16},{8,24},{16,0},{24,8},{1,17},{9,25},{17,1},{25,9},{2,18},{10... | collective-permute-start | bytes 49160 | tf_op jit(solution)/shard_map/ppermute | solution.py:76
  53.8 1.4 %collective-permute-start.14 = (bf16[16,512]{1,0:T(8,128)(2,1)S(1)}, bf16[16,512]{1,0:T(8,128)(2,1)S(1)}, u32[]{:S(2)}, u32[]{:S(2)}) collective-permute-start(bf16[16,512]{1,0:T(8,128)(2,1)S(1)} %reshape.58), channel_id=1, source_target_pairs={{0,24},{8,0},{16,8},{24,16},{1,25},{9,1},{17,9},{25,17},{2,26},{10... | collective-permute-start | bytes 49160 | tf_op jit(solution)/shard_map/ppermute | solution.py:76
  55.2 0.7 %collective-permute-done.12 = bf16[16,512]{1,0:T(8,128)(2,1)S(1)} collective-permute-done((bf16[16,512]{1,0:T(8,128)(2,1)S(1)}, bf16[16,512]{1,0:T(8,128)(2,1)S(1)}, u32[]{:S(2)}, u32[]{:S(2)}) %collective-permute-start.12) | collective-permute-done | bytes 16416 | tf_op jit(solution)/shard_map/ppermute | solution.py:76
  55.9 0.8 %collective-permute-done.13 = bf16[16,512]{1,0:T(8,128)(2,1)S(1)} collective-permute-done((bf16[16,512]{1,0:T(8,128)(2,1)S(1)}, bf16[16,512]{1,0:T(8,128)(2,1)S(1)}, u32[]{:S(2)}, u32[]{:S(2)}) %collective-permute-start.13) | collective-permute-done | bytes 16416 | tf_op jit(solution)/shard_map/ppermute | solution.py:76
  56.7 0.7 %convolution_convert_fusion = bf16[4,16,1792]{2,1,0:T(8,128)(2,1)S(1)} fusion(bf16[1792,512]{1,0:T(8,128)(2,1)S(1)} %fusion.18, bf16[1,16,512]{2,1,0:T(8,128)(2,1)S(1)} %get-tuple-element.24, bf16[1,16,512]{2,1,0:T(8,128)(2,1)S(1)} %get-tuple-element.25, bf16[1,16,512]{2,1,0:T(8,128)(2,1)S(1)} %get-tuple-element.26, ...), kind=kOutput, calls=%fused_computation.25 | convolution fusion | flops 117653504 | bytes 2129920 | tf_op jit(solution)/shard_map/dot_general | solution.py:134
  57.5 0.6 collective-permute-start.16
  58.1 3.3 %collective-permute-start.17 = (bf16[16,1792]{1,0:T(8,128)(2,1)S(1)}, bf16[16,1792]{1,0:T(8,128)(2,1)S(1)}, u32[]{:S(2)}, u32[]{:S(2)}) collective-permute-start(bf16[16,1792]{1,0:T(8,128)(2,1)S(1)} %get-tuple-element.17), channel_id=1, source_target_pairs={{0,6},{2,0},{4,2},{6,4},{1,7},{3,1},{5,3},{7,5},{8,14},{10,8},{12,... | collective-permute-start | bytes 172040 | tf_op jit(solution)/shard_map/ppermute | solution.py:76
  62.1 2.1 %collective-permute-done.15 = bf16[16,1792]{1,0:T(8,128)(2,1)S(1)} collective-permute-done((bf16[16,1792]{1,0:T(8,128)(2,1)S(1)}, bf16[16,1792]{1,0:T(8,128)(2,1)S(1)}, u32[]{:S(2)}, u32[]{:S(2)}) %collective-permute-start.15) | collective-permute-done | bytes 57376 | tf_op jit(solution)/shard_map/ppermute | solution.py:76
  64.2 1.4 %collective-permute-done.16 = bf16[16,1792]{1,0:T(8,128)(2,1)S(1)} collective-permute-done((bf16[16,1792]{1,0:T(8,128)(2,1)S(1)}, bf16[16,1792]{1,0:T(8,128)(2,1)S(1)}, u32[]{:S(2)}, u32[]{:S(2)}) %collective-permute-start.16) | collective-permute-done | bytes 57376 | tf_op jit(solution)/shard_map/ppermute | solution.py:76
  65.8 1.2 %multiply_divide_fusion = (f32[16,7168]{1,0:T(8,128)}, f32[16,7168]{1,0:T(8,128)}, f32[16,7168]{1,0:T(8,128)}) fusion(f32[]{:T(128)} %bitcast.38, f32[]{:T(128)} %bitcast.37, f32[16,7168]{1,0:T(8,128)S(1)} %bitcast.125, f32[16,7168]{1,0:T(8,128)S(1)} %copy-done, f32[16,7168]{1,0:T(8,128)S(1)} %copy-done.1), kind=kLoop, calls=%fused_computation.31 | loop fusion | flops 1261568 | bytes 2752520 | tf_op jit(solution)/shard_map/div | solution.py:46
  (31 shorter events, 0.8 us)
Async XLA Ops:
  1.9 28.0 %collective-permute-start = (bf16[64,1792]{1,0:T(8,128)(2,1)S(1)}, bf16[64,1792]{1,0:T(8,128)(2,1)S(1)}, u32[]{:S(2)}, u32[]{:S(2)}) collective-permute-start(bf16[64,1792]{1,0:T(8,128)(2,1)S(1)} %get-tuple-element.11), channel_id=1, source_target_pairs={{0,2},{2,4},{4,6},{6,0},{1,3},{3,5},{5,7},{7,1},{8,10},{10,12},{12... | collective-permute-start | bytes 688136 | tf_op jit(solution)/shard_map/ppermute | solution.py:76
  5.0 24.9 %collective-permute-start.1 = (bf16[64,1792]{1,0:T(8,128)(2,1)S(1)}, bf16[64,1792]{1,0:T(8,128)(2,1)S(1)}, u32[]{:S(2)}, u32[]{:S(2)}) collective-permute-start(bf16[64,1792]{1,0:T(8,128)(2,1)S(1)} %get-tuple-element.12), channel_id=1, source_target_pairs={{0,4},{2,6},{4,0},{6,2},{1,5},{3,7},{5,1},{7,3},{8,12},{10,14},{12... | collective-permute-start | bytes 688136 | tf_op jit(solution)/shard_map/ppermute | solution.py:76
  7.6 22.4 %collective-permute-start.2 = (bf16[64,1792]{1,0:T(8,128)(2,1)S(1)}, bf16[64,1792]{1,0:T(8,128)(2,1)S(1)}, u32[]{:S(2)}, u32[]{:S(2)}) collective-permute-start(bf16[64,1792]{1,0:T(8,128)(2,1)S(1)} %get-tuple-element.10), channel_id=1, source_target_pairs={{0,6},{2,0},{4,2},{6,4},{1,7},{3,1},{5,3},{7,5},{8,14},{10,8},{12,... | collective-permute-start | bytes 688136 | tf_op jit(solution)/shard_map/ppermute | solution.py:76
  32.0 3.4 %collective-permute-start.3 = (f32[16,512]{1,0:T(8,128)S(1)}, f32[16,512]{1,0:T(8,128)S(1)}, u32[]{:S(2)}, u32[]{:S(2)}) collective-permute-start(f32[16,512]{1,0:T(8,128)S(1)} %get-tuple-element.20), channel_id=1, source_target_pairs={{0,8},{8,16},{16,24},{24,0},{1,9},{9,17},{17,25},{25,1},{2,10},{10... | collective-permute-start | bytes 98312 | tf_op jit(solution)/shard_map/ppermute | solution.py:76
  32.1 4.0 %collective-permute-start.4 = (f32[16,512]{1,0:T(8,128)S(1)}, f32[16,512]{1,0:T(8,128)S(1)}, u32[]{:S(2)}, u32[]{:S(2)}) collective-permute-start(f32[16,512]{1,0:T(8,128)S(1)} %get-tuple-element.22), channel_id=1, source_target_pairs={{0,16},{8,24},{16,0},{24,8},{1,17},{9,25},{17,1},{25,9},{2,18},{10... | collective-permute-start | bytes 98312 | tf_op jit(solution)/shard_map/ppermute | solution.py:76
  33.6 3.0 %collective-permute-start.5 = (f32[16,512]{1,0:T(8,128)S(1)}, f32[16,512]{1,0:T(8,128)S(1)}, u32[]{:S(2)}, u32[]{:S(2)}) collective-permute-start(f32[16,512]{1,0:T(8,128)S(1)} %get-tuple-element.21), channel_id=1, source_target_pairs={{0,24},{8,0},{16,8},{24,16},{1,25},{9,1},{17,9},{25,17},{2,26},{10... | collective-permute-start | bytes 98312 | tf_op jit(solution)/shard_map/ppermute | solution.py:76
  36.7 5.6 %collective-permute-start.6 = (f32[4,512]{1,0:T(4,128)S(1)}, f32[4,512]{1,0:T(4,128)S(1)}, u32[]{:S(2)}, u32[]{:S(2)}) collective-permute-start(f32[4,512]{1,0:T(4,128)S(1)} %get-tuple-element.27), channel_id=1, source_target_pairs={{0,2},{2,4},{4,6},{6,0},{1,3},{3,5},{5,7},{7,1},{8,10},{10,12},{12... | collective-permute-start | bytes 24584 | tf_op jit(solution)/shard_map/ppermute | solution.py:76
  37.4 4.8 %collective-permute-start.7 = (f32[4,512]{1,0:T(4,128)S(1)}, f32[4,512]{1,0:T(4,128)S(1)}, u32[]{:S(2)}, u32[]{:S(2)}) collective-permute-start(f32[4,512]{1,0:T(4,128)S(1)} %get-tuple-element.29), channel_id=1, source_target_pairs={{0,4},{2,6},{4,0},{6,2},{1,5},{3,7},{5,1},{7,3},{8,12},{10,14},{12... | collective-permute-start | bytes 24584 | tf_op jit(solution)/shard_map/ppermute | solution.py:76
  37.8 5.0 %collective-permute-start.8 = (f32[4,512]{1,0:T(4,128)S(1)}, f32[4,512]{1,0:T(4,128)S(1)}, u32[]{:S(2)}, u32[]{:S(2)}) collective-permute-start(f32[4,512]{1,0:T(4,128)S(1)} %get-tuple-element.28), channel_id=1, source_target_pairs={{0,6},{2,0},{4,2},{6,4},{1,7},{3,1},{5,3},{7,5},{8,14},{10,8},{12,... | collective-permute-start | bytes 24584 | tf_op jit(solution)/shard_map/ppermute | solution.py:76
  42.8 4.6 %collective-permute-start.10 = (bf16[4,512]{1,0:T(4,128)(2,1)S(1)}, bf16[4,512]{1,0:T(4,128)(2,1)S(1)}, u32[]{:S(2)}, u32[]{:S(2)}) collective-permute-start(bf16[4,512]{1,0:T(4,128)(2,1)S(1)} %fusion.52), channel_id=1, source_target_pairs={{0,4},{2,6},{4,0},{6,2},{1,5},{3,7},{5,1},{7,3},{8,12},{10,14},{12... | collective-permute-start | bytes 12296 | tf_op jit(solution)/shard_map/ppermute | solution.py:76
  44.1 4.5 %collective-permute-start.11 = (bf16[4,512]{1,0:T(4,128)(2,1)S(1)}, bf16[4,512]{1,0:T(4,128)(2,1)S(1)}, u32[]{:S(2)}, u32[]{:S(2)}) collective-permute-start(bf16[4,512]{1,0:T(4,128)(2,1)S(1)} %fusion.52), channel_id=1, source_target_pairs={{0,6},{2,0},{4,2},{6,4},{1,7},{3,1},{5,3},{7,5},{8,14},{10,8},{12,... | collective-permute-start | bytes 12296 | tf_op jit(solution)/shard_map/ppermute | solution.py:76
  47.2 5.4 %collective-permute-start.9 = (bf16[4,512]{1,0:T(4,128)(2,1)S(1)}, bf16[4,512]{1,0:T(4,128)(2,1)S(1)}, u32[]{:S(2)}, u32[]{:S(2)}) collective-permute-start(bf16[4,512]{1,0:T(4,128)(2,1)S(1)} %fusion.52), channel_id=1, source_target_pairs={{0,2},{2,4},{4,6},{6,0},{1,3},{3,5},{5,7},{7,1},{8,10},{10,12},{12... | collective-permute-start | bytes 12296 | tf_op jit(solution)/shard_map/ppermute | solution.py:76
  52.7 3.2 %collective-permute-start.12 = (bf16[16,512]{1,0:T(8,128)(2,1)S(1)}, bf16[16,512]{1,0:T(8,128)(2,1)S(1)}, u32[]{:S(2)}, u32[]{:S(2)}) collective-permute-start(bf16[16,512]{1,0:T(8,128)(2,1)S(1)} %reshape.58), channel_id=1, source_target_pairs={{0,8},{8,16},{16,24},{24,0},{1,9},{9,17},{17,25},{25,1},{2,10},{10... | collective-permute-start | bytes 49160 | tf_op jit(solution)/shard_map/ppermute | solution.py:76
  52.8 3.9 %collective-permute-start.13 = (bf16[16,512]{1,0:T(8,128)(2,1)S(1)}, bf16[16,512]{1,0:T(8,128)(2,1)S(1)}, u32[]{:S(2)}, u32[]{:S(2)}) collective-permute-start(bf16[16,512]{1,0:T(8,128)(2,1)S(1)} %reshape.58), channel_id=1, source_target_pairs={{0,16},{8,24},{16,0},{24,8},{1,17},{9,25},{17,1},{25,9},{2,18},{10... | collective-permute-start | bytes 49160 | tf_op jit(solution)/shard_map/ppermute | solution.py:76
  53.8 2.9 %collective-permute-start.14 = (bf16[16,512]{1,0:T(8,128)(2,1)S(1)}, bf16[16,512]{1,0:T(8,128)(2,1)S(1)}, u32[]{:S(2)}, u32[]{:S(2)}) collective-permute-start(bf16[16,512]{1,0:T(8,128)(2,1)S(1)} %reshape.58), channel_id=1, source_target_pairs={{0,24},{8,0},{16,8},{24,16},{1,25},{9,1},{17,9},{25,17},{2,26},{10... | collective-permute-start | bytes 49160 | tf_op jit(solution)/shard_map/ppermute | solution.py:76
  56.7 9.0 %copy-start = (f32[16,7168]{1,0:T(8,128)S(1)}, f32[16,7168]{1,0:T(8,128)}, u32[]{:S(2)}) copy-start(f32[16,7168]{1,0:T(8,128)} %param.9) | copy-start | bytes 1376260
  56.7 9.0 %copy-start.1 = (f32[16,7168]{1,0:T(8,128)S(1)}, f32[16,7168]{1,0:T(8,128)}, u32[]{:S(2)}) copy-start(f32[16,7168]{1,0:T(8,128)} %param.8) | copy-start | bytes 1376260
  57.4 6.7 %collective-permute-start.15 = (bf16[16,1792]{1,0:T(8,128)(2,1)S(1)}, bf16[16,1792]{1,0:T(8,128)(2,1)S(1)}, u32[]{:S(2)}, u32[]{:S(2)}) collective-permute-start(bf16[16,1792]{1,0:T(8,128)(2,1)S(1)} %get-tuple-element.19), channel_id=1, source_target_pairs={{0,2},{2,4},{4,6},{6,0},{1,3},{3,5},{5,7},{7,1},{8,10},{10,12},{12... | collective-permute-start | bytes 172040 | tf_op jit(solution)/shard_map/ppermute | solution.py:76
  57.5 8.1 %collective-permute-start.16 = (bf16[16,1792]{1,0:T(8,128)(2,1)S(1)}, bf16[16,1792]{1,0:T(8,128)(2,1)S(1)}, u32[]{:S(2)}, u32[]{:S(2)}) collective-permute-start(bf16[16,1792]{1,0:T(8,128)(2,1)S(1)} %get-tuple-element.18), channel_id=1, source_target_pairs={{0,4},{2,6},{4,0},{6,2},{1,5},{3,7},{5,1},{7,3},{8,12},{10,14},{12... | collective-permute-start | bytes 172040 | tf_op jit(solution)/shard_map/ppermute | solution.py:76
  58.1 7.5 %collective-permute-start.17 = (bf16[16,1792]{1,0:T(8,128)(2,1)S(1)}, bf16[16,1792]{1,0:T(8,128)(2,1)S(1)}, u32[]{:S(2)}, u32[]{:S(2)}) collective-permute-start(bf16[16,1792]{1,0:T(8,128)(2,1)S(1)} %get-tuple-element.17), channel_id=1, source_target_pairs={{0,6},{2,0},{4,2},{6,4},{1,7},{3,1},{5,3},{7,5},{8,14},{10,8},{12,... | collective-permute-start | bytes 172040 | tf_op jit(solution)/shard_map/ppermute | solution.py:76

commit v10 on v9

--- a/solution.py
+++ b/solution.py
@@ -20,7 +20,8 @@
 
 
 def projection_block(first_column, columns, rank, seeds):
-    seed_key = seeds[0] ^ seeds[1] * jnp.int32(668265263)
+    scaled = seeds * jnp.array([1, 668265263], jnp.int32)
+    seed_key = lax.reduce(scaled, jnp.int32(0), lax.bitwise_xor, (0,))
     column = lax.broadcasted_iota(jnp.int32, (columns, rank), 0) + first_column
     entry = lax.broadcasted_iota(jnp.int32, (columns, rank), 1)
     counter = (column * jnp.int32(rank) + entry) * jnp.int32(2)

time: 67.2 us -> 66.5 us (0.990)
  other arithmetic: 21 us -> 22.9 us
  local copies, waits for them, and re-layouts: 2.66 us -> 1.34 us
  between operations: 3.05 us -> 1.75 us
    slice x1 -> x0, local copies, waits for them, and re-layouts: 1.31 us -> none  [projection_block(): seed_key = seeds[0] ^ seeds[1] * jnp.int32(668265263)]
    another operation x0 -> x1, other arithmetic: none -> 1.31 us  [projection_block(): seed_key = lax.reduce(scaled, jnp.int32(0), lax.bitwise_xor, (0,))]
  transfers between devices with their start and end apart: 18 -> 18, of which waited for: 12 -> 12; matrix products, arithmetic and copies ran while one was open for 29% -> 30% of each run, Pallas kernels for 0% -> 0%
where the time goes in v10:
time: 66.5 us; the launch traced here: 66.3 us
  starting transfers between devices  24.7 us (37%)
  other arithmetic  22.9 us (34%)
  waiting for transfers between devices  14.3 us (22%)
  between operations  1.75 us (3%)
  local copies, waits for them, and re-layouts  1.34 us (2%)
  matrix products  1.31 us (2%)
    ppermute x18, starting transfers between devices, shifted(): got.append(lax.ppermute(value_of(k), axis, pairs))  24.7 us
    convert_element_type x1, other arithmetic, projection_block(): return (gauss * rank ** (-0.5)).astype(jnp.bfloat16)  18.9 us
    ppermute x18, waiting for transfers between devices, shifted(): got.append(lax.ppermute(value_of(k), axis, pairs))  14.3 us
    another operation x6, other arithmetic, by_source(): jnp.stack([lax.select_n((index - p) % size, *got) for p in range(size)])  1.43 us
  transfers between devices with their start and end apart: 18, of which 12 were waited for; matrix products, arithmetic and copies ran while one was open for 30% of the time, Pallas kernels for 0%

profile of v10, /device:TPU:0, one launch (start us, length us, event | category | flops | bytes accessed | tf_op | source)
XLA Modules:
  0.0 66.3 jit_solution(11401603942685022509)
XLA Ops:
  0.7 1.2 %dynamic-slice_bitcast_fusion = (bf16[64,1792]{1,0:T(8,128)(2,1)S(1)}, bf16[64,1792]{1,0:T(8,128)(2,1)S(1)}, bf16[64,1792]{1,0:T(8,128)(2,1)S(1)}) fusion(bf16[1,64,7168]{2,1,0:T(8,128)(2,1)} %param.6, s32[]{:T(128)S(6)} %select_n.544, s32[]{:T(128)S(6)} %select_n.537, s32[]{:T(128)S(6)} %select_n.542), kind=kLoop, calls=%fused_computation.45 | loop fusion | bytes 1376268 | tf_op jit(solution)/shard_map/dynamic_slice | solution.py:119
  1.9 3.1 %collective-permute-start = (bf16[64,1792]{1,0:T(8,128)(2,1)S(1)}, bf16[64,1792]{1,0:T(8,128)(2,1)S(1)}, u32[]{:S(2)}, u32[]{:S(2)}) collective-permute-start(bf16[64,1792]{1,0:T(8,128)(2,1)S(1)} %get-tuple-element.11), channel_id=1, source_target_pairs={{0,2},{2,4},{4,6},{6,0},{1,3},{3,5},{5,7},{7,1},{8,10},{10,12},{12... | collective-permute-start | bytes 688136 | tf_op jit(solution)/shard_map/ppermute | solution.py:77
  5.0 2.6 %collective-permute-start.1 = (bf16[64,1792]{1,0:T(8,128)(2,1)S(1)}, bf16[64,1792]{1,0:T(8,128)(2,1)S(1)}, u32[]{:S(2)}, u32[]{:S(2)}) collective-permute-start(bf16[64,1792]{1,0:T(8,128)(2,1)S(1)} %get-tuple-element.12), channel_id=1, source_target_pairs={{0,4},{2,6},{4,0},{6,2},{1,5},{3,7},{5,1},{7,3},{8,12},{10,14},{12... | collective-permute-start | bytes 688136 | tf_op jit(solution)/shard_map/ppermute | solution.py:77
  7.6 1.3 %collective-permute-start.2 = (bf16[64,1792]{1,0:T(8,128)(2,1)S(1)}, bf16[64,1792]{1,0:T(8,128)(2,1)S(1)}, u32[]{:S(2)}, u32[]{:S(2)}) collective-permute-start(bf16[64,1792]{1,0:T(8,128)(2,1)S(1)} %get-tuple-element.10), channel_id=1, source_target_pairs={{0,6},{2,0},{4,2},{6,4},{1,7},{3,1},{5,3},{7,5},{8,14},{10,8},{12,... | collective-permute-start | bytes 688136 | tf_op jit(solution)/shard_map/ppermute | solution.py:77
  8.9 1.3 %multiply_reduce_fusion = s32[]{:T(128)} fusion(s32[2]{0:T(128)} %param.7, s32[2]{0:T(128)} %constant.206.clone), kind=kLoop, calls=%fused_computation.100 | loop fusion | flops 3 | bytes 20 | tf_op jit(solution)/shard_map/reduce | solution.py:24
  10.3 18.9 %fusion.18 = bf16[1792,512]{1,0:T(8,128)(2,1)S(1)} fusion(s32[]{:T(128)} %multiply_reduce_fusion, s32[1792]{0:T(1024)S(1)} %add_multiply_fusion), kind=kLoop, calls=%fused_computation.24 | loop fusion | flops 32112640 | bytes 1842180 | tf_op jit(solution)/shard_map/convert_element_type | solution.py:38
  29.3 1.2 %fusion.22 = (bf16[1,64,1792]{2,1,0:T(8,128)(2,1)S(1)}, bf16[1,64,1792]{2,1,0:T(8,128)(2,1)S(1)}, bf16[1,64,1792]{2,1,0:T(8,128)(2,1)S(1)}, bf16[1,64,1792]{2,1,0:T(8,128)(2,1)S(1)}) fusion(bf16[64,1792]{1,0:T(8,128)(2,1)S(1)} %collective-permute-done, bf16[64,1792]{1,0:T(8,128)(2,1)S(1)} %collective-permute-done.1, ...), kind=kLoop, calls=%fused_computation.38 | loop fusion | flops 1376256 | bytes 1835024 | tf_op jit(solution)/shard_map/stack | solution.py:82
  30.7 0.6 fusion.55
  31.4 1.6 %collective-permute-start.4 = (f32[16,512]{1,0:T(8,128)S(1)}, f32[16,512]{1,0:T(8,128)S(1)}, u32[]{:S(2)}, u32[]{:S(2)}) collective-permute-start(f32[16,512]{1,0:T(8,128)S(1)} %get-tuple-element.22), channel_id=1, source_target_pairs={{0,16},{8,24},{16,0},{24,8},{1,17},{9,25},{17,1},{25,9},{2,18},{10... | collective-permute-start | bytes 98312 | tf_op jit(solution)/shard_map/ppermute | solution.py:77
  33.0 1.4 %collective-permute-start.5 = (f32[16,512]{1,0:T(8,128)S(1)}, f32[16,512]{1,0:T(8,128)S(1)}, u32[]{:S(2)}, u32[]{:S(2)}) collective-permute-start(f32[16,512]{1,0:T(8,128)S(1)} %get-tuple-element.21), channel_id=1, source_target_pairs={{0,24},{8,0},{16,8},{24,16},{1,25},{9,1},{17,9},{25,17},{2,26},{10... | collective-permute-start | bytes 98312 | tf_op jit(solution)/shard_map/ppermute | solution.py:77
  34.4 0.4 collective-permute-done.3
  34.8 0.7 collective-permute-done.4
  35.4 0.6 collective-permute-done.5
  36.0 0.7 %collective-permute-start.6 = (f32[4,512]{1,0:T(4,128)S(1)}, f32[4,512]{1,0:T(4,128)S(1)}, u32[]{:S(2)}, u32[]{:S(2)}) collective-permute-start(f32[4,512]{1,0:T(4,128)S(1)} %get-tuple-element.27), channel_id=1, source_target_pairs={{0,2},{2,4},{4,6},{6,0},{1,3},{3,5},{5,7},{7,1},{8,10},{10,12},{12... | collective-permute-start | bytes 24584 | tf_op jit(solution)/shard_map/ppermute | solution.py:77
  36.8 0.3 collective-permute-start.7
  37.1 2.8 %collective-permute-start.8 = (f32[4,512]{1,0:T(4,128)S(1)}, f32[4,512]{1,0:T(4,128)S(1)}, u32[]{:S(2)}, u32[]{:S(2)}) collective-permute-start(f32[4,512]{1,0:T(4,128)S(1)} %get-tuple-element.28), channel_id=1, source_target_pairs={{0,6},{2,0},{4,2},{6,4},{1,7},{3,1},{5,3},{7,5},{8,14},{10,8},{12,... | collective-permute-start | bytes 24584 | tf_op jit(solution)/shard_map/ppermute | solution.py:77
  39.9 1.7 %collective-permute-done.6 = f32[4,512]{1,0:T(4,128)S(1)} collective-permute-done((f32[4,512]{1,0:T(4,128)S(1)}, f32[4,512]{1,0:T(4,128)S(1)}, u32[]{:S(2)}, u32[]{:S(2)}) %collective-permute-start.6) | collective-permute-done | bytes 8224 | tf_op jit(solution)/shard_map/ppermute | solution.py:77
  41.6 0.5 collective-permute-done.8
  42.1 1.3 %collective-permute-start.10 = (bf16[4,512]{1,0:T(4,128)(2,1)S(1)}, bf16[4,512]{1,0:T(4,128)(2,1)S(1)}, u32[]{:S(2)}, u32[]{:S(2)}) collective-permute-start(bf16[4,512]{1,0:T(4,128)(2,1)S(1)} %fusion.52), channel_id=1, source_target_pairs={{0,4},{2,6},{4,0},{6,2},{1,5},{3,7},{5,1},{7,3},{8,12},{10,14},{12... | collective-permute-start | bytes 12296 | tf_op jit(solution)/shard_map/ppermute | solution.py:77
  43.4 3.1 %collective-permute-start.11 = (bf16[4,512]{1,0:T(4,128)(2,1)S(1)}, bf16[4,512]{1,0:T(4,128)(2,1)S(1)}, u32[]{:S(2)}, u32[]{:S(2)}) collective-permute-start(bf16[4,512]{1,0:T(4,128)(2,1)S(1)} %fusion.52), channel_id=1, source_target_pairs={{0,6},{2,0},{4,2},{6,4},{1,7},{3,1},{5,3},{7,5},{8,14},{10,8},{12,... | collective-permute-start | bytes 12296 | tf_op jit(solution)/shard_map/ppermute | solution.py:77
  46.7 1.2 %collective-permute-done.11 = bf16[4,512]{1,0:T(4,128)(2,1)S(1)} collective-permute-done((bf16[4,512]{1,0:T(4,128)(2,1)S(1)}, bf16[4,512]{1,0:T(4,128)(2,1)S(1)}, u32[]{:S(2)}, u32[]{:S(2)}) %collective-permute-start.11) | collective-permute-done | bytes 4128 | tf_op jit(solution)/shard_map/ppermute | solution.py:77
  47.9 4.1 %collective-permute-done.9 = bf16[4,512]{1,0:T(4,128)(2,1)S(1)} collective-permute-done((bf16[4,512]{1,0:T(4,128)(2,1)S(1)}, bf16[4,512]{1,0:T(4,128)(2,1)S(1)}, u32[]{:S(2)}, u32[]{:S(2)}) %collective-permute-start.9) | collective-permute-done | bytes 4128 | tf_op jit(solution)/shard_map/ppermute | solution.py:77
  52.1 1.0 %collective-permute-start.13 = (bf16[16,512]{1,0:T(8,128)(2,1)S(1)}, bf16[16,512]{1,0:T(8,128)(2,1)S(1)}, u32[]{:S(2)}, u32[]{:S(2)}) collective-permute-start(bf16[16,512]{1,0:T(8,128)(2,1)S(1)} %reshape.55), channel_id=1, source_target_pairs={{0,16},{8,24},{16,0},{24,8},{1,17},{9,25},{17,1},{25,9},{2,18},{10... | collective-permute-start | bytes 49160 | tf_op jit(solution)/shard_map/ppermute | solution.py:77
  53.1 1.4 %collective-permute-start.14 = (bf16[16,512]{1,0:T(8,128)(2,1)S(1)}, bf16[16,512]{1,0:T(8,128)(2,1)S(1)}, u32[]{:S(2)}, u32[]{:S(2)}) collective-permute-start(bf16[16,512]{1,0:T(8,128)(2,1)S(1)} %reshape.55), channel_id=1, source_target_pairs={{0,24},{8,0},{16,8},{24,16},{1,25},{9,1},{17,9},{25,17},{2,26},{10... | collective-permute-start | bytes 49160 | tf_op jit(solution)/shard_map/ppermute | solution.py:77
  54.5 0.7 %collective-permute-done.12 = bf16[16,512]{1,0:T(8,128)(2,1)S(1)} collective-permute-done((bf16[16,512]{1,0:T(8,128)(2,1)S(1)}, bf16[16,512]{1,0:T(8,128)(2,1)S(1)}, u32[]{:S(2)}, u32[]{:S(2)}) %collective-permute-start.12) | collective-permute-done | bytes 16416 | tf_op jit(solution)/shard_map/ppermute | solution.py:77
  55.2 0.8 %collective-permute-done.13 = bf16[16,512]{1,0:T(8,128)(2,1)S(1)} collective-permute-done((bf16[16,512]{1,0:T(8,128)(2,1)S(1)}, bf16[16,512]{1,0:T(8,128)(2,1)S(1)}, u32[]{:S(2)}, u32[]{:S(2)}) %collective-permute-start.13) | collective-permute-done | bytes 16416 | tf_op jit(solution)/shard_map/ppermute | solution.py:77
  56.1 0.7 %convolution_convert_fusion = bf16[4,16,1792]{2,1,0:T(8,128)(2,1)S(1)} fusion(bf16[1792,512]{1,0:T(8,128)(2,1)S(1)} %fusion.18, bf16[1,16,512]{2,1,0:T(8,128)(2,1)S(1)} %get-tuple-element.24, bf16[1,16,512]{2,1,0:T(8,128)(2,1)S(1)} %get-tuple-element.25, bf16[1,16,512]{2,1,0:T(8,128)(2,1)S(1)} %get-tuple-element.26, ...), kind=kOutput, calls=%fused_computation.25 | convolution fusion | flops 117653504 | bytes 2129920 | tf_op jit(solution)/shard_map/dot_general | solution.py:135
  56.8 0.6 collective-permute-start.16
  57.4 3.3 %collective-permute-start.17 = (bf16[16,1792]{1,0:T(8,128)(2,1)S(1)}, bf16[16,1792]{1,0:T(8,128)(2,1)S(1)}, u32[]{:S(2)}, u32[]{:S(2)}) collective-permute-start(bf16[16,1792]{1,0:T(8,128)(2,1)S(1)} %get-tuple-element.17), channel_id=1, source_target_pairs={{0,6},{2,0},{4,2},{6,4},{1,7},{3,1},{5,3},{7,5},{8,14},{10,8},{12,... | collective-permute-start | bytes 172040 | tf_op jit(solution)/shard_map/ppermute | solution.py:77
  61.4 2.1 %collective-permute-done.15 = bf16[16,1792]{1,0:T(8,128)(2,1)S(1)} collective-permute-done((bf16[16,1792]{1,0:T(8,128)(2,1)S(1)}, bf16[16,1792]{1,0:T(8,128)(2,1)S(1)}, u32[]{:S(2)}, u32[]{:S(2)}) %collective-permute-start.15) | collective-permute-done | bytes 57376 | tf_op jit(solution)/shard_map/ppermute | solution.py:77
  63.5 1.4 %collective-permute-done.16 = bf16[16,1792]{1,0:T(8,128)(2,1)S(1)} collective-permute-done((bf16[16,1792]{1,0:T(8,128)(2,1)S(1)}, bf16[16,1792]{1,0:T(8,128)(2,1)S(1)}, u32[]{:S(2)}, u32[]{:S(2)}) %collective-permute-start.16) | collective-permute-done | bytes 57376 | tf_op jit(solution)/shard_map/ppermute | solution.py:77
  65.1 1.2 %multiply_divide_fusion = (f32[16,7168]{1,0:T(8,128)}, f32[16,7168]{1,0:T(8,128)}, f32[16,7168]{1,0:T(8,128)}) fusion(f32[]{:T(128)} %bitcast.37, f32[]{:T(128)} %bitcast.36, f32[16,7168]{1,0:T(8,128)S(1)} %bitcast.124, f32[16,7168]{1,0:T(8,128)S(1)} %copy-done, f32[16,7168]{1,0:T(8,128)S(1)} %copy-done.1), kind=kLoop, calls=%fused_computation.31 | loop fusion | flops 1261568 | bytes 2752520 | tf_op jit(solution)/shard_map/div | solution.py:47
  (31 shorter events, 0.8 us)
Async XLA Ops:
  1.9 27.4 %collective-permute-start = (bf16[64,1792]{1,0:T(8,128)(2,1)S(1)}, bf16[64,1792]{1,0:T(8,128)(2,1)S(1)}, u32[]{:S(2)}, u32[]{:S(2)}) collective-permute-start(bf16[64,1792]{1,0:T(8,128)(2,1)S(1)} %get-tuple-element.11), channel_id=1, source_target_pairs={{0,2},{2,4},{4,6},{6,0},{1,3},{3,5},{5,7},{7,1},{8,10},{10,12},{12... | collective-permute-start | bytes 688136 | tf_op jit(solution)/shard_map/ppermute | solution.py:77
  5.0 24.3 %collective-permute-start.1 = (bf16[64,1792]{1,0:T(8,128)(2,1)S(1)}, bf16[64,1792]{1,0:T(8,128)(2,1)S(1)}, u32[]{:S(2)}, u32[]{:S(2)}) collective-permute-start(bf16[64,1792]{1,0:T(8,128)(2,1)S(1)} %get-tuple-element.12), channel_id=1, source_target_pairs={{0,4},{2,6},{4,0},{6,2},{1,5},{3,7},{5,1},{7,3},{8,12},{10,14},{12... | collective-permute-start | bytes 688136 | tf_op jit(solution)/shard_map/ppermute | solution.py:77
  7.6 21.7 %collective-permute-start.2 = (bf16[64,1792]{1,0:T(8,128)(2,1)S(1)}, bf16[64,1792]{1,0:T(8,128)(2,1)S(1)}, u32[]{:S(2)}, u32[]{:S(2)}) collective-permute-start(bf16[64,1792]{1,0:T(8,128)(2,1)S(1)} %get-tuple-element.10), channel_id=1, source_target_pairs={{0,6},{2,0},{4,2},{6,4},{1,7},{3,1},{5,3},{7,5},{8,14},{10,8},{12,... | collective-permute-start | bytes 688136 | tf_op jit(solution)/shard_map/ppermute | solution.py:77
  31.4 3.4 %collective-permute-start.3 = (f32[16,512]{1,0:T(8,128)S(1)}, f32[16,512]{1,0:T(8,128)S(1)}, u32[]{:S(2)}, u32[]{:S(2)}) collective-permute-start(f32[16,512]{1,0:T(8,128)S(1)} %get-tuple-element.20), channel_id=1, source_target_pairs={{0,8},{8,16},{16,24},{24,0},{1,9},{9,17},{17,25},{25,1},{2,10},{10... | collective-permute-start | bytes 98312 | tf_op jit(solution)/shard_map/ppermute | solution.py:77
  31.4 4.0 %collective-permute-start.4 = (f32[16,512]{1,0:T(8,128)S(1)}, f32[16,512]{1,0:T(8,128)S(1)}, u32[]{:S(2)}, u32[]{:S(2)}) collective-permute-start(f32[16,512]{1,0:T(8,128)S(1)} %get-tuple-element.22), channel_id=1, source_target_pairs={{0,16},{8,24},{16,0},{24,8},{1,17},{9,25},{17,1},{25,9},{2,18},{10... | collective-permute-start | bytes 98312 | tf_op jit(solution)/shard_map/ppermute | solution.py:77
  33.0 3.0 %collective-permute-start.5 = (f32[16,512]{1,0:T(8,128)S(1)}, f32[16,512]{1,0:T(8,128)S(1)}, u32[]{:S(2)}, u32[]{:S(2)}) collective-permute-start(f32[16,512]{1,0:T(8,128)S(1)} %get-tuple-element.21), channel_id=1, source_target_pairs={{0,24},{8,0},{16,8},{24,16},{1,25},{9,1},{17,9},{25,17},{2,26},{10... | collective-permute-start | bytes 98312 | tf_op jit(solution)/shard_map/ppermute | solution.py:77
  36.0 5.6 %collective-permute-start.6 = (f32[4,512]{1,0:T(4,128)S(1)}, f32[4,512]{1,0:T(4,128)S(1)}, u32[]{:S(2)}, u32[]{:S(2)}) collective-permute-start(f32[4,512]{1,0:T(4,128)S(1)} %get-tuple-element.27), channel_id=1, source_target_pairs={{0,2},{2,4},{4,6},{6,0},{1,3},{3,5},{5,7},{7,1},{8,10},{10,12},{12... | collective-permute-start | bytes 24584 | tf_op jit(solution)/shard_map/ppermute | solution.py:77
  36.8 4.8 %collective-permute-start.7 = (f32[4,512]{1,0:T(4,128)S(1)}, f32[4,512]{1,0:T(4,128)S(1)}, u32[]{:S(2)}, u32[]{:S(2)}) collective-permute-start(f32[4,512]{1,0:T(4,128)S(1)} %get-tuple-element.29), channel_id=1, source_target_pairs={{0,4},{2,6},{4,0},{6,2},{1,5},{3,7},{5,1},{7,3},{8,12},{10,14},{12... | collective-permute-start | bytes 24584 | tf_op jit(solution)/shard_map/ppermute | solution.py:77
  37.1 5.0 %collective-permute-start.8 = (f32[4,512]{1,0:T(4,128)S(1)}, f32[4,512]{1,0:T(4,128)S(1)}, u32[]{:S(2)}, u32[]{:S(2)}) collective-permute-start(f32[4,512]{1,0:T(4,128)S(1)} %get-tuple-element.28), channel_id=1, source_target_pairs={{0,6},{2,0},{4,2},{6,4},{1,7},{3,1},{5,3},{7,5},{8,14},{10,8},{12,... | collective-permute-start | bytes 24584 | tf_op jit(solution)/shard_map/ppermute | solution.py:77
  42.1 4.6 %collective-permute-start.10 = (bf16[4,512]{1,0:T(4,128)(2,1)S(1)}, bf16[4,512]{1,0:T(4,128)(2,1)S(1)}, u32[]{:S(2)}, u32[]{:S(2)}) collective-permute-start(bf16[4,512]{1,0:T(4,128)(2,1)S(1)} %fusion.52), channel_id=1, source_target_pairs={{0,4},{2,6},{4,0},{6,2},{1,5},{3,7},{5,1},{7,3},{8,12},{10,14},{12... | collective-permute-start | bytes 12296 | tf_op jit(solution)/shard_map/ppermute | solution.py:77
  43.4 4.5 %collective-permute-start.11 = (bf16[4,512]{1,0:T(4,128)(2,1)S(1)}, bf16[4,512]{1,0:T(4,128)(2,1)S(1)}, u32[]{:S(2)}, u32[]{:S(2)}) collective-permute-start(bf16[4,512]{1,0:T(4,128)(2,1)S(1)} %fusion.52), channel_id=1, source_target_pairs={{0,6},{2,0},{4,2},{6,4},{1,7},{3,1},{5,3},{7,5},{8,14},{10,8},{12,... | collective-permute-start | bytes 12296 | tf_op jit(solution)/shard_map/ppermute | solution.py:77
  46.6 5.4 %collective-permute-start.9 = (bf16[4,512]{1,0:T(4,128)(2,1)S(1)}, bf16[4,512]{1,0:T(4,128)(2,1)S(1)}, u32[]{:S(2)}, u32[]{:S(2)}) collective-permute-start(bf16[4,512]{1,0:T(4,128)(2,1)S(1)} %fusion.52), channel_id=1, source_target_pairs={{0,2},{2,4},{4,6},{6,0},{1,3},{3,5},{5,7},{7,1},{8,10},{10,12},{12... | collective-permute-start | bytes 12296 | tf_op jit(solution)/shard_map/ppermute | solution.py:77
  52.0 3.2 %collective-permute-start.12 = (bf16[16,512]{1,0:T(8,128)(2,1)S(1)}, bf16[16,512]{1,0:T(8,128)(2,1)S(1)}, u32[]{:S(2)}, u32[]{:S(2)}) collective-permute-start(bf16[16,512]{1,0:T(8,128)(2,1)S(1)} %reshape.55), channel_id=1, source_target_pairs={{0,8},{8,16},{16,24},{24,0},{1,9},{9,17},{17,25},{25,1},{2,10},{10... | collective-permute-start | bytes 49160 | tf_op jit(solution)/shard_map/ppermute | solution.py:77
  52.1 3.9 %collective-permute-start.13 = (bf16[16,512]{1,0:T(8,128)(2,1)S(1)}, bf16[16,512]{1,0:T(8,128)(2,1)S(1)}, u32[]{:S(2)}, u32[]{:S(2)}) collective-permute-start(bf16[16,512]{1,0:T(8,128)(2,1)S(1)} %reshape.55), channel_id=1, source_target_pairs={{0,16},{8,24},{16,0},{24,8},{1,17},{9,25},{17,1},{25,9},{2,18},{10... | collective-permute-start | bytes 49160 | tf_op jit(solution)/shard_map/ppermute | solution.py:77
  53.1 2.9 %collective-permute-start.14 = (bf16[16,512]{1,0:T(8,128)(2,1)S(1)}, bf16[16,512]{1,0:T(8,128)(2,1)S(1)}, u32[]{:S(2)}, u32[]{:S(2)}) collective-permute-start(bf16[16,512]{1,0:T(8,128)(2,1)S(1)} %reshape.55), channel_id=1, source_target_pairs={{0,24},{8,0},{16,8},{24,16},{1,25},{9,1},{17,9},{25,17},{2,26},{10... | collective-permute-start | bytes 49160 | tf_op jit(solution)/shard_map/ppermute | solution.py:77
  56.0 9.0 %copy-start = (f32[16,7168]{1,0:T(8,128)S(1)}, f32[16,7168]{1,0:T(8,128)}, u32[]{:S(2)}) copy-start(f32[16,7168]{1,0:T(8,128)} %param.10) | copy-start | bytes 1376260
  56.1 9.0 %copy-start.1 = (f32[16,7168]{1,0:T(8,128)S(1)}, f32[16,7168]{1,0:T(8,128)}, u32[]{:S(2)}) copy-start(f32[16,7168]{1,0:T(8,128)} %param.9) | copy-start | bytes 1376260
  56.8 6.7 %collective-permute-start.15 = (bf16[16,1792]{1,0:T(8,128)(2,1)S(1)}, bf16[16,1792]{1,0:T(8,128)(2,1)S(1)}, u32[]{:S(2)}, u32[]{:S(2)}) collective-permute-start(bf16[16,1792]{1,0:T(8,128)(2,1)S(1)} %get-tuple-element.19), channel_id=1, source_target_pairs={{0,2},{2,4},{4,6},{6,0},{1,3},{3,5},{5,7},{7,1},{8,10},{10,12},{12... | collective-permute-start | bytes 172040 | tf_op jit(solution)/shard_map/ppermute | solution.py:77
  56.8 8.1 %collective-permute-start.16 = (bf16[16,1792]{1,0:T(8,128)(2,1)S(1)}, bf16[16,1792]{1,0:T(8,128)(2,1)S(1)}, u32[]{:S(2)}, u32[]{:S(2)}) collective-permute-start(bf16[16,1792]{1,0:T(8,128)(2,1)S(1)} %get-tuple-element.18), channel_id=1, source_target_pairs={{0,4},{2,6},{4,0},{6,2},{1,5},{3,7},{5,1},{7,3},{8,12},{10,14},{12... | collective-permute-start | bytes 172040 | tf_op jit(solution)/shard_map/ppermute | solution.py:77
  57.4 7.6 %collective-permute-start.17 = (bf16[16,1792]{1,0:T(8,128)(2,1)S(1)}, bf16[16,1792]{1,0:T(8,128)(2,1)S(1)}, u32[]{:S(2)}, u32[]{:S(2)}) collective-permute-start(bf16[16,1792]{1,0:T(8,128)(2,1)S(1)} %get-tuple-element.17), channel_id=1, source_target_pairs={{0,6},{2,0},{4,2},{6,4},{1,7},{3,1},{5,3},{7,5},{8,14},{10,8},{12,... | collective-permute-start | bytes 172040 | tf_op jit(solution)/shard_map/ppermute | solution.py:77

commit v11 on v10

--- a/solution.py
+++ b/solution.py
@@ -120,7 +120,7 @@
         "replica",
         n_rep,
     )
-    held = by_source(got, member, n_rep)
+    held = jnp.stack(got)
 
     terms = jnp.dot(
         held.reshape(n_rep * rows, width), projection, preferred_element_type=jnp.float32

time: 66.5 us -> 64.7 us (0.973)
  other arithmetic: 22.9 us -> 21 us
    another operation x6 -> x4, other arithmetic: 1.43 us -> 0.09 us  [by_source(): jnp.stack([lax.select_n((index - p) % size, *got) for p in range(size)])]
    another operation x1, other arithmetic: 1.31 us -> 0.63 us  [projection_block(): seed_key = lax.reduce(scaled, jnp.int32(0), lax.bitwise_xor, (0,))]
where the time goes in v11:
time: 64.7 us; the launch traced here: 64.5 us
  starting transfers between devices  24.7 us (38%)
  other arithmetic  21 us (32%)
  waiting for transfers between devices  14.3 us (22%)
  between operations  1.69 us (3%)
  local copies, waits for them, and re-layouts  1.49 us (2%)
  matrix products  1.31 us (2%)
    ppermute x18, starting transfers between devices, shifted(): got.append(lax.ppermute(value_of(k), axis, pairs))  24.7 us
    convert_element_type x1, other arithmetic, projection_block(): return (gauss * rank ** (-0.5)).astype(jnp.bfloat16)  18.9 us
    ppermute x18, waiting for transfers between devices, shifted(): got.append(lax.ppermute(value_of(k), axis, pairs))  14.3 us
    dynamic_slice x1, local copies, waits for them, and re-layouts, per_device(): lax.dynamic_slice_in_dim(gradient, (member + k) % n_rep * width, width, 1)  1.35 us
  transfers between devices with their start and end apart: 18, of which 12 were waited for; matrix products, arithmetic and copies ran while one was open for 30% of the time, Pallas kernels for 0%

profile of v11, /device:TPU:0, one launch (start us, length us, event | category | flops | bytes accessed | tf_op | source)
XLA Modules:
  0.0 64.5 jit_solution(12174946153854695495)
XLA Ops:
  0.7 1.4 %constant_dynamic-slice_fusion = (bf16[1,64,1792]{2,1,0:T(8,128)(2,1)S(1)}, bf16[64,1792]{1,0:T(8,128)(2,1)S(1)}, bf16[64,1792]{1,0:T(8,128)(2,1)S(1)}, bf16[64,1792]{1,0:T(8,128)(2,1)S(1)}) fusion(bf16[1,64,7168]{2,1,0:T(8,128)(2,1)} %param.6, s32[]{:T(128)S(6)} %select_n.441, s32[]{:T(128)S(6)} %select_n.443, s32[]{:T(128)S(6)} %select_n.447, s32[]{:T(128)S(6)} %select_n.445), kind=kLoop, calls=%fused_computation.88 | loop fusion | bytes 1835024 | tf_op jit(solution)/shard_map/dynamic_slice | solution.py:119
  2.1 3.1 %collective-permute-start = (bf16[64,1792]{1,0:T(8,128)(2,1)S(1)}, bf16[64,1792]{1,0:T(8,128)(2,1)S(1)}, u32[]{:S(2)}, u32[]{:S(2)}) collective-permute-start(bf16[64,1792]{1,0:T(8,128)(2,1)S(1)} %get-tuple-element.7), channel_id=1, source_target_pairs={{0,2},{2,4},{4,6},{6,0},{1,3},{3,5},{5,7},{7,1},{8,10},{10,12},{12... | collective-permute-start | bytes 688136 | tf_op jit(solution)/shard_map/ppermute | solution.py:77
  5.2 2.6 %collective-permute-start.1 = (bf16[64,1792]{1,0:T(8,128)(2,1)S(1)}, bf16[64,1792]{1,0:T(8,128)(2,1)S(1)}, u32[]{:S(2)}, u32[]{:S(2)}) collective-permute-start(bf16[64,1792]{1,0:T(8,128)(2,1)S(1)} %get-tuple-element.9), channel_id=1, source_target_pairs={{0,4},{2,6},{4,0},{6,2},{1,5},{3,7},{5,1},{7,3},{8,12},{10,14},{12... | collective-permute-start | bytes 688136 | tf_op jit(solution)/shard_map/ppermute | solution.py:77
  7.8 1.3 %collective-permute-start.2 = (bf16[64,1792]{1,0:T(8,128)(2,1)S(1)}, bf16[64,1792]{1,0:T(8,128)(2,1)S(1)}, u32[]{:S(2)}, u32[]{:S(2)}) collective-permute-start(bf16[64,1792]{1,0:T(8,128)(2,1)S(1)} %get-tuple-element.8), channel_id=1, source_target_pairs={{0,6},{2,0},{4,2},{6,4},{1,7},{3,1},{5,3},{7,5},{8,14},{10,8},{12,... | collective-permute-start | bytes 688136 | tf_op jit(solution)/shard_map/ppermute | solution.py:77
  9.1 0.6 multiply_reduce_fusion
  9.8 18.9 %fusion.18 = bf16[1792,512]{1,0:T(8,128)(2,1)S(1)} fusion(s32[]{:T(128)} %multiply_reduce_fusion, s32[1792]{0:T(1024)S(1)} %add_multiply_fusion), kind=kLoop, calls=%fused_computation.24 | loop fusion | flops 32112640 | bytes 1842180 | tf_op jit(solution)/shard_map/convert_element_type | solution.py:38
  28.7 0.1 pad_maximum_fusion
  28.9 0.6 fusion.47
  29.6 1.6 %collective-permute-start.4 = (f32[16,512]{1,0:T(8,128)S(1)}, f32[16,512]{1,0:T(8,128)S(1)}, u32[]{:S(2)}, u32[]{:S(2)}) collective-permute-start(f32[16,512]{1,0:T(8,128)S(1)} %get-tuple-element.19), channel_id=1, source_target_pairs={{0,16},{8,24},{16,0},{24,8},{1,17},{9,25},{17,1},{25,9},{2,18},{10... | collective-permute-start | bytes 98312 | tf_op jit(solution)/shard_map/ppermute | solution.py:77
  31.2 1.4 %collective-permute-start.5 = (f32[16,512]{1,0:T(8,128)S(1)}, f32[16,512]{1,0:T(8,128)S(1)}, u32[]{:S(2)}, u32[]{:S(2)}) collective-permute-start(f32[16,512]{1,0:T(8,128)S(1)} %get-tuple-element.18), channel_id=1, source_target_pairs={{0,24},{8,0},{16,8},{24,16},{1,25},{9,1},{17,9},{25,17},{2,26},{10... | collective-permute-start | bytes 98312 | tf_op jit(solution)/shard_map/ppermute | solution.py:77
  32.6 0.4 collective-permute-done.3
  33.0 0.7 %collective-permute-done.4 = f32[16,512]{1,0:T(8,128)S(1)} collective-permute-done((f32[16,512]{1,0:T(8,128)S(1)}, f32[16,512]{1,0:T(8,128)S(1)}, u32[]{:S(2)}, u32[]{:S(2)}) %collective-permute-start.4) | collective-permute-done | bytes 32800 | tf_op jit(solution)/shard_map/ppermute | solution.py:77
  33.6 0.6 collective-permute-done.5
  34.2 0.7 %collective-permute-start.6 = (f32[4,512]{1,0:T(4,128)S(1)}, f32[4,512]{1,0:T(4,128)S(1)}, u32[]{:S(2)}, u32[]{:S(2)}) collective-permute-start(f32[4,512]{1,0:T(4,128)S(1)} %get-tuple-element.24), channel_id=1, source_target_pairs={{0,2},{2,4},{4,6},{6,0},{1,3},{3,5},{5,7},{7,1},{8,10},{10,12},{12... | collective-permute-start | bytes 24584 | tf_op jit(solution)/shard_map/ppermute | solution.py:77
  35.0 0.3 collective-permute-start.7
  35.3 2.8 %collective-permute-start.8 = (f32[4,512]{1,0:T(4,128)S(1)}, f32[4,512]{1,0:T(4,128)S(1)}, u32[]{:S(2)}, u32[]{:S(2)}) collective-permute-start(f32[4,512]{1,0:T(4,128)S(1)} %get-tuple-element.25), channel_id=1, source_target_pairs={{0,6},{2,0},{4,2},{6,4},{1,7},{3,1},{5,3},{7,5},{8,14},{10,8},{12,... | collective-permute-start | bytes 24584 | tf_op jit(solution)/shard_map/ppermute | solution.py:77
  38.1 1.7 %collective-permute-done.6 = f32[4,512]{1,0:T(4,128)S(1)} collective-permute-done((f32[4,512]{1,0:T(4,128)S(1)}, f32[4,512]{1,0:T(4,128)S(1)}, u32[]{:S(2)}, u32[]{:S(2)}) %collective-permute-start.6) | collective-permute-done | bytes 8224 | tf_op jit(solution)/shard_map/ppermute | solution.py:77
  39.8 0.5 collective-permute-done.8
  40.3 1.3 %collective-permute-start.10 = (bf16[4,512]{1,0:T(4,128)(2,1)S(1)}, bf16[4,512]{1,0:T(4,128)(2,1)S(1)}, u32[]{:S(2)}, u32[]{:S(2)}) collective-permute-start(bf16[4,512]{1,0:T(4,128)(2,1)S(1)} %fusion.44), channel_id=1, source_target_pairs={{0,4},{2,6},{4,0},{6,2},{1,5},{3,7},{5,1},{7,3},{8,12},{10,14},{12... | collective-permute-start | bytes 12296 | tf_op jit(solution)/shard_map/ppermute | solution.py:77
  41.6 3.1 %collective-permute-start.11 = (bf16[4,512]{1,0:T(4,128)(2,1)S(1)}, bf16[4,512]{1,0:T(4,128)(2,1)S(1)}, u32[]{:S(2)}, u32[]{:S(2)}) collective-permute-start(bf16[4,512]{1,0:T(4,128)(2,1)S(1)} %fusion.44), channel_id=1, source_target_pairs={{0,6},{2,0},{4,2},{6,4},{1,7},{3,1},{5,3},{7,5},{8,14},{10,8},{12,... | collective-permute-start | bytes 12296 | tf_op jit(solution)/shard_map/ppermute | solution.py:77
  44.9 1.2 %collective-permute-done.11 = bf16[4,512]{1,0:T(4,128)(2,1)S(1)} collective-permute-done((bf16[4,512]{1,0:T(4,128)(2,1)S(1)}, bf16[4,512]{1,0:T(4,128)(2,1)S(1)}, u32[]{:S(2)}, u32[]{:S(2)}) %collective-permute-start.11) | collective-permute-done | bytes 4128 | tf_op jit(solution)/shard_map/ppermute | solution.py:77
  46.1 4.1 %collective-permute-done.9 = bf16[4,512]{1,0:T(4,128)(2,1)S(1)} collective-permute-done((bf16[4,512]{1,0:T(4,128)(2,1)S(1)}, bf16[4,512]{1,0:T(4,128)(2,1)S(1)}, u32[]{:S(2)}, u32[]{:S(2)}) %collective-permute-start.9) | collective-permute-done | bytes 4128 | tf_op jit(solution)/shard_map/ppermute | solution.py:77
  50.3 1.0 %collective-permute-start.13 = (bf16[16,512]{1,0:T(8,128)(2,1)S(1)}, bf16[16,512]{1,0:T(8,128)(2,1)S(1)}, u32[]{:S(2)}, u32[]{:S(2)}) collective-permute-start(bf16[16,512]{1,0:T(8,128)(2,1)S(1)} %reshape.56), channel_id=1, source_target_pairs={{0,16},{8,24},{16,0},{24,8},{1,17},{9,25},{17,1},{25,9},{2,18},{10... | collective-permute-start | bytes 49160 | tf_op jit(solution)/shard_map/ppermute | solution.py:77
  51.3 1.4 %collective-permute-start.14 = (bf16[16,512]{1,0:T(8,128)(2,1)S(1)}, bf16[16,512]{1,0:T(8,128)(2,1)S(1)}, u32[]{:S(2)}, u32[]{:S(2)}) collective-permute-start(bf16[16,512]{1,0:T(8,128)(2,1)S(1)} %reshape.56), channel_id=1, source_target_pairs={{0,24},{8,0},{16,8},{24,16},{1,25},{9,1},{17,9},{25,17},{2,26},{10... | collective-permute-start | bytes 49160 | tf_op jit(solution)/shard_map/ppermute | solution.py:77
  52.7 0.7 %collective-permute-done.12 = bf16[16,512]{1,0:T(8,128)(2,1)S(1)} collective-permute-done((bf16[16,512]{1,0:T(8,128)(2,1)S(1)}, bf16[16,512]{1,0:T(8,128)(2,1)S(1)}, u32[]{:S(2)}, u32[]{:S(2)}) %collective-permute-start.12) | collective-permute-done | bytes 16416 | tf_op jit(solution)/shard_map/ppermute | solution.py:77
  53.4 0.8 %collective-permute-done.13 = bf16[16,512]{1,0:T(8,128)(2,1)S(1)} collective-permute-done((bf16[16,512]{1,0:T(8,128)(2,1)S(1)}, bf16[16,512]{1,0:T(8,128)(2,1)S(1)}, u32[]{:S(2)}, u32[]{:S(2)}) %collective-permute-start.13) | collective-permute-done | bytes 16416 | tf_op jit(solution)/shard_map/ppermute | solution.py:77
  54.3 0.7 %convolution_convert_fusion = bf16[4,16,1792]{2,1,0:T(8,128)(2,1)S(1)} fusion(bf16[1792,512]{1,0:T(8,128)(2,1)S(1)} %fusion.18, bf16[1,16,512]{2,1,0:T(8,128)(2,1)S(1)} %get-tuple-element.21, bf16[1,16,512]{2,1,0:T(8,128)(2,1)S(1)} %get-tuple-element.22, bf16[1,16,512]{2,1,0:T(8,128)(2,1)S(1)} %get-tuple-element.23, ...), kind=kOutput, calls=%fused_computation.25 | convolution fusion | flops 117653504 | bytes 2129920 | tf_op jit(solution)/shard_map/dot_general | solution.py:135
  55.0 0.6 collective-permute-start.16
  55.6 3.3 %collective-permute-start.17 = (bf16[16,1792]{1,0:T(8,128)(2,1)S(1)}, bf16[16,1792]{1,0:T(8,128)(2,1)S(1)}, u32[]{:S(2)}, u32[]{:S(2)}) collective-permute-start(bf16[16,1792]{1,0:T(8,128)(2,1)S(1)} %get-tuple-element.14), channel_id=1, source_target_pairs={{0,6},{2,0},{4,2},{6,4},{1,7},{3,1},{5,3},{7,5},{8,14},{10,8},{12,... | collective-permute-start | bytes 172040 | tf_op jit(solution)/shard_map/ppermute | solution.py:77
  59.6 2.1 %collective-permute-done.15 = bf16[16,1792]{1,0:T(8,128)(2,1)S(1)} collective-permute-done((bf16[16,1792]{1,0:T(8,128)(2,1)S(1)}, bf16[16,1792]{1,0:T(8,128)(2,1)S(1)}, u32[]{:S(2)}, u32[]{:S(2)}) %collective-permute-start.15) | collective-permute-done | bytes 57376 | tf_op jit(solution)/shard_map/ppermute | solution.py:77
  61.7 1.4 %collective-permute-done.16 = bf16[16,1792]{1,0:T(8,128)(2,1)S(1)} collective-permute-done((bf16[16,1792]{1,0:T(8,128)(2,1)S(1)}, bf16[16,1792]{1,0:T(8,128)(2,1)S(1)}, u32[]{:S(2)}, u32[]{:S(2)}) %collective-permute-start.16) | collective-permute-done | bytes 57376 | tf_op jit(solution)/shard_map/ppermute | solution.py:77
  63.3 1.2 %multiply_divide_fusion = (f32[16,7168]{1,0:T(8,128)}, f32[16,7168]{1,0:T(8,128)}, f32[16,7168]{1,0:T(8,128)}) fusion(f32[]{:T(128)} %bitcast.35, f32[]{:T(128)} %bitcast.34, f32[16,7168]{1,0:T(8,128)S(1)} %bitcast.98, f32[16,7168]{1,0:T(8,128)S(1)} %copy-done, f32[16,7168]{1,0:T(8,128)S(1)} %copy-done.1), kind=kLoop, calls=%fused_computation.31 | loop fusion | flops 1261568 | bytes 2752520 | tf_op jit(solution)/shard_map/div | solution.py:47
  (34 shorter events, 0.6 us)
Async XLA Ops:
  0.6 8.5 %copy-start.3 = (s32[2]{0:T(128)S(1)}, s32[2]{0:T(128)}, u32[]{:S(2)}) copy-start(s32[2]{0:T(128)} %constant.198.clone) | copy-start | bytes 28
  0.6 8.5 %copy-start.2 = (s32[2]{0:T(128)S(1)}, s32[2]{0:T(128)}, u32[]{:S(2)}) copy-start(s32[2]{0:T(128)} %param.7) | copy-start | bytes 28
  2.1 26.6 %collective-permute-start = (bf16[64,1792]{1,0:T(8,128)(2,1)S(1)}, bf16[64,1792]{1,0:T(8,128)(2,1)S(1)}, u32[]{:S(2)}, u32[]{:S(2)}) collective-permute-start(bf16[64,1792]{1,0:T(8,128)(2,1)S(1)} %get-tuple-element.7), channel_id=1, source_target_pairs={{0,2},{2,4},{4,6},{6,0},{1,3},{3,5},{5,7},{7,1},{8,10},{10,12},{12... | collective-permute-start | bytes 688136 | tf_op jit(solution)/shard_map/ppermute | solution.py:77
  5.2 23.5 %collective-permute-start.1 = (bf16[64,1792]{1,0:T(8,128)(2,1)S(1)}, bf16[64,1792]{1,0:T(8,128)(2,1)S(1)}, u32[]{:S(2)}, u32[]{:S(2)}) collective-permute-start(bf16[64,1792]{1,0:T(8,128)(2,1)S(1)} %get-tuple-element.9), channel_id=1, source_target_pairs={{0,4},{2,6},{4,0},{6,2},{1,5},{3,7},{5,1},{7,3},{8,12},{10,14},{12... | collective-permute-start | bytes 688136 | tf_op jit(solution)/shard_map/ppermute | solution.py:77
  7.8 20.9 %collective-permute-start.2 = (bf16[64,1792]{1,0:T(8,128)(2,1)S(1)}, bf16[64,1792]{1,0:T(8,128)(2,1)S(1)}, u32[]{:S(2)}, u32[]{:S(2)}) collective-permute-start(bf16[64,1792]{1,0:T(8,128)(2,1)S(1)} %get-tuple-element.8), channel_id=1, source_target_pairs={{0,6},{2,0},{4,2},{6,4},{1,7},{3,1},{5,3},{7,5},{8,14},{10,8},{12,... | collective-permute-start | bytes 688136 | tf_op jit(solution)/shard_map/ppermute | solution.py:77
  29.6 3.4 %collective-permute-start.3 = (f32[16,512]{1,0:T(8,128)S(1)}, f32[16,512]{1,0:T(8,128)S(1)}, u32[]{:S(2)}, u32[]{:S(2)}) collective-permute-start(f32[16,512]{1,0:T(8,128)S(1)} %get-tuple-element.17), channel_id=1, source_target_pairs={{0,8},{8,16},{16,24},{24,0},{1,9},{9,17},{17,25},{25,1},{2,10},{10... | collective-permute-start | bytes 98312 | tf_op jit(solution)/shard_map/ppermute | solution.py:77
  29.6 4.0 %collective-permute-start.4 = (f32[16,512]{1,0:T(8,128)S(1)}, f32[16,512]{1,0:T(8,128)S(1)}, u32[]{:S(2)}, u32[]{:S(2)}) collective-permute-start(f32[16,512]{1,0:T(8,128)S(1)} %get-tuple-element.19), channel_id=1, source_target_pairs={{0,16},{8,24},{16,0},{24,8},{1,17},{9,25},{17,1},{25,9},{2,18},{10... | collective-permute-start | bytes 98312 | tf_op jit(solution)/shard_map/ppermute | solution.py:77
  31.2 3.0 %collective-permute-start.5 = (f32[16,512]{1,0:T(8,128)S(1)}, f32[16,512]{1,0:T(8,128)S(1)}, u32[]{:S(2)}, u32[]{:S(2)}) collective-permute-start(f32[16,512]{1,0:T(8,128)S(1)} %get-tuple-element.18), channel_id=1, source_target_pairs={{0,24},{8,0},{16,8},{24,16},{1,25},{9,1},{17,9},{25,17},{2,26},{10... | collective-permute-start | bytes 98312 | tf_op jit(solution)/shard_map/ppermute | solution.py:77
  34.2 5.6 %collective-permute-start.6 = (f32[4,512]{1,0:T(4,128)S(1)}, f32[4,512]{1,0:T(4,128)S(1)}, u32[]{:S(2)}, u32[]{:S(2)}) collective-permute-start(f32[4,512]{1,0:T(4,128)S(1)} %get-tuple-element.24), channel_id=1, source_target_pairs={{0,2},{2,4},{4,6},{6,0},{1,3},{3,5},{5,7},{7,1},{8,10},{10,12},{12... | collective-permute-start | bytes 24584 | tf_op jit(solution)/shard_map/ppermute | solution.py:77
  35.0 4.8 %collective-permute-start.7 = (f32[4,512]{1,0:T(4,128)S(1)}, f32[4,512]{1,0:T(4,128)S(1)}, u32[]{:S(2)}, u32[]{:S(2)}) collective-permute-start(f32[4,512]{1,0:T(4,128)S(1)} %get-tuple-element.26), channel_id=1, source_target_pairs={{0,4},{2,6},{4,0},{6,2},{1,5},{3,7},{5,1},{7,3},{8,12},{10,14},{12... | collective-permute-start | bytes 24584 | tf_op jit(solution)/shard_map/ppermute | solution.py:77
  35.3 5.0 %collective-permute-start.8 = (f32[4,512]{1,0:T(4,128)S(1)}, f32[4,512]{1,0:T(4,128)S(1)}, u32[]{:S(2)}, u32[]{:S(2)}) collective-permute-start(f32[4,512]{1,0:T(4,128)S(1)} %get-tuple-element.25), channel_id=1, source_target_pairs={{0,6},{2,0},{4,2},{6,4},{1,7},{3,1},{5,3},{7,5},{8,14},{10,8},{12,... | collective-permute-start | bytes 24584 | tf_op jit(solution)/shard_map/ppermute | solution.py:77
  40.3 4.6 %collective-permute-start.10 = (bf16[4,512]{1,0:T(4,128)(2,1)S(1)}, bf16[4,512]{1,0:T(4,128)(2,1)S(1)}, u32[]{:S(2)}, u32[]{:S(2)}) collective-permute-start(bf16[4,512]{1,0:T(4,128)(2,1)S(1)} %fusion.44), channel_id=1, source_target_pairs={{0,4},{2,6},{4,0},{6,2},{1,5},{3,7},{5,1},{7,3},{8,12},{10,14},{12... | collective-permute-start | bytes 12296 | tf_op jit(solution)/shard_map/ppermute | solution.py:77
  41.6 4.5 %collective-permute-start.11 = (bf16[4,512]{1,0:T(4,128)(2,1)S(1)}, bf16[4,512]{1,0:T(4,128)(2,1)S(1)}, u32[]{:S(2)}, u32[]{:S(2)}) collective-permute-start(bf16[4,512]{1,0:T(4,128)(2,1)S(1)} %fusion.44), channel_id=1, source_target_pairs={{0,6},{2,0},{4,2},{6,4},{1,7},{3,1},{5,3},{7,5},{8,14},{10,8},{12,... | collective-permute-start | bytes 12296 | tf_op jit(solution)/shard_map/ppermute | solution.py:77
  44.8 5.4 %collective-permute-start.9 = (bf16[4,512]{1,0:T(4,128)(2,1)S(1)}, bf16[4,512]{1,0:T(4,128)(2,1)S(1)}, u32[]{:S(2)}, u32[]{:S(2)}) collective-permute-start(bf16[4,512]{1,0:T(4,128)(2,1)S(1)} %fusion.44), channel_id=1, source_target_pairs={{0,2},{2,4},{4,6},{6,0},{1,3},{3,5},{5,7},{7,1},{8,10},{10,12},{12... | collective-permute-start | bytes 12296 | tf_op jit(solution)/shard_map/ppermute | solution.py:77
  50.2 3.2 %collective-permute-start.12 = (bf16[16,512]{1,0:T(8,128)(2,1)S(1)}, bf16[16,512]{1,0:T(8,128)(2,1)S(1)}, u32[]{:S(2)}, u32[]{:S(2)}) collective-permute-start(bf16[16,512]{1,0:T(8,128)(2,1)S(1)} %reshape.56), channel_id=1, source_target_pairs={{0,8},{8,16},{16,24},{24,0},{1,9},{9,17},{17,25},{25,1},{2,10},{10... | collective-permute-start | bytes 49160 | tf_op jit(solution)/shard_map/ppermute | solution.py:77
  50.3 3.9 %collective-permute-start.13 = (bf16[16,512]{1,0:T(8,128)(2,1)S(1)}, bf16[16,512]{1,0:T(8,128)(2,1)S(1)}, u32[]{:S(2)}, u32[]{:S(2)}) collective-permute-start(bf16[16,512]{1,0:T(8,128)(2,1)S(1)} %reshape.56), channel_id=1, source_target_pairs={{0,16},{8,24},{16,0},{24,8},{1,17},{9,25},{17,1},{25,9},{2,18},{10... | collective-permute-start | bytes 49160 | tf_op jit(solution)/shard_map/ppermute | solution.py:77
  51.3 2.9 %collective-permute-start.14 = (bf16[16,512]{1,0:T(8,128)(2,1)S(1)}, bf16[16,512]{1,0:T(8,128)(2,1)S(1)}, u32[]{:S(2)}, u32[]{:S(2)}) collective-permute-start(bf16[16,512]{1,0:T(8,128)(2,1)S(1)} %reshape.56), channel_id=1, source_target_pairs={{0,24},{8,0},{16,8},{24,16},{1,25},{9,1},{17,9},{25,17},{2,26},{10... | collective-permute-start | bytes 49160 | tf_op jit(solution)/shard_map/ppermute | solution.py:77
  54.2 9.0 %copy-start = (f32[16,7168]{1,0:T(8,128)S(1)}, f32[16,7168]{1,0:T(8,128)}, u32[]{:S(2)}) copy-start(f32[16,7168]{1,0:T(8,128)} %param.10) | copy-start | bytes 1376260
  54.3 9.0 %copy-start.1 = (f32[16,7168]{1,0:T(8,128)S(1)}, f32[16,7168]{1,0:T(8,128)}, u32[]{:S(2)}) copy-start(f32[16,7168]{1,0:T(8,128)} %param.9) | copy-start | bytes 1376260
  55.0 6.7 %collective-permute-start.15 = (bf16[16,1792]{1,0:T(8,128)(2,1)S(1)}, bf16[16,1792]{1,0:T(8,128)(2,1)S(1)}, u32[]{:S(2)}, u32[]{:S(2)}) collective-permute-start(bf16[16,1792]{1,0:T(8,128)(2,1)S(1)} %get-tuple-element.16), channel_id=1, source_target_pairs={{0,2},{2,4},{4,6},{6,0},{1,3},{3,5},{5,7},{7,1},{8,10},{10,12},{12... | collective-permute-start | bytes 172040 | tf_op jit(solution)/shard_map/ppermute | solution.py:77
  55.0 8.1 %collective-permute-start.16 = (bf16[16,1792]{1,0:T(8,128)(2,1)S(1)}, bf16[16,1792]{1,0:T(8,128)(2,1)S(1)}, u32[]{:S(2)}, u32[]{:S(2)}) collective-permute-start(bf16[16,1792]{1,0:T(8,128)(2,1)S(1)} %get-tuple-element.15), channel_id=1, source_target_pairs={{0,4},{2,6},{4,0},{6,2},{1,5},{3,7},{5,1},{7,3},{8,12},{10,14},{12... | collective-permute-start | bytes 172040 | tf_op jit(solution)/shard_map/ppermute | solution.py:77
  55.6 7.6 %collective-permute-start.17 = (bf16[16,1792]{1,0:T(8,128)(2,1)S(1)}, bf16[16,1792]{1,0:T(8,128)(2,1)S(1)}, u32[]{:S(2)}, u32[]{:S(2)}) collective-permute-start(bf16[16,1792]{1,0:T(8,128)(2,1)S(1)} %get-tuple-element.14), channel_id=1, source_target_pairs={{0,6},{2,0},{4,2},{6,4},{1,7},{3,1},{5,3},{7,5},{8,14},{10,8},{12,... | collective-permute-start | bytes 172040 | tf_op jit(solution)/shard_map/ppermute | solution.py:77
